TPU v7x, 128 devices: a whole 4x4x4 slice. The times are simulated.
128 devices in a mesh: seq: 16 (over x_hi, z, core), tp: 8 (over y, x_lo).
Axes of the slice: x: 4 (x_hi: 2, x_lo: 2; x = x_hi * 2 + x_lo), y: 4, z: 4, core: 2. Of those that a mesh axis runs over, the one named last changes fastest.
Arguments:
- tokens: bfloat16 [4, 2048, 4096], P(None, 'seq', 'tp'), may hold values from -6 to 6
- new_tokens: bfloat16 [4, 4096], P(None, 'tp'), may hold values from -6 to 6
- w_qkv: bfloat16 [3, 4096, 4096], P(None, None, 'tp')
- w_out: bfloat16 [4096, 4096], P('tp')
- q_gain: float32 [4096], P('tp'), may hold values from 0.5 to 6
- k_gain: float32 [4096], P('tp'), may hold values from 0.5 to 6
- post_gain: float32 [4096], P('tp'), may hold values from 0.5 to 1.5
- lengths: int32 [4], replicated, may hold values from 1 to 2048, 6144 in all
Outputs:
- hidden_out: bfloat16 [4, 2048, 4096], P(None, 'seq', 'tp')
- new_out: bfloat16 [4, 4096], P(None, 'tp')
Inputs may be any that keep to these rules, and one draw needn't show every extreme that they name: `lengths`: one prompt has exactly 2048 live tokens.
All inputs are finite; a program needn't handle non-finite values.
Results may differ from a plain program's by a relative error of at most 0.012.
The roundings to bfloat16 on the way count: a program that leaves them out, or rounds other values in their place, can miss the bound.
Values may be sent and summed in bfloat16 or wider, within the bound.
No kernel may reach another device: no remote copies, remote signals or barrier semaphores. Data moves between devices by JAX's collectives and lax.ppermute only.
A program may use at most 128 MiB of HBM per device.

v0:
```python
import jax
import jax.numpy as jnp
from jax import lax
from jax.experimental import pallas as pl
from jax.experimental.pallas import tpu as pltpu
from jax.sharding import PartitionSpec as P

HD = 128


rope_base = 500000.0
norm_eps = 1e-06
masked_fill = -1e30


RELATIVE = ("own", "ax", "aup", "adn", "m1", "m2", "m3", "m4")


def tp_links(width):
    size = 8
    cross = [(i, i ^ 1) for i in range(size)]
    up = [(i, (i + 2) % size) for i in range(size)]
    down = [(i, (i - 2) % size) for i in range(size)]
    t = lax.axis_index("tp")
    y, x = t // 2, t % 2
    other = 1 - x

    def block(dy, side):
        return ((y + dy) % 4) * 2 + side

    order = {
        "own": block(0, x), "ax": block(0, other), "aup": block(-1, x), "adn": block(1, x),
        "m1": block(1, other), "m2": block(-1, other), "m3": block(2, x), "m4": block(2, other),
    }
    return cross, up, down, order


def tp_gather(piece):
    width = piece.shape[1]
    half, quarter = width // 2, width // 4
    cross, up, down, order = tp_links(width)
    send = lambda value, perm: lax.ppermute(value, "tp", perm)
    ax = send(piece, cross)
    aup = send(piece, up)
    adn = send(piece, down)
    bx = send(jnp.concatenate([adn[:, :half], aup[:, :half]], 1), cross)
    bdn = send(jnp.concatenate([ax[:, half:], adn[:, :half]], 1), down)
    bup = send(jnp.concatenate([ax[:, half:], aup[:, half:]], 1), up)
    m1 = jnp.concatenate([bx[:, :half], bdn[:, :half]], 1)
    m2 = jnp.concatenate([bx[:, half:], bup[:, :half]], 1)
    m3 = jnp.concatenate([bdn[:, half:], bup[:, half:]], 1)
    cx = send(m3[:, :half], cross)
    cdn = send(m1[:, half:half + quarter], down)
    cup = send(m2[:, half + quarter:], up)
    m4 = jnp.concatenate([cx, cdn, cup], 1)
    return [[piece, ax, aup, adn], [m1, m2, m3], [m4]], order


def tp_reduce_scatter(b, width):
    half, quarter = width // 2, width // 4
    cross, up, down, order = tp_links(width)
    send = lambda value, perm: lax.ppermute(value.astype(jnp.bfloat16), "tp", perm).astype(jnp.float32)
    rx = send(b["m4"][:, :half], cross)
    rup = send(b["m4"][:, half:half + quarter], up)
    rdn = send(b["m4"][:, half + quarter:], down)
    m1, m2, m3 = b["m1"], b["m2"], b["m3"]
    m3 = jnp.concatenate([m3[:, :half] + rx, m3[:, half:]], 1)
    m1 = jnp.concatenate([m1[:, :half], m1[:, half:half + quarter] + rup, m1[:, half + quarter:]], 1)
    m2 = jnp.concatenate([m2[:, :half + quarter], m2[:, half + quarter:] + rdn], 1)
    rx = send(jnp.concatenate([m1[:, :half], m2[:, :half]], 1), cross)
    rup = send(jnp.concatenate([m1[:, half:], m3[:, :half]], 1), up)
    rdn = send(jnp.concatenate([m2[:, half:], m3[:, half:]], 1), down)
    ax = jnp.concatenate([b["ax"][:, :half], b["ax"][:, half:] + rup[:, :half] + rdn[:, :half]], 1)
    adn = jnp.concatenate([b["adn"][:, :half] + rx[:, :half] + rup[:, half:], b["adn"][:, half:]], 1)
    aup = jnp.concatenate([b["aup"][:, :half] + rx[:, half:], b["aup"][:, half:] + rdn[:, half:]], 1)
    return b["own"] + send(ax, cross) + send(adn, up) + send(aup, down)


def tp_sum(values):
    size = 8
    column = values
    for shift in (2, -2, 4):
        column = column + lax.ppermute(values, "tp", [(i, (i + shift) % size) for i in range(size)])
    return column + lax.ppermute(column, "tp", [(i, i ^ 1) for i in range(size)])


def rope_pack(proj, square, gains, cosine, sine, seqs, pos_dev, full_width):
    _, rows, width = proj.shape
    heads = width // HD

    def kernel(proj_ref, square_ref, gain_ref, cos_ref, sin_ref, pack_ref, fresh_ref):
        cos_v = cos_ref[...]
        sin_v = sin_ref[...]
        for c in range(3):
            x = proj_ref[c]
            if c < 2:
                x = x * lax.rsqrt(square_ref[c] / full_width + norm_eps) * gain_ref[c]
            for h in range(heads):
                xh = x[:, h * HD:(h + 1) * HD]
                if c < 2:
                    xh = xh * cos_v + pltpu.roll(xh, HD // 2, 1) * sin_v
                xh = xh.astype(jnp.bfloat16)
                for b in range(seqs):
                    pack_ref[b * heads + h, c] = xh[b * pos_dev:(b + 1) * pos_dev]
                fresh_ref[c, :, h * HD:(h + 1) * HD] = xh[seqs * pos_dev:].astype(jnp.float32)

    return pl.pallas_call(
        kernel,
        out_shape=(
            jax.ShapeDtypeStruct((seqs * heads, 3, pos_dev, HD), jnp.bfloat16),
            jax.ShapeDtypeStruct((3, rows - seqs * pos_dev, width), jnp.float32),
        ),
    )(proj, square, gains, cosine, sine)


def attend_pair(q_all, k_all, v_all, q_new, k_new, v_new, length):
    count = q_all.shape[0]
    scale = HD ** (-0.5)
    bounds = (0, count // 2, count)
    outs = []
    for begin, stop in zip(bounds[:-1], bounds[1:]):
        scores = (
            jnp.dot(q_all[begin:stop], k_all[:stop].T, preferred_element_type=jnp.float32)
            * scale
        )
        query_pos = begin + jnp.arange(stop - begin, dtype=jnp.int32)[:, None]
        key_pos = jnp.arange(stop, dtype=jnp.int32)[None, :]
        valid = (key_pos <= query_pos) & (key_pos < length)
        scores = jnp.where(valid, scores, masked_fill)
        top = jnp.max(scores, -1, keepdims=True)
        weights = jnp.where(valid, jnp.exp(scores - top), 0.0)
        total = jnp.sum(weights, -1, keepdims=True)
        outs.append(
            jnp.dot(weights.astype(jnp.bfloat16), v_all[:stop], preferred_element_type=jnp.float32)
            / total
        )
    prompt_out = jnp.concatenate(outs, 0).astype(jnp.bfloat16)
    new_scores = jnp.dot(k_all, q_new, preferred_element_type=jnp.float32) * scale
    live = jnp.arange(count, dtype=jnp.int32) < length
    new_scores = jnp.where(live, new_scores, masked_fill)
    self_score = jnp.dot(q_new, k_new, preferred_element_type=jnp.float32) * scale
    new_top = jnp.maximum(jnp.max(new_scores), self_score)
    new_weights = jnp.where(live, jnp.exp(new_scores - new_top), 0.0)
    own_weight = jnp.exp(self_score - new_top)
    new_total = jnp.sum(new_weights) + own_weight
    own_rounded = lax.optimization_barrier(own_weight.astype(jnp.bfloat16)).astype(jnp.float32)
    numer = jnp.dot(new_weights.astype(jnp.bfloat16), v_all, preferred_element_type=jnp.float32)
    numer = numer + own_rounded * v_new.astype(jnp.float32)
    return prompt_out, (numer / new_total).astype(jnp.bfloat16)


def body(tokens, new_tokens, w_qkv, w_out, q_gain, k_gain, post_gain, lengths):
    seqs, pos_dev, width_local = tokens.shape
    heads_local = width_local // HD
    full_width = w_qkv.shape[1]
    n_seq = lax.axis_size("seq")
    pairs = seqs * heads_local
    assert pairs == n_seq
    prompt_rows = seqs * pos_dev
    full_len = pos_dev * n_seq
    flat_rows = tokens.reshape(prompt_rows, width_local)
    local_rows = jnp.concatenate([flat_rows, new_tokens], 0)
    rounds, order = tp_gather(local_rows)

    def in_relative_order(weight, axis):
        return [
            lax.dynamic_slice_in_dim(weight, order[name] * width_local, width_local, axis)
            for name in RELATIVE
        ]

    w_blocks = in_relative_order(w_qkv, 1)
    proj, start = None, 0
    for blocks in rounds:
        stop = start + len(blocks)
        term = jnp.einsum(
            "tn,cnf->ctf",
            jnp.concatenate(blocks, 1),
            jnp.concatenate(w_blocks[start:stop], 1),
            preferred_element_type=jnp.float32,
        )
        proj = term if proj is None else proj + term
        start = stop
    query_raw, key_raw = proj[0], proj[1]
    squares = tp_sum(jnp.stack([jnp.sum(query_raw * query_raw, -1), jnp.sum(key_raw * key_raw, -1)]))

    seq_index = lax.axis_index("seq")
    query_pos = seq_index * pos_dev + jnp.arange(pos_dev, dtype=jnp.int32)
    row_pos = jnp.concatenate([jnp.tile(query_pos, seqs), lengths.astype(jnp.int32)], 0)
    half = HD // 2
    freq = rope_base ** (-(jnp.arange(half, dtype=jnp.float32) * 2.0) / HD)
    angle = row_pos.astype(jnp.float32)[:, None] * freq
    cosine, sine = jnp.cos(angle), jnp.sin(angle)
    qkv, fresh = rope_pack(
        proj,
        squares[:, :, None],
        jnp.stack([q_gain, k_gain])[:, None, :],
        jnp.concatenate([cosine, cosine], 1),
        jnp.concatenate([-sine, sine], 1),
        seqs,
        pos_dev,
        full_width,
    )

    got = lax.all_to_all(qkv, "seq", 0, 0, tiled=True)
    full = got.transpose(1, 0, 2, 3).reshape(3, full_len, HD)

    owner = seq_index
    own_prompt = owner // heads_local
    fresh = fresh.astype(jnp.bfloat16).reshape(3, pairs, HD)
    new_q, new_k, new_v = fresh[0, owner], fresh[1, owner], fresh[2, owner]
    prompt_out, new_out = attend_pair(
        full[0], full[1], full[2], new_q, new_k, new_v, lengths[own_prompt]
    )

    pad = 8
    back = jnp.concatenate(
        [prompt_out.reshape(n_seq, pos_dev, HD), jnp.broadcast_to(new_out, (n_seq, pad, HD))], 1
    )
    ret = lax.all_to_all(back, "seq", 0, 0, tiled=True)
    ret = ret.reshape(seqs, heads_local, pos_dev + pad, HD)
    attn_rows = ret[:, :, :pos_dev].transpose(0, 2, 1, 3).reshape(prompt_rows, width_local)
    attn_new = ret[:, :, pos_dev].reshape(seqs, width_local)
    attention = jnp.concatenate([attn_rows, attn_new], 0)

    wo_blocks = in_relative_order(w_out, 1)
    part = {}
    for names in (RELATIVE[7:], RELATIVE[4:7], RELATIVE[:4]):
        columns = [wo_blocks[RELATIVE.index(name)] for name in names]
        value = jnp.dot(attention, jnp.concatenate(columns, 1), preferred_element_type=jnp.float32)
        for i, name in enumerate(names):
            part[name] = value[:, i * width_local:(i + 1) * width_local]
    summed = tp_reduce_scatter(part, width_local)
    square = tp_sum(jnp.sum(summed * summed, -1))
    out = (
        local_rows.astype(jnp.float32)
        + summed * lax.rsqrt(square[:, None] / full_width + norm_eps) * post_gain
    ).astype(jnp.bfloat16)
    return (
        out[:prompt_rows].reshape(seqs, pos_dev, width_local),
        out[prompt_rows:],
    )


def solution(mesh):
    in_specs = (
        P(None, "seq", "tp"),
        P(None, "tp"),
        P(None, None, "tp"),
        P("tp", None),
        P("tp"),
        P("tp"),
        P("tp"),
        P(),
    )
    out_specs = (P(None, "seq", "tp"), P(None, "tp"))
    return jax.shard_map(body, mesh=mesh, in_specs=in_specs, out_specs=out_specs, check_vma=False)
```

profile of v0, /device:TPU:32, one launch (start us, length us, event | category | flops | bytes accessed | tf_op | source)
XLA Modules:
  0.0 194.5 jit_solution(8043406737837035134)
XLA Ops:
  0.6 1.9 pad_maximum_fusion.4
  2.5 3.0 %collective-permute-start.2 = (bf16[516,512]{1,0:T(8,128)(2,1)}, bf16[516,512]{1,0:T(8,128)(2,1)}, u32[]{:S(2)}, u32[]{:S(2)}) collective-permute-start(bf16[516,512]{1,0:T(8,128)(2,1)} %pad_maximum_fusion.4), channel_id=1, source_target_pairs={{0,6},{1,7},{2,0},{3,1},{4,2},{5,3},{6,4},{7,5},{8,14},{9,15},{10,... | collective-permute-start | bytes 1585160 | tf_op jit(solution)/shard_map/ppermute | solution.py:42
  5.5 1.5 collective-permute-start
  7.0 7.4 %constant_dynamic-slice_fusion.12 = (bf16[3,512,512]{2,1,0:T(8,128)(2,1)S(1)}, bf16[3,512,512]{2,1,0:T(8,128)(2,1)S(1)}, bf16[3,512,512]{2,1,0:T(8,128)(2,1)}, b...) fusion(bf16[3,4096,512]{2,1,0:T(8,128)(2,1)} %param.10, ...), kind=kLoop, calls=%fused_computation.144 | loop fusion | bytes 22020124 | tf_op jit(solution)/shard_map/dynamic_slice | solution.py:167
  14.5 1.0 fusion.82
  15.5 3.9 %collective-permute-done = bf16[516,512]{1,0:T(8,128)(2,1)} collective-permute-done((bf16[516,512]{1,0:T(8,128)(2,1)}, bf16[516,512]{1,0:T(8,128)(2,1)}, u32[]{:S(2)}, u32[]{:S(2)}) %collective-permute-start) | collective-permute-done | bytes 528416 | tf_op jit(solution)/shard_map/ppermute | solution.py:42
  19.4 1.0 slice.258
  20.6 1.2 fusion.112
  21.9 1.0 slice.255
  23.0 2.8 %collective-permute-start.4 = (bf16[516,512]{1,0:T(8,128)(2,1)S(1)}, bf16[516,512]{1,0:T(8,128)(2,1)S(1)}, u32[]{:S(2)}, u32[]{:S(2)}) collective-permute-start(bf16[516,512]{1,0:T(8,128)(2,1)S(1)} %get-tuple-element.46), channel_id=1, source_target_pairs={{0,6},{1,7},{2,0},{3,1},{4,2},{5,3},{6,4},{7,5},{8,14},{9,15},{10,... | collective-permute-start | bytes 1585160 | tf_op jit(solution)/shard_map/ppermute | solution.py:42
  25.8 1.5 collective-permute-start.3
  27.4 5.4 %fusion.2 = f32[3,512,516]{1,2,0:T(8,128)S(1)} fusion(bf16[3,512,512]{2,1,0:T(8,128)(2,1)S(1)} %copy-done.4, bf16[3,512,512]{2,1,0:T(8,128)(2,1)S(1)} %copy-done.5, bf16[3,512,512]{2,1,0:T(8,128)(2,1)S(1)} %copy-done.6, bf16[3,512,512]{2,1,0:T(8,128)(2,1)} %get-tuple-element.13, bf16[516,512]{1,0:T(8,128)(2,1)} %collective-permute-done.2, ...), kind=kOutput, calls=%fused_computation.5 | convolution fusion | flops 3282124800 | bytes 11575296 | tf_op jit(solution)/shard_map/tn,cnf->ctf/dot_general | solution.py:175
  32.8 7.5 %collective-permute-done.5 = bf16[516,512]{1,0:T(8,128)(2,1)S(1)} collective-permute-done((bf16[516,512]{1,0:T(8,128)(2,1)S(1)}, bf16[516,512]{1,0:T(8,128)(2,1)S(1)}, u32[]{:S(2)}, u32[]{:S(2)}) %collective-permute-start.5) | collective-permute-done | bytes 528416 | tf_op jit(solution)/shard_map/ppermute | solution.py:42
  40.5 3.3 %collective-permute-start.7 = (bf16[516,128]{1,0:T(8,128)(2,1)S(1)}, bf16[516,128]{1,0:T(8,128)(2,1)S(1)}, u32[]{:S(2)}, u32[]{:S(2)}) collective-permute-start(bf16[516,128]{1,0:T(8,128)(2,1)S(1)} %slice.265), channel_id=1, source_target_pairs={{0,6},{1,7},{2,0},{3,1},{4,2},{5,3},{6,4},{7,5},{8,14},{9,15},{10,... | collective-permute-start | bytes 396296 | tf_op jit(solution)/shard_map/ppermute | solution.py:42
  43.9 0.8 collective-permute-start.6
  44.7 2.8 %fusion.10 = f32[3,512,516]{1,2,0:T(8,128)S(1)} fusion(bf16[3,512,512]{2,1,0:T(8,128)(2,1)S(1)} %copy-done.3, bf16[3,512,512]{2,1,0:T(8,128)(2,1)S(1)} %get-tuple-element.9, bf16[3,512,512]{2,1,0:T(8,128)(2,1)S(1)} %get-tuple-element.8, bf16[516,1536]{1,0:T(8,128)(2,1)S(1)} %slice_dynamic-update-slice_fusion), kind=kOutput, calls=%fused_computation.13 | convolution fusion | flops 2448949248 | bytes 9474048 | tf_op jit(solution)/shard_map/tn,cnf->ctf/dot_general | solution.py:175
  47.6 3.0 %collective-permute-done.6 = bf16[516,256]{1,0:T(8,128)(2,1)S(1)} collective-permute-done((bf16[516,256]{1,0:T(8,128)(2,1)S(1)}, bf16[516,256]{1,0:T(8,128)(2,1)S(1)}, u32[]{:S(2)}, u32[]{:S(2)}) %collective-permute-start.6) | collective-permute-done | bytes 264224 | tf_op jit(solution)/shard_map/ppermute | solution.py:42
  50.6 2.7 %add_bitcast_fusion.proj_ref = f32[3,516,512]{2,1,0:T(8,128)S(1)} fusion(f32[3,512,516]{1,2,0:T(8,128)S(1)} %fusion.2, f32[3,512,516]{1,2,0:T(8,128)S(1)} %fusion.10, bf16[3,4096,512]{2,1,0:T(8,128)(2,1)} %param.10, s32[]{:T(128)S(6)} %select_n.114, bf16[516,128]{1,0:T(8,128)(2,1)S(1)} %collective-permute-done.8, ...), kind=kOutput, calls=%fused_computation.26 | convolution fusion | flops 814768128 | bytes 11612164 | tf_op jit(solution)/shard_map/tn,cnf->ctf/dot_general | solution.py:175
  53.7 1.5 collective-permute-start.10
  55.2 0.6 collective-permute-start.9
  55.8 1.0 pad_maximum_fusion.12
  56.8 2.0 %collective-permute-done.11 = f32[2,516]{1,0:T(2,128)S(1)} collective-permute-done((f32[2,516]{1,0:T(2,128)S(1)}, f32[2,516]{1,0:T(2,128)S(1)}, u32[]{:S(2)}, u32[]{:S(2)}) %collective-permute-start.11) | collective-permute-done | bytes 4160 | tf_op jit(solution)/shard_map/ppermute | solution.py:83
  58.8 1.2 collective-permute-done.9
  60.0 0.6 collective-permute-start.12
  61.3 2.5 %collective-permute-done.12 = f32[2,516]{1,0:T(2,128)S(1)} collective-permute-done((f32[2,516]{1,0:T(2,128)S(1)}, f32[2,516]{1,0:T(2,128)S(1)}, u32[]{:S(2)}, u32[]{:S(2)}) %collective-permute-start.12) | collective-permute-done | bytes 4160 | tf_op jit(solution)/shard_map/ppermute | solution.py:84
  63.8 1.1 copy.10.square_ref
  64.8 4.1 %shard_map.95 = (bf16[16,3,128,128]{3,2,1,0:T(8,128)(2,1)}, f32[3,4,512]{2,1,0:T(4,128)}) custom-call(f32[3,516,512]{2,1,0:T(8,128)} %copy-done, f32[2,516,1]{2,1,0:T(8,128)} %copy.10.square_ref, f32[2,1,512]{2,1,0:T(1,128)} %broadcast_in_dim.43.gain_ref, f32[516,128]{1,0:T(8,128)} %get-tuple-element.61.cos_ref, f32[516,128]{1,0:T(8,128)} %get-tuple-element.62.sin_ref), custom_call_target="tpu_custom_call" | custom-call | tf_op jit(solution)/shard_map/pallas_call | solution.py:107
  68.9 7.7 %all-to-all-start = ((bf16[16,3,128,128]{3,2,1,0:T(8,128)(2,1)}), bf16[16,3,128,128]{3,2,1,0:T(8,128)(2,1)S(1)}, u32[]{:S(2)}, u32[]{:S(2)}) async-start(bf16[16,3,128,128]{3,2,1,0:T(8,128)(2,1)} %get-tuple-element.4), calls=%async_computation | async-start | bytes 3145728 | tf_op jit(solution)/shard_map/all_to_all | solution.py:204
  77.2 0.6 iota_compare_fusion.3
  77.9 0.7 iota_compare_fusion.2
  78.6 0.6 fusion.91
  79.9 16.9 %all-to-all-done = bf16[16,3,128,128]{3,2,1,0:T(8,128)(2,1)S(1)} async-done(((bf16[16,3,128,128]{3,2,1,0:T(8,128)(2,1)}), bf16[16,3,128,128]{3,2,1,0:T(8,128)(2,1)S(1)}, u32[]{:S(2)}, u32[]{:S(2)}) %all-to-all-start) | async-done | bytes 1572896 | tf_op jit(solution)/shard_map/all_to_all | solution.py:204
  97.1 1.3 fusion.83
  99.0 1.3 fusion.86
  100.3 0.8 fusion.108
  101.9 3.9 %fusion.1 = (f32[1024]{0:T(1024)S(1)}, f32[1024,2048]{1,0:T(8,128)S(1)}) fusion(s32[1024]{0:T(1024)S(1)} %iota_add_fusion, pred[2048]{0:T(1024)(128)(4,1)S(1)} %iota_compare_fusion.2, bf16[1024,128]{1,0:T(8,128)(2,1)} %bitcast.97, bf16[2048,128]{1,0:T(8,128)(2,1)S(1)} %bitcast.92), kind=kOutput, calls=%fused_computation.4 | convolution fusion | flops 547355648 | bytes 9185280 | tf_op jit(solution)/shard_map/dot_general | solution.py:123
  105.8 3.9 %fusion.105 = f32[1024]{0:T(1024)S(1)} fusion(f32[1024]{0:T(1024)S(1)} %get-tuple-element.53, f32[1024,2048]{1,0:T(8,128)S(1)} %get-tuple-element.54, pred[2048]{0:T(1024)(128)(4,1)S(1)} %iota_compare_fusion.2, s32[1024]{0:T(1024)S(1)} %iota_add_fusion), kind=kLoop, calls=%fused_computation.178 | loop fusion | flops 14679040 | bytes 8402944 | tf_op jit(solution)/shard_map/reduce_sum | solution.py:132
  109.7 3.6 %fusion.55 = bf16[1024,128]{1,0:T(8,128)(2,1)S(1)} fusion(bf16[2048,128]{1,0:T(8,128)(2,1)S(1)} %bitcast.89, f32[1024]{0:T(1024)S(1)} %fusion.105, f32[1024,2048]{1,0:T(8,128)S(1)} %get-tuple-element.54, f32[1024]{0:T(1024)S(1)} %get-tuple-element.53, s32[1024]{0:T(1024)S(1)} %iota_add_fusion, pred[2048]{0:T(1024)(128)(4,1)S(1)} %iota_compare_fusion.2), kind=kOutput, calls=%fused_computation.58 | convolution fusion | flops 551813120 | bytes 9189376 | tf_op jit(solution)/shard_map/dot_general | solution.py:134
  113.3 1.6 fusion.19
  114.9 2.1 %fusion.68 = f32[1024]{0:T(1024)S(1)} fusion(f32[1024]{0:T(1024)S(1)} %get-tuple-element.55, f32[1024,1024]{0,1:T(8,128)S(1)} %get-tuple-element.56, pred[1024]{0:T(1024)(128)(4,1)S(1)} %iota_compare_fusion.3), kind=kLoop, calls=%fused_computation.73 | loop fusion | flops 7339008 | bytes 4203520 | tf_op jit(solution)/shard_map/reduce_sum | solution.py:132
  117.0 1.1 fusion.58
  118.4 0.9 pad_maximum_fusion.2
  119.2 8.0 %all-to-all-start.1 = ((bf16[16,136,128]{2,1,0:T(8,128)(2,1)}), bf16[16,136,128]{2,1,0:T(8,128)(2,1)S(1)}, u32[]{:S(2)}, u32[]{:S(2)}) async-start(bf16[16,136,128]{2,1,0:T(8,128)(2,1)} %pad_maximum_fusion.2), calls=%async_computation.1 | async-start | bytes 1114112 | tf_op jit(solution)/shard_map/all_to_all | solution.py:219
  127.3 3.4 %constant_dynamic-slice_fusion.6 = (bf16[512,512]{1,0:T(8,128)(2,1)S(1)}, bf16[512,512]{1,0:T(8,128)(2,1)S(1)}, bf16[512,512]{1,0:T(8,128)(2,1)S(1)}, bf16[512,5...) fusion(bf16[512,4096]{1,0:T(8,128)(2,1)} %param.11, ...), kind=kLoop, calls=%fused_computation.137 | loop fusion | bytes 7340060 | tf_op jit(solution)/shard_map/dynamic_slice | solution.py:167
  130.7 5.7 %all-to-all-done.1 = bf16[16,136,128]{2,1,0:T(8,128)(2,1)S(1)} async-done(((bf16[16,136,128]{2,1,0:T(8,128)(2,1)}), bf16[16,136,128]{2,1,0:T(8,128)(2,1)S(1)}, u32[]{:S(2)}, u32[]{:S(2)}) %all-to-all-start.1) | async-done | bytes 557088 | tf_op jit(solution)/shard_map/all_to_all | solution.py:219
  136.9 1.5 convolution_convert_fusion
  138.5 3.2 %collective-permute-start.16 = (bf16[516,128]{1,0:T(8,128)(2,1)S(1)}, bf16[516,128]{1,0:T(8,128)(2,1)S(1)}, u32[]{:S(2)}, u32[]{:S(2)}) collective-permute-start(bf16[516,128]{1,0:T(8,128)(2,1)S(1)} %get-tuple-element.40), channel_id=1, source_target_pairs={{0,6},{1,7},{2,0},{3,1},{4,2},{5,3},{6,4},{7,5},{8,14},{9,15},{10,... | collective-permute-start | bytes 396296 | tf_op jit(solution)/shard_map/ppermute | solution.py:62
  141.7 1.0 fusion.113
  143.3 2.1 %collective-permute-start.19 = (bf16[516,512]{1,0:T(8,128)(2,1)S(1)}, bf16[516,512]{1,0:T(8,128)(2,1)S(1)}, u32[]{:S(2)}, u32[]{:S(2)}) collective-permute-start(bf16[516,512]{1,0:T(8,128)(2,1)S(1)} %pad_maximum_fusion.8), channel_id=1, source_target_pairs={{0,1},{1,0},{2,3},{3,2},{4,5},{5,4},{6,7},{7,6},{8,9},{9,8},{10,11... | collective-permute-start | bytes 1585160 | tf_op jit(solution)/shard_map/ppermute | solution.py:62
  146.1 3.0 %collective-permute-start.17 = (bf16[516,512]{1,0:T(8,128)(2,1)S(1)}, bf16[516,512]{1,0:T(8,128)(2,1)S(1)}, u32[]{:S(2)}, u32[]{:S(2)}) collective-permute-start(bf16[516,512]{1,0:T(8,128)(2,1)S(1)} %fusion.73), channel_id=1, source_target_pairs={{0,6},{1,7},{2,0},{3,1},{4,2},{5,3},{6,4},{7,5},{8,14},{9,15},{10,... | collective-permute-start | bytes 1585160 | tf_op jit(solution)/shard_map/ppermute | solution.py:62
  149.1 3.4 %collective-permute-done.14 = bf16[516,256]{1,0:T(8,128)(2,1)S(1)} collective-permute-done((bf16[516,256]{1,0:T(8,128)(2,1)S(1)}, bf16[516,256]{1,0:T(8,128)(2,1)S(1)}, u32[]{:S(2)}, u32[]{:S(2)}) %collective-permute-start.14) | collective-permute-done | bytes 264224 | tf_op jit(solution)/shard_map/ppermute | solution.py:62
  152.7 1.3 fusion.114
  154.1 9.1 %collective-permute-done.19 = bf16[516,512]{1,0:T(8,128)(2,1)S(1)} collective-permute-done((bf16[516,512]{1,0:T(8,128)(2,1)S(1)}, bf16[516,512]{1,0:T(8,128)(2,1)S(1)}, u32[]{:S(2)}, u32[]{:S(2)}) %collective-permute-start.19) | collective-permute-done | bytes 528416 | tf_op jit(solution)/shard_map/ppermute | solution.py:62
  163.4 3.1 %collective-permute-done.15 = bf16[516,512]{1,0:T(8,128)(2,1)S(1)} collective-permute-done((bf16[516,512]{1,0:T(8,128)(2,1)S(1)}, bf16[516,512]{1,0:T(8,128)(2,1)S(1)}, u32[]{:S(2)}, u32[]{:S(2)}) %collective-permute-start.15) | collective-permute-done | bytes 528416 | tf_op jit(solution)/shard_map/ppermute | solution.py:62
  167.5 2.1 %collective-permute-start.20 = (bf16[516,512]{1,0:T(8,128)(2,1)S(1)}, bf16[516,512]{1,0:T(8,128)(2,1)S(1)}, u32[]{:S(2)}, u32[]{:S(2)}) collective-permute-start(bf16[516,512]{1,0:T(8,128)(2,1)S(1)} %pad_maximum_fusion.9), channel_id=1, source_target_pairs={{0,2},{1,3},{2,4},{3,5},{4,6},{5,7},{6,0},{7,1},{8,10},{9,11},{10,... | collective-permute-start | bytes 1585160 | tf_op jit(solution)/shard_map/ppermute | solution.py:62
  169.6 0.7 collective-permute-start.18
  170.3 8.9 %collective-permute-done.21 = bf16[516,512]{1,0:T(8,128)(2,1)S(1)} collective-permute-done((bf16[516,512]{1,0:T(8,128)(2,1)S(1)}, bf16[516,512]{1,0:T(8,128)(2,1)S(1)}, u32[]{:S(2)}, u32[]{:S(2)}) %collective-permute-start.21) | collective-permute-done | bytes 528416 | tf_op jit(solution)/shard_map/ppermute | solution.py:62
  179.1 1.4 collective-permute-done.20
  181.8 2.5 %collective-permute-start.23 = (f32[516]{0:T(1024)S(1)}, f32[516]{0:T(1024)S(1)}, u32[]{:S(2)}, u32[]{:S(2)}) collective-permute-start(f32[516]{0:T(1024)S(1)} %multiply_reduce_fusion), channel_id=1, source_target_pairs={{0,6},{1,7},{2,0},{3,1},{4,2},{5,3},{6,4},{7,5},{8,14},{9,15},{10,... | collective-permute-start | bytes 6200 | tf_op jit(solution)/shard_map/ppermute | solution.py:83
  184.3 2.1 %collective-permute-done.24 = f32[516]{0:T(1024)S(1)} collective-permute-done((f32[516]{0:T(1024)S(1)}, f32[516]{0:T(1024)S(1)}, u32[]{:S(2)}, u32[]{:S(2)}) %collective-permute-start.24) | collective-permute-done | bytes 2096 | tf_op jit(solution)/shard_map/ppermute | solution.py:83
  186.4 2.7 %collective-permute-done.22 = f32[516]{0:T(1024)S(1)} collective-permute-done((f32[516]{0:T(1024)S(1)}, f32[516]{0:T(1024)S(1)}, u32[]{:S(2)}, u32[]{:S(2)}) %collective-permute-start.22) | collective-permute-done | bytes 2096 | tf_op jit(solution)/shard_map/ppermute | solution.py:83
  189.1 1.2 collective-permute-start.25
  190.3 2.4 %collective-permute-done.25 = f32[516]{0:T(1024)S(1)} collective-permute-done((f32[516]{0:T(1024)S(1)}, f32[516]{0:T(1024)S(1)}, u32[]{:S(2)}, u32[]{:S(2)}) %collective-permute-start.25) | collective-permute-done | bytes 2096 | tf_op jit(solution)/shard_map/ppermute | solution.py:84
  193.1 0.8 slice.301
  (112 shorter events, 8.3 us)
Async XLA Ops:
  2.5 19.3 %collective-permute-start.2 = (bf16[516,512]{1,0:T(8,128)(2,1)}, bf16[516,512]{1,0:T(8,128)(2,1)}, u32[]{:S(2)}, u32[]{:S(2)}) collective-permute-start(bf16[516,512]{1,0:T(8,128)(2,1)} %pad_maximum_fusion.4), channel_id=1, source_target_pairs={{0,6},{1,7},{2,0},{3,1},{4,2},{5,3},{6,4},{7,5},{8,14},{9,15},{10,... | collective-permute-start | bytes 1585160 | tf_op jit(solution)/shard_map/ppermute | solution.py:42
  5.5 15.1 %collective-permute-start.1 = (bf16[516,512]{1,0:T(8,128)(2,1)}, bf16[516,512]{1,0:T(8,128)(2,1)}, u32[]{:S(2)}, u32[]{:S(2)}) collective-permute-start(bf16[516,512]{1,0:T(8,128)(2,1)} %pad_maximum_fusion.4), channel_id=1, source_target_pairs={{0,2},{1,3},{2,4},{3,5},{4,6},{5,7},{6,0},{7,1},{8,10},{9,11},{10,... | collective-permute-start | bytes 1585160 | tf_op jit(solution)/shard_map/ppermute | solution.py:42
  5.5 13.9 %collective-permute-start = (bf16[516,512]{1,0:T(8,128)(2,1)}, bf16[516,512]{1,0:T(8,128)(2,1)}, u32[]{:S(2)}, u32[]{:S(2)}) collective-permute-start(bf16[516,512]{1,0:T(8,128)(2,1)} %pad_maximum_fusion.4), channel_id=1, source_target_pairs={{0,1},{1,0},{2,3},{3,2},{4,5},{5,4},{6,7},{7,6},{8,9},{9,8},{10,11... | collective-permute-start | bytes 1585160 | tf_op jit(solution)/shard_map/ppermute | solution.py:42
  7.0 7.4 %copy-start.14 = (s32[4]{0:T(128)S(1)}, s32[4]{0:T(128)}, u32[]{:S(2)}) copy-start(s32[4]{0:T(128)} %param.15) | copy-start | bytes 52
  14.5 12.9 %copy-start.6 = (bf16[3,512,512]{2,1,0:T(8,128)(2,1)S(1)}, bf16[3,512,512]{2,1,0:T(8,128)(2,1)}, u32[]{:S(2)}) copy-start(bf16[3,512,512]{2,1,0:T(8,128)(2,1)} %get-tuple-element.12) | copy-start | bytes 4718596
  20.4 6.9 %copy-start.1 = (bf16[4,128,512]{2,1,0:T(8,128)(2,1)S(1)}, bf16[4,128,512]{2,1,0:T(8,128)(2,1)}, u32[]{:S(2)}) copy-start(bf16[4,128,512]{2,1,0:T(8,128)(2,1)} %param.8) | copy-start | bytes 1572868
  20.4 6.9 %copy-start.4 = (bf16[3,512,512]{2,1,0:T(8,128)(2,1)S(1)}, bf16[3,512,512]{2,1,0:T(8,128)(2,1)}, u32[]{:S(2)}) copy-start(bf16[3,512,512]{2,1,0:T(8,128)(2,1)} %get-tuple-element.10) | copy-start | bytes 4718596
  20.4 6.9 %copy-start.5 = (bf16[3,512,512]{2,1,0:T(8,128)(2,1)S(1)}, bf16[3,512,512]{2,1,0:T(8,128)(2,1)}, u32[]{:S(2)}) copy-start(bf16[3,512,512]{2,1,0:T(8,128)(2,1)} %get-tuple-element.11) | copy-start | bytes 4718596
  20.4 6.9 %copy-start.10 = (bf16[4,512]{1,0:T(4,128)(2,1)S(1)}, bf16[4,512]{1,0:T(4,128)(2,1)}, u32[]{:S(2)}) copy-start(bf16[4,512]{1,0:T(4,128)(2,1)} %param.9) | copy-start | bytes 12292
  23.0 17.4 %collective-permute-start.4 = (bf16[516,512]{1,0:T(8,128)(2,1)S(1)}, bf16[516,512]{1,0:T(8,128)(2,1)S(1)}, u32[]{:S(2)}, u32[]{:S(2)}) collective-permute-start(bf16[516,512]{1,0:T(8,128)(2,1)S(1)} %get-tuple-element.46), channel_id=1, source_target_pairs={{0,6},{1,7},{2,0},{3,1},{4,2},{5,3},{6,4},{7,5},{8,14},{9,15},{10,... | collective-permute-start | bytes 1585160 | tf_op jit(solution)/shard_map/ppermute | solution.py:42
  25.8 17.9 %collective-permute-start.3 = (bf16[516,512]{1,0:T(8,128)(2,1)S(1)}, bf16[516,512]{1,0:T(8,128)(2,1)S(1)}, u32[]{:S(2)}, u32[]{:S(2)}) collective-permute-start(bf16[516,512]{1,0:T(8,128)(2,1)S(1)} %get-tuple-element.47), channel_id=1, source_target_pairs={{0,1},{1,0},{2,3},{3,2},{4,5},{5,4},{6,7},{7,6},{8,9},{9,8},{10,11... | collective-permute-start | bytes 1585160 | tf_op jit(solution)/shard_map/ppermute | solution.py:42
  27.3 13.0 %collective-permute-start.5 = (bf16[516,512]{1,0:T(8,128)(2,1)S(1)}, bf16[516,512]{1,0:T(8,128)(2,1)S(1)}, u32[]{:S(2)}, u32[]{:S(2)}) collective-permute-start(bf16[516,512]{1,0:T(8,128)(2,1)S(1)} %get-tuple-element.45), channel_id=1, source_target_pairs={{0,2},{1,3},{2,4},{3,5},{4,6},{5,7},{6,0},{7,1},{8,10},{9,11},{10,... | collective-permute-start | bytes 1585160 | tf_op jit(solution)/shard_map/ppermute | solution.py:42
  32.8 11.9 %copy-start.3 = (bf16[3,512,512]{2,1,0:T(8,128)(2,1)S(1)}, bf16[3,512,512]{2,1,0:T(8,128)(2,1)}, u32[]{:S(2)}) copy-start(bf16[3,512,512]{2,1,0:T(8,128)(2,1)} %get-tuple-element.14) | copy-start | bytes 4718596
  40.3 7.2 %collective-permute-start.8 = (bf16[516,128]{1,0:T(8,128)(2,1)S(1)}, bf16[516,128]{1,0:T(8,128)(2,1)S(1)}, u32[]{:S(2)}, u32[]{:S(2)}) collective-permute-start(bf16[516,128]{1,0:T(8,128)(2,1)S(1)} %slice.266), channel_id=1, source_target_pairs={{0,2},{1,3},{2,4},{3,5},{4,6},{5,7},{6,0},{7,1},{8,10},{9,11},{10,... | collective-permute-start | bytes 396296 | tf_op jit(solution)/shard_map/ppermute | solution.py:42
  40.5 7.1 %collective-permute-start.7 = (bf16[516,128]{1,0:T(8,128)(2,1)S(1)}, bf16[516,128]{1,0:T(8,128)(2,1)S(1)}, u32[]{:S(2)}, u32[]{:S(2)}) collective-permute-start(bf16[516,128]{1,0:T(8,128)(2,1)S(1)} %slice.265), channel_id=1, source_target_pairs={{0,6},{1,7},{2,0},{3,1},{4,2},{5,3},{6,4},{7,5},{8,14},{9,15},{10,... | collective-permute-start | bytes 396296 | tf_op jit(solution)/shard_map/ppermute | solution.py:42
  43.9 6.7 %collective-permute-start.6 = (bf16[516,256]{1,0:T(8,128)(2,1)S(1)}, bf16[516,256]{1,0:T(8,128)(2,1)S(1)}, u32[]{:S(2)}, u32[]{:S(2)}) collective-permute-start(bf16[516,256]{1,0:T(8,128)(2,1)S(1)} %get-tuple-element.41), channel_id=1, source_target_pairs={{0,1},{1,0},{2,3},{3,2},{4,5},{5,4},{6,7},{7,6},{8,9},{9,8},{10,11... | collective-permute-start | bytes 792584 | tf_op jit(solution)/shard_map/ppermute | solution.py:42
  53.3 11.5 %copy-start = (f32[3,516,512]{2,1,0:T(8,128)}, f32[3,516,512]{2,1,0:T(8,128)S(1)}, u32[]{:S(2)}) copy-start(f32[3,516,512]{2,1,0:T(8,128)S(1)} %add_bitcast_fusion.proj_ref) | copy-start | bytes 9510916
  53.3 7.4 %copy-start.12 = (f32[512]{0:T(512)S(1)}, f32[512]{0:T(512)}, u32[]{:S(2)}) copy-start(f32[512]{0:T(512)} %param.13) | copy-start | bytes 6148
  53.3 7.3 %copy-start.13 = (f32[512]{0:T(512)S(1)}, f32[512]{0:T(512)}, u32[]{:S(2)}) copy-start(f32[512]{0:T(512)} %param.12) | copy-start | bytes 6148
  53.6 5.2 %collective-permute-start.11 = (f32[2,516]{1,0:T(2,128)S(1)}, f32[2,516]{1,0:T(2,128)S(1)}, u32[]{:S(2)}, u32[]{:S(2)}) collective-permute-start(f32[2,516]{1,0:T(2,128)S(1)} %pad_maximum_fusion.14), channel_id=1, source_target_pairs={{0,4},{1,5},{2,6},{3,7},{4,0},{5,1},{6,2},{7,3},{8,12},{9,13},{10,... | collective-permute-start | bytes 12392 | tf_op jit(solution)/shard_map/ppermute | solution.py:83
  53.7 5.1 %collective-permute-start.10 = (f32[2,516]{1,0:T(2,128)S(1)}, f32[2,516]{1,0:T(2,128)S(1)}, u32[]{:S(2)}, u32[]{:S(2)}) collective-permute-start(f32[2,516]{1,0:T(2,128)S(1)} %pad_maximum_fusion.14), channel_id=1, source_target_pairs={{0,6},{1,7},{2,0},{3,1},{4,2},{5,3},{6,4},{7,5},{8,14},{9,15},{10,... | collective-permute-start | bytes 12392 | tf_op jit(solution)/shard_map/ppermute | solution.py:83
  55.2 4.8 %collective-permute-start.9 = (f32[2,516]{1,0:T(2,128)S(1)}, f32[2,516]{1,0:T(2,128)S(1)}, u32[]{:S(2)}, u32[]{:S(2)}) collective-permute-start(f32[2,516]{1,0:T(2,128)S(1)} %pad_maximum_fusion.14), channel_id=1, source_target_pairs={{0,2},{1,3},{2,4},{3,5},{4,6},{5,7},{6,0},{7,1},{8,10},{9,11},{10,... | collective-permute-start | bytes 12392 | tf_op jit(solution)/shard_map/ppermute | solution.py:83
  60.0 3.7 %collective-permute-start.12 = (f32[2,516]{1,0:T(2,128)S(1)}, f32[2,516]{1,0:T(2,128)S(1)}, u32[]{:S(2)}, u32[]{:S(2)}) collective-permute-start(f32[2,516]{1,0:T(2,128)S(1)} %add_add_fusion), channel_id=1, source_target_pairs={{0,1},{1,0},{2,3},{3,2},{4,5},{5,4},{6,7},{7,6},{8,9},{9,8},{10,11... | collective-permute-start | bytes 12392 | tf_op jit(solution)/shard_map/ppermute | solution.py:84
  68.9 9.6 %copy-start.9 = (f32[3,4,512]{2,1,0:T(4,128)S(1)}, f32[3,4,512]{2,1,0:T(4,128)}, u32[]{:S(2)}) copy-start(f32[3,4,512]{2,1,0:T(4,128)} %get-tuple-element.5) | copy-start | bytes 73732
  68.9 27.8 %all-to-all-start = ((bf16[16,3,128,128]{3,2,1,0:T(8,128)(2,1)}), bf16[16,3,128,128]{3,2,1,0:T(8,128)(2,1)S(1)}, u32[]{:S(2)}, u32[]{:S(2)}) async-start(bf16[16,3,128,128]{3,2,1,0:T(8,128)(2,1)} %get-tuple-element.4), calls=%async_computation | async-start | bytes 3145728 | tf_op jit(solution)/shard_map/all_to_all | solution.py:204
  119.2 17.1 %all-to-all-start.1 = ((bf16[16,136,128]{2,1,0:T(8,128)(2,1)}), bf16[16,136,128]{2,1,0:T(8,128)(2,1)S(1)}, u32[]{:S(2)}, u32[]{:S(2)}) async-start(bf16[16,136,128]{2,1,0:T(8,128)(2,1)} %pad_maximum_fusion.2), calls=%async_computation.1 | async-start | bytes 1114112 | tf_op jit(solution)/shard_map/all_to_all | solution.py:219
  138.4 7.5 %collective-permute-start.13 = (bf16[516,128]{1,0:T(8,128)(2,1)S(1)}, bf16[516,128]{1,0:T(8,128)(2,1)S(1)}, u32[]{:S(2)}, u32[]{:S(2)}) collective-permute-start(bf16[516,128]{1,0:T(8,128)(2,1)S(1)} %get-tuple-element.39), channel_id=1, source_target_pairs={{0,2},{1,3},{2,4},{3,5},{4,6},{5,7},{6,0},{7,1},{8,10},{9,11},{10,... | collective-permute-start | bytes 396296 | tf_op jit(solution)/shard_map/ppermute | solution.py:62
  138.5 7.4 %collective-permute-start.16 = (bf16[516,128]{1,0:T(8,128)(2,1)S(1)}, bf16[516,128]{1,0:T(8,128)(2,1)S(1)}, u32[]{:S(2)}, u32[]{:S(2)}) collective-permute-start(bf16[516,128]{1,0:T(8,128)(2,1)S(1)} %get-tuple-element.40), channel_id=1, source_target_pairs={{0,6},{1,7},{2,0},{3,1},{4,2},{5,3},{6,4},{7,5},{8,14},{9,15},{10,... | collective-permute-start | bytes 396296 | tf_op jit(solution)/shard_map/ppermute | solution.py:62
  142.9 9.6 %collective-permute-start.14 = (bf16[516,256]{1,0:T(8,128)(2,1)S(1)}, bf16[516,256]{1,0:T(8,128)(2,1)S(1)}, u32[]{:S(2)}, u32[]{:S(2)}) collective-permute-start(bf16[516,256]{1,0:T(8,128)(2,1)S(1)} %slice.284), channel_id=1, source_target_pairs={{0,1},{1,0},{2,3},{3,2},{4,5},{5,4},{6,7},{7,6},{8,9},{9,8},{10,11... | collective-permute-start | bytes 792584 | tf_op jit(solution)/shard_map/ppermute | solution.py:62
  143.3 19.9 %collective-permute-start.19 = (bf16[516,512]{1,0:T(8,128)(2,1)S(1)}, bf16[516,512]{1,0:T(8,128)(2,1)S(1)}, u32[]{:S(2)}, u32[]{:S(2)}) collective-permute-start(bf16[516,512]{1,0:T(8,128)(2,1)S(1)} %pad_maximum_fusion.8), channel_id=1, source_target_pairs={{0,1},{1,0},{2,3},{3,2},{4,5},{5,4},{6,7},{7,6},{8,9},{9,8},{10,11... | collective-permute-start | bytes 1585160 | tf_op jit(solution)/shard_map/ppermute | solution.py:62
  145.9 6.8 %copy-start.7 = (bf16[512,512]{1,0:T(8,128)(2,1)S(1)}, bf16[512,512]{1,0:T(8,128)(2,1)}, u32[]{:S(2)}) copy-start(bf16[512,512]{1,0:T(8,128)(2,1)} %get-tuple-element.23) | copy-start | bytes 1572868
  145.9 6.8 %copy-start.8 = (bf16[512,512]{1,0:T(8,128)(2,1)S(1)}, bf16[512,512]{1,0:T(8,128)(2,1)}, u32[]{:S(2)}) copy-start(bf16[512,512]{1,0:T(8,128)(2,1)} %get-tuple-element.24) | copy-start | bytes 1572868
  146.1 17.2 %collective-permute-start.17 = (bf16[516,512]{1,0:T(8,128)(2,1)S(1)}, bf16[516,512]{1,0:T(8,128)(2,1)S(1)}, u32[]{:S(2)}, u32[]{:S(2)}) collective-permute-start(bf16[516,512]{1,0:T(8,128)(2,1)S(1)} %fusion.73), channel_id=1, source_target_pairs={{0,6},{1,7},{2,0},{3,1},{4,2},{5,3},{6,4},{7,5},{8,14},{9,15},{10,... | collective-permute-start | bytes 1585160 | tf_op jit(solution)/shard_map/ppermute | solution.py:62
  152.6 14.0 %collective-permute-start.15 = (bf16[516,512]{1,0:T(8,128)(2,1)S(1)}, bf16[516,512]{1,0:T(8,128)(2,1)S(1)}, u32[]{:S(2)}, u32[]{:S(2)}) collective-permute-start(bf16[516,512]{1,0:T(8,128)(2,1)S(1)} %pad_maximum_fusion.6), channel_id=1, source_target_pairs={{0,2},{1,3},{2,4},{3,5},{4,6},{5,7},{6,0},{7,1},{8,10},{9,11},{10,... | collective-permute-start | bytes 1585160 | tf_op jit(solution)/shard_map/ppermute | solution.py:62
  167.3 11.8 %collective-permute-start.21 = (bf16[516,512]{1,0:T(8,128)(2,1)S(1)}, bf16[516,512]{1,0:T(8,128)(2,1)S(1)}, u32[]{:S(2)}, u32[]{:S(2)}) collective-permute-start(bf16[516,512]{1,0:T(8,128)(2,1)S(1)} %pad_maximum_fusion.10), channel_id=1, source_target_pairs={{0,6},{1,7},{2,0},{3,1},{4,2},{5,3},{6,4},{7,5},{8,14},{9,15},{10,... | collective-permute-start | bytes 1585160 | tf_op jit(solution)/shard_map/ppermute | solution.py:62
  167.4 25.3 %copy-start.2 = (bf16[4,128,512]{2,1,0:T(8,128)(2,1)S(1)}, bf16[4,128,512]{2,1,0:T(8,128)(2,1)}, u32[]{:S(2)}) copy-start(bf16[4,128,512]{2,1,0:T(8,128)(2,1)} %param.8) | copy-start | bytes 1572868
  167.4 25.3 %copy-start.11 = (f32[512]{0:T(512)S(1)}, f32[512]{0:T(512)}, u32[]{:S(2)}) copy-start(f32[512]{0:T(512)} %param.14) | copy-start | bytes 6148
  167.5 13.0 %collective-permute-start.20 = (bf16[516,512]{1,0:T(8,128)(2,1)S(1)}, bf16[516,512]{1,0:T(8,128)(2,1)S(1)}, u32[]{:S(2)}, u32[]{:S(2)}) collective-permute-start(bf16[516,512]{1,0:T(8,128)(2,1)S(1)} %pad_maximum_fusion.9), channel_id=1, source_target_pairs={{0,2},{1,3},{2,4},{3,5},{4,6},{5,7},{6,0},{7,1},{8,10},{9,11},{10,... | collective-permute-start | bytes 1585160 | tf_op jit(solution)/shard_map/ppermute | solution.py:62
  169.6 11.3 %collective-permute-start.18 = (bf16[516,512]{1,0:T(8,128)(2,1)S(1)}, bf16[516,512]{1,0:T(8,128)(2,1)S(1)}, u32[]{:S(2)}, u32[]{:S(2)}) collective-permute-start(bf16[516,512]{1,0:T(8,128)(2,1)S(1)} %pad_maximum_fusion.7), channel_id=1, source_target_pairs={{0,1},{1,0},{2,3},{3,2},{4,5},{5,4},{6,7},{7,6},{8,9},{9,8},{10,11... | collective-permute-start | bytes 1585160 | tf_op jit(solution)/shard_map/ppermute | solution.py:62
  181.2 5.2 %collective-permute-start.24 = (f32[516]{0:T(1024)S(1)}, f32[516]{0:T(1024)S(1)}, u32[]{:S(2)}, u32[]{:S(2)}) collective-permute-start(f32[516]{0:T(1024)S(1)} %multiply_reduce_fusion), channel_id=1, source_target_pairs={{0,4},{1,5},{2,6},{3,7},{4,0},{5,1},{6,2},{7,3},{8,12},{9,13},{10,... | collective-permute-start | bytes 6200 | tf_op jit(solution)/shard_map/ppermute | solution.py:83
  181.8 4.6 %collective-permute-start.23 = (f32[516]{0:T(1024)S(1)}, f32[516]{0:T(1024)S(1)}, u32[]{:S(2)}, u32[]{:S(2)}) collective-permute-start(f32[516]{0:T(1024)S(1)} %multiply_reduce_fusion), channel_id=1, source_target_pairs={{0,6},{1,7},{2,0},{3,1},{4,2},{5,3},{6,4},{7,5},{8,14},{9,15},{10,... | collective-permute-start | bytes 6200 | tf_op jit(solution)/shard_map/ppermute | solution.py:83
  184.3 4.8 %collective-permute-start.22 = (f32[516]{0:T(1024)S(1)}, f32[516]{0:T(1024)S(1)}, u32[]{:S(2)}, u32[]{:S(2)}) collective-permute-start(f32[516]{0:T(1024)S(1)} %multiply_reduce_fusion), channel_id=1, source_target_pairs={{0,2},{1,3},{2,4},{3,5},{4,6},{5,7},{6,0},{7,1},{8,10},{9,11},{10,... | collective-permute-start | bytes 6200 | tf_op jit(solution)/shard_map/ppermute | solution.py:83
  189.1 3.6 %collective-permute-start.25 = (f32[516]{0:T(1024)S(1)}, f32[516]{0:T(1024)S(1)}, u32[]{:S(2)}, u32[]{:S(2)}) collective-permute-start(f32[516]{0:T(1024)S(1)} %add_add_fusion.1), channel_id=1, source_target_pairs={{0,1},{1,0},{2,3},{3,2},{4,5},{5,4},{6,7},{7,6},{8,9},{9,8},{10,11... | collective-permute-start | bytes 6200 | tf_op jit(solution)/shard_map/ppermute | solution.py:84
where the time goes:
time: 195 us
  waiting for transfers between devices  76.8 us (39%)
  starting transfers between devices  47.5 us (24%)
  matrix products  25.4 us (13%)
  local copies, waits for them, and re-layouts  19.5 us (10%)
  other arithmetic  17.9 us (9%)
  Pallas kernels  4.1 us (2%)
  between operations  3.37 us (2%)
    ppermute x9, waiting for transfers between devices, tp_reduce_scatter(): lax.ppermute(value.astype(jnp.bfloat16), 'tp', perm).astype(jnp.float32)  26.8 us
    all_to_all x1, waiting for transfers between devices, body(): got = lax.all_to_all(qkv, 'seq', 0, 0, tiled=True)  16.9 us
    ppermute x9, waiting for transfers between devices, tp_gather(): send = lambda value, perm: lax.ppermute(value, 'tp', perm)  14.6 us
    ppermute x9, starting transfers between devices, tp_gather(): send = lambda value, perm: lax.ppermute(value, 'tp', perm)  13 us
    ppermute x9, starting transfers between devices, tp_reduce_scatter(): lax.ppermute(value.astype(jnp.bfloat16), 'tp', perm).astype(jnp.float32)  11.7 us
    dot_general x3, matrix products, body(): jnp.einsum('tn,cnf->ctf', jnp.concatenate(blocks, 1), jnp.concatenate(w_b...  11 us
    dynamic_slice x2, local copies, waits for them, and re-layouts, in_relative_order(): lax.dynamic_slice_in_dim(weight, order[name] * width_local, width_local,...  10.8 us
    all_to_all x1, starting transfers between devices, body(): ret = lax.all_to_all(back, 'seq', 0, 0, tiled=True)  8.03 us
  transfers between devices with their start and end apart: 28, of which 19 were waited for; matrix products, arithmetic and copies ran while one was open for 15% of the time, Pallas kernels for 0%

commit v1 on v0

--- a/solution.py
+++ b/solution.py
@@ -49,10 +49,9 @@
     m1 = jnp.concatenate([bx[:, :half], bdn[:, :half]], 1)
     m2 = jnp.concatenate([bx[:, half:], bup[:, :half]], 1)
     m3 = jnp.concatenate([bdn[:, half:], bup[:, half:]], 1)
-    cx = send(m3[:, :half], cross)
-    cdn = send(m1[:, half:half + quarter], down)
-    cup = send(m2[:, half + quarter:], up)
-    m4 = jnp.concatenate([cx, cdn, cup], 1)
+    cdn = send(m1[:, :half], down)
+    cup = send(m2[:, half:], up)
+    m4 = jnp.concatenate([cdn, cup], 1)
     return [[piece, ax, aup, adn], [m1, m2, m3], [m4]], order
 
 
@@ -60,13 +59,11 @@
     half, quarter = width // 2, width // 4
     cross, up, down, order = tp_links(width)
     send = lambda value, perm: lax.ppermute(value.astype(jnp.bfloat16), "tp", perm).astype(jnp.float32)
-    rx = send(b["m4"][:, :half], cross)
-    rup = send(b["m4"][:, half:half + quarter], up)
-    rdn = send(b["m4"][:, half + quarter:], down)
+    rup = send(b["m4"][:, :half], up)
+    rdn = send(b["m4"][:, half:], down)
     m1, m2, m3 = b["m1"], b["m2"], b["m3"]
-    m3 = jnp.concatenate([m3[:, :half] + rx, m3[:, half:]], 1)
-    m1 = jnp.concatenate([m1[:, :half], m1[:, half:half + quarter] + rup, m1[:, half + quarter:]], 1)
-    m2 = jnp.concatenate([m2[:, :half + quarter], m2[:, half + quarter:] + rdn], 1)
+    m1 = jnp.concatenate([m1[:, :half] + rup, m1[:, half:]], 1)
+    m2 = jnp.concatenate([m2[:, :half], m2[:, half:] + rdn], 1)
     rx = send(jnp.concatenate([m1[:, :half], m2[:, :half]], 1), cross)
     rup = send(jnp.concatenate([m1[:, half:], m3[:, :half]], 1), up)
     rdn = send(jnp.concatenate([m2[:, half:], m3[:, half:]], 1), down)

time: 195 us -> 192 us (0.985)
  waiting for transfers between devices: 76.8 us -> 74.6 us
    ppermute x9 -> x8, waiting for transfers between devices: 14.6 us -> 9.46 us  [tp_gather(): send = lambda value, perm: lax.ppermute(value, 'tp', perm)]
    ppermute x9 -> x8, waiting for transfers between devices: 26.8 us -> 30.4 us  [tp_reduce_scatter(): lax.ppermute(value.astype(jnp.bfloat16), 'tp', perm).astype(jnp.float32)]
    ppermute x6, starting transfers between devices: 5.23 us -> 8.39 us  [tp_sum(): lax.ppermute(values, 'tp', [(i, (i + shift) % size) for i in range(size)])]
    ppermute x9 -> x8, starting transfers between devices: 11.7 us -> 9.08 us  [tp_reduce_scatter(): lax.ppermute(value.astype(jnp.bfloat16), 'tp', perm).astype(jnp.float32)]
    ppermute x9 -> x8, starting transfers between devices: 13 us -> 13.3 us  [tp_gather(): send = lambda value, perm: lax.ppermute(value, 'tp', perm)]
  transfers between devices with their start and end apart: 28 -> 26, of which waited for: 19 -> 19; matrix products, arithmetic and copies ran while one was open for 15% -> 15% of each run, Pallas kernels for 0% -> 0%
where the time goes in v1:
time: 192 us
  waiting for transfers between devices  74.6 us (39%)
  starting transfers between devices  47.6 us (25%)
  matrix products  25.4 us (13%)
  local copies, waits for them, and re-layouts  19.4 us (10%)
  other arithmetic  17.7 us (9%)
  Pallas kernels  4.1 us (2%)
  between operations  3.14 us (2%)
    ppermute x8, waiting for transfers between devices, tp_reduce_scatter(): lax.ppermute(value.astype(jnp.bfloat16), 'tp', perm).astype(jnp.float32)  30.4 us
    all_to_all x1, waiting for transfers between devices, body(): got = lax.all_to_all(qkv, 'seq', 0, 0, tiled=True)  16.9 us
    ppermute x8, starting transfers between devices, tp_gather(): send = lambda value, perm: lax.ppermute(value, 'tp', perm)  13.3 us
    dot_general x3, matrix products, body(): jnp.einsum('tn,cnf->ctf', jnp.concatenate(blocks, 1), jnp.concatenate(w_b...  11 us
    dynamic_slice x2, local copies, waits for them, and re-layouts, in_relative_order(): lax.dynamic_slice_in_dim(weight, order[name] * width_local, width_local,...  10.8 us
    ppermute x8, waiting for transfers between devices, tp_gather(): send = lambda value, perm: lax.ppermute(value, 'tp', perm)  9.46 us
    ppermute x8, starting transfers between devices, tp_reduce_scatter(): lax.ppermute(value.astype(jnp.bfloat16), 'tp', perm).astype(jnp.float32)  9.08 us
    ppermute x6, starting transfers between devices, tp_sum(): lax.ppermute(values, 'tp', [(i, (i + shift) % size) for i in range(size)])  8.39 us
  transfers between devices with their start and end apart: 26, of which 19 were waited for; matrix products, arithmetic and copies ran while one was open for 15% of the time, Pallas kernels for 0%

profile of v1, /device:TPU:32, one launch (start us, length us, event | category | flops | bytes accessed | tf_op | source)
XLA Modules:
  0.0 191.9 jit_solution(3992631590021195403)
XLA Ops:
  0.6 1.9 pad_maximum_fusion.3
  2.5 3.0 %collective-permute-start.2 = (bf16[516,512]{1,0:T(8,128)(2,1)}, bf16[516,512]{1,0:T(8,128)(2,1)}, u32[]{:S(2)}, u32[]{:S(2)}) collective-permute-start(bf16[516,512]{1,0:T(8,128)(2,1)} %pad_maximum_fusion.3), channel_id=1, source_target_pairs={{0,6},{1,7},{2,0},{3,1},{4,2},{5,3},{6,4},{7,5},{8,14},{9,15},{10,... | collective-permute-start | bytes 1585160 | tf_op jit(solution)/shard_map/ppermute | solution.py:42
  5.5 1.5 collective-permute-start
  7.0 7.4 %constant_dynamic-slice_fusion.12 = (bf16[3,512,512]{2,1,0:T(8,128)(2,1)S(1)}, bf16[3,512,512]{2,1,0:T(8,128)(2,1)S(1)}, bf16[3,512,512]{2,1,0:T(8,128)(2,1)}, b...) fusion(bf16[3,4096,512]{2,1,0:T(8,128)(2,1)} %param.10, ...), kind=kLoop, calls=%fused_computation.139 | loop fusion | bytes 22020124 | tf_op jit(solution)/shard_map/dynamic_slice | solution.py:164
  14.4 1.0 fusion.78
  15.5 3.9 %collective-permute-done = bf16[516,512]{1,0:T(8,128)(2,1)} collective-permute-done((bf16[516,512]{1,0:T(8,128)(2,1)}, bf16[516,512]{1,0:T(8,128)(2,1)}, u32[]{:S(2)}, u32[]{:S(2)}) %collective-permute-start) | collective-permute-done | bytes 528416 | tf_op jit(solution)/shard_map/ppermute | solution.py:42
  19.4 1.0 slice.227
  20.6 1.2 fusion.109
  21.8 1.0 slice.224
  23.2 1.5 collective-permute-start.3
  24.7 3.1 %collective-permute-start.4 = (bf16[516,512]{1,0:T(8,128)(2,1)S(1)}, bf16[516,512]{1,0:T(8,128)(2,1)S(1)}, u32[]{:S(2)}, u32[]{:S(2)}) collective-permute-start(bf16[516,512]{1,0:T(8,128)(2,1)S(1)} %get-tuple-element.49), channel_id=1, source_target_pairs={{0,6},{1,7},{2,0},{3,1},{4,2},{5,3},{6,4},{7,5},{8,14},{9,15},{10,... | collective-permute-start | bytes 1585160 | tf_op jit(solution)/shard_map/ppermute | solution.py:42
  27.8 5.4 %fusion.2 = f32[3,512,516]{1,2,0:T(8,128)S(1)} fusion(bf16[3,512,512]{2,1,0:T(8,128)(2,1)S(1)} %copy-done.4, bf16[3,512,512]{2,1,0:T(8,128)(2,1)S(1)} %copy-done.5, bf16[3,512,512]{2,1,0:T(8,128)(2,1)S(1)} %copy-done.6, bf16[3,512,512]{2,1,0:T(8,128)(2,1)} %get-tuple-element.13, bf16[516,512]{1,0:T(8,128)(2,1)} %collective-permute-done.2, ...), kind=kOutput, calls=%fused_computation.5 | convolution fusion | flops 3282124800 | bytes 11575296 | tf_op jit(solution)/shard_map/tn,cnf->ctf/dot_general | solution.py:172
  33.3 2.5 %collective-permute-done.3 = bf16[516,512]{1,0:T(8,128)(2,1)S(1)} collective-permute-done((bf16[516,512]{1,0:T(8,128)(2,1)S(1)}, bf16[516,512]{1,0:T(8,128)(2,1)S(1)}, u32[]{:S(2)}, u32[]{:S(2)}) %collective-permute-start.3) | collective-permute-done | bytes 528416 | tf_op jit(solution)/shard_map/ppermute | solution.py:42
  35.8 1.6 collective-permute-done.4
  37.5 1.5 collective-permute-start.7
  39.0 2.6 %collective-permute-start.6 = (bf16[516,256]{1,0:T(8,128)(2,1)S(1)}, bf16[516,256]{1,0:T(8,128)(2,1)S(1)}, u32[]{:S(2)}, u32[]{:S(2)}) collective-permute-start(bf16[516,256]{1,0:T(8,128)(2,1)S(1)} %get-tuple-element.42), channel_id=1, source_target_pairs={{0,6},{1,7},{2,0},{3,1},{4,2},{5,3},{6,4},{7,5},{8,14},{9,15},{10,... | collective-permute-start | bytes 792584 | tf_op jit(solution)/shard_map/ppermute | solution.py:42
  41.6 2.8 %fusion.10 = f32[3,512,516]{1,2,0:T(8,128)S(1)} fusion(bf16[3,512,512]{2,1,0:T(8,128)(2,1)S(1)} %copy-done.3, bf16[3,512,512]{2,1,0:T(8,128)(2,1)S(1)} %get-tuple-element.9, bf16[3,512,512]{2,1,0:T(8,128)(2,1)S(1)} %get-tuple-element.8, bf16[516,1536]{1,0:T(8,128)(2,1)S(1)} %slice_dynamic-update-slice_fusion), kind=kOutput, calls=%fused_computation.13 | convolution fusion | flops 2448949248 | bytes 9474048 | tf_op jit(solution)/shard_map/tn,cnf->ctf/dot_general | solution.py:172
  44.4 1.2 collective-permute-done.7
  45.6 2.7 %add_bitcast_fusion.proj_ref = f32[3,516,512]{2,1,0:T(8,128)S(1)} fusion(f32[3,512,516]{1,2,0:T(8,128)S(1)} %fusion.2, f32[3,512,516]{1,2,0:T(8,128)S(1)} %fusion.10, bf16[3,4096,512]{2,1,0:T(8,128)(2,1)} %param.10, s32[]{:T(128)S(6)} %select_n.114, bf16[516,256]{1,0:T(8,128)(2,1)S(1)} %collective-permute-done.7, ...), kind=kOutput, calls=%fused_computation.26 | convolution fusion | flops 814239744 | bytes 11612164 | tf_op jit(solution)/shard_map/tn,cnf->ctf/dot_general | solution.py:172
  48.7 3.6 %collective-permute-start.10 = (f32[2,516]{1,0:T(2,128)S(1)}, f32[2,516]{1,0:T(2,128)S(1)}, u32[]{:S(2)}, u32[]{:S(2)}) collective-permute-start(f32[2,516]{1,0:T(2,128)S(1)} %pad_maximum_fusion.14), channel_id=1, source_target_pairs={{0,4},{1,5},{2,6},{3,7},{4,0},{5,1},{6,2},{7,3},{8,12},{9,13},{10,... | collective-permute-start | bytes 12392 | tf_op jit(solution)/shard_map/ppermute | solution.py:80
  52.3 0.7 collective-permute-start.9
  52.9 1.4 collective-permute-start.8
  54.3 1.0 pad_maximum_fusion.12
  55.9 1.9 collective-permute-done.8
  57.8 0.6 collective-permute-start.11
  59.0 2.5 %collective-permute-done.11 = f32[2,516]{1,0:T(2,128)S(1)} collective-permute-done((f32[2,516]{1,0:T(2,128)S(1)}, f32[2,516]{1,0:T(2,128)S(1)}, u32[]{:S(2)}, u32[]{:S(2)}) %collective-permute-start.11) | collective-permute-done | bytes 4160 | tf_op jit(solution)/shard_map/ppermute | solution.py:81
  61.5 1.0 copy.10.square_ref
  62.5 4.1 %shard_map.95 = (bf16[16,3,128,128]{3,2,1,0:T(8,128)(2,1)}, f32[3,4,512]{2,1,0:T(4,128)}) custom-call(f32[3,516,512]{2,1,0:T(8,128)} %copy-done, f32[2,516,1]{2,1,0:T(8,128)} %copy.10.square_ref, f32[2,1,512]{2,1,0:T(1,128)} %broadcast_in_dim.43.gain_ref, f32[516,128]{1,0:T(8,128)} %get-tuple-element.64.cos_ref, f32[516,128]{1,0:T(8,128)} %get-tuple-element.65.sin_ref), custom_call_target="tpu_custom_call" | custom-call | tf_op jit(solution)/shard_map/pallas_call | solution.py:104
  66.6 7.7 %all-to-all-start = ((bf16[16,3,128,128]{3,2,1,0:T(8,128)(2,1)}), bf16[16,3,128,128]{3,2,1,0:T(8,128)(2,1)S(1)}, u32[]{:S(2)}, u32[]{:S(2)}) async-start(bf16[16,3,128,128]{3,2,1,0:T(8,128)(2,1)} %get-tuple-element.4), calls=%async_computation | async-start | bytes 3145728 | tf_op jit(solution)/shard_map/all_to_all | solution.py:201
  74.9 0.6 iota_compare_fusion.3
  75.6 0.7 iota_compare_fusion.2
  76.3 0.6 fusion.87
  77.6 16.9 %all-to-all-done = bf16[16,3,128,128]{3,2,1,0:T(8,128)(2,1)S(1)} async-done(((bf16[16,3,128,128]{3,2,1,0:T(8,128)(2,1)}), bf16[16,3,128,128]{3,2,1,0:T(8,128)(2,1)S(1)}, u32[]{:S(2)}, u32[]{:S(2)}) %all-to-all-start) | async-done | bytes 1572896 | tf_op jit(solution)/shard_map/all_to_all | solution.py:201
  94.8 1.3 fusion.79
  96.7 1.2 fusion.82
  97.9 0.8 fusion.104
  99.4 3.9 %fusion.1 = (f32[1024]{0:T(1024)S(1)}, f32[1024,2048]{1,0:T(8,128)S(1)}) fusion(s32[1024]{0:T(1024)S(1)} %iota_add_fusion, pred[2048]{0:T(1024)(128)(4,1)S(1)} %iota_compare_fusion.2, bf16[1024,128]{1,0:T(8,128)(2,1)} %bitcast.97, bf16[2048,128]{1,0:T(8,128)(2,1)S(1)} %bitcast.92), kind=kOutput, calls=%fused_computation.4 | convolution fusion | flops 547355648 | bytes 9185280 | tf_op jit(solution)/shard_map/dot_general | solution.py:120
  103.3 3.9 %fusion.101 = f32[1024]{0:T(1024)S(1)} fusion(f32[1024]{0:T(1024)S(1)} %get-tuple-element.56, f32[1024,2048]{1,0:T(8,128)S(1)} %get-tuple-element.57, pred[2048]{0:T(1024)(128)(4,1)S(1)} %iota_compare_fusion.2, s32[1024]{0:T(1024)S(1)} %iota_add_fusion), kind=kLoop, calls=%fused_computation.173 | loop fusion | flops 14679040 | bytes 8402944 | tf_op jit(solution)/shard_map/reduce_sum | solution.py:129
  107.2 3.6 %fusion.55 = bf16[1024,128]{1,0:T(8,128)(2,1)S(1)} fusion(bf16[2048,128]{1,0:T(8,128)(2,1)S(1)} %bitcast.89, f32[1024]{0:T(1024)S(1)} %fusion.101, f32[1024,2048]{1,0:T(8,128)S(1)} %get-tuple-element.57, f32[1024]{0:T(1024)S(1)} %get-tuple-element.56, s32[1024]{0:T(1024)S(1)} %iota_add_fusion, pred[2048]{0:T(1024)(128)(4,1)S(1)} %iota_compare_fusion.2), kind=kOutput, calls=%fused_computation.58 | convolution fusion | flops 551813120 | bytes 9189376 | tf_op jit(solution)/shard_map/dot_general | solution.py:131
  110.8 1.6 fusion.19
  112.4 2.1 %fusion.68 = f32[1024]{0:T(1024)S(1)} fusion(f32[1024]{0:T(1024)S(1)} %get-tuple-element.58, f32[1024,1024]{0,1:T(8,128)S(1)} %get-tuple-element.59, pred[1024]{0:T(1024)(128)(4,1)S(1)} %iota_compare_fusion.3), kind=kLoop, calls=%fused_computation.73 | loop fusion | flops 7339008 | bytes 4203520 | tf_op jit(solution)/shard_map/reduce_sum | solution.py:129
  114.5 1.1 fusion.58
  115.9 0.8 pad_maximum_fusion.2
  116.7 8.0 %all-to-all-start.1 = ((bf16[16,136,128]{2,1,0:T(8,128)(2,1)}), bf16[16,136,128]{2,1,0:T(8,128)(2,1)S(1)}, u32[]{:S(2)}, u32[]{:S(2)}) async-start(bf16[16,136,128]{2,1,0:T(8,128)(2,1)} %pad_maximum_fusion.2), calls=%async_computation.1 | async-start | bytes 1114112 | tf_op jit(solution)/shard_map/all_to_all | solution.py:216
  124.8 3.4 %constant_dynamic-slice_fusion.6 = (bf16[512,512]{1,0:T(8,128)(2,1)S(1)}, bf16[512,512]{1,0:T(8,128)(2,1)S(1)}, bf16[512,512]{1,0:T(8,128)(2,1)S(1)}, bf16[512,5...) fusion(bf16[512,4096]{1,0:T(8,128)(2,1)} %param.11, ...), kind=kLoop, calls=%fused_computation.132 | loop fusion | bytes 7340060 | tf_op jit(solution)/shard_map/dynamic_slice | solution.py:164
  128.2 5.7 %all-to-all-done.1 = bf16[16,136,128]{2,1,0:T(8,128)(2,1)S(1)} async-done(((bf16[16,136,128]{2,1,0:T(8,128)(2,1)}), bf16[16,136,128]{2,1,0:T(8,128)(2,1)S(1)}, u32[]{:S(2)}, u32[]{:S(2)}) %all-to-all-start.1) | async-done | bytes 557088 | tf_op jit(solution)/shard_map/all_to_all | solution.py:216
  134.4 1.5 convolution_convert_fusion
  136.2 3.1 %collective-permute-start.13 = (bf16[516,256]{1,0:T(8,128)(2,1)S(1)}, bf16[516,256]{1,0:T(8,128)(2,1)S(1)}, u32[]{:S(2)}, u32[]{:S(2)}) collective-permute-start(bf16[516,256]{1,0:T(8,128)(2,1)S(1)} %get-tuple-element.41), channel_id=1, source_target_pairs={{0,6},{1,7},{2,0},{3,1},{4,2},{5,3},{6,4},{7,5},{8,14},{9,15},{10,... | collective-permute-start | bytes 792584 | tf_op jit(solution)/shard_map/ppermute | solution.py:61
  139.3 1.0 fusion.110
  140.7 5.8 %collective-permute-done.16 = bf16[516,256]{1,0:T(8,128)(2,1)S(1)} collective-permute-done((bf16[516,256]{1,0:T(8,128)(2,1)S(1)}, bf16[516,256]{1,0:T(8,128)(2,1)S(1)}, u32[]{:S(2)}, u32[]{:S(2)}) %collective-permute-start.16) | collective-permute-done | bytes 264224 | tf_op jit(solution)/shard_map/ppermute | solution.py:61
  146.7 2.8 %collective-permute-start.14 = (bf16[516,512]{1,0:T(8,128)(2,1)S(1)}, bf16[516,512]{1,0:T(8,128)(2,1)S(1)}, u32[]{:S(2)}, u32[]{:S(2)}) collective-permute-start(bf16[516,512]{1,0:T(8,128)(2,1)S(1)} %pad_maximum_fusion.6), channel_id=1, source_target_pairs={{0,6},{1,7},{2,0},{3,1},{4,2},{5,3},{6,4},{7,5},{8,14},{9,15},{10,... | collective-permute-start | bytes 1585160 | tf_op jit(solution)/shard_map/ppermute | solution.py:61
  149.7 1.3 fusion.111
  151.0 6.7 %collective-permute-done.12 = bf16[516,512]{1,0:T(8,128)(2,1)S(1)} collective-permute-done((bf16[516,512]{1,0:T(8,128)(2,1)S(1)}, bf16[516,512]{1,0:T(8,128)(2,1)S(1)}, u32[]{:S(2)}, u32[]{:S(2)}) %collective-permute-start.12) | collective-permute-done | bytes 528416 | tf_op jit(solution)/shard_map/ppermute | solution.py:61
  157.9 2.9 %collective-permute-done.14 = bf16[516,512]{1,0:T(8,128)(2,1)S(1)} collective-permute-done((bf16[516,512]{1,0:T(8,128)(2,1)S(1)}, bf16[516,512]{1,0:T(8,128)(2,1)S(1)}, u32[]{:S(2)}, u32[]{:S(2)}) %collective-permute-start.14) | collective-permute-done | bytes 528416 | tf_op jit(solution)/shard_map/ppermute | solution.py:61
  160.9 2.2 %collective-permute-done.17 = bf16[516,512]{1,0:T(8,128)(2,1)S(1)} collective-permute-done((bf16[516,512]{1,0:T(8,128)(2,1)S(1)}, bf16[516,512]{1,0:T(8,128)(2,1)S(1)}, u32[]{:S(2)}, u32[]{:S(2)}) %collective-permute-start.17) | collective-permute-done | bytes 528416 | tf_op jit(solution)/shard_map/ppermute | solution.py:61
  163.7 1.6 collective-permute-start.19
  166.3 9.9 %collective-permute-done.19 = bf16[516,512]{1,0:T(8,128)(2,1)S(1)} collective-permute-done((bf16[516,512]{1,0:T(8,128)(2,1)S(1)}, bf16[516,512]{1,0:T(8,128)(2,1)S(1)}, u32[]{:S(2)}, u32[]{:S(2)}) %collective-permute-start.19) | collective-permute-done | bytes 528416 | tf_op jit(solution)/shard_map/ppermute | solution.py:61
  176.3 2.9 %collective-permute-done.18 = bf16[516,512]{1,0:T(8,128)(2,1)S(1)} collective-permute-done((bf16[516,512]{1,0:T(8,128)(2,1)S(1)}, bf16[516,512]{1,0:T(8,128)(2,1)S(1)}, u32[]{:S(2)}, u32[]{:S(2)}) %collective-permute-start.18) | collective-permute-done | bytes 528416 | tf_op jit(solution)/shard_map/ppermute | solution.py:61
  180.0 1.6 collective-permute-start.21
  181.6 0.8 collective-permute-start.20
  182.3 2.4 %collective-permute-done.22 = f32[516]{0:T(1024)S(1)} collective-permute-done((f32[516]{0:T(1024)S(1)}, f32[516]{0:T(1024)S(1)}, u32[]{:S(2)}, u32[]{:S(2)}) %collective-permute-start.22) | collective-permute-done | bytes 2096 | tf_op jit(solution)/shard_map/ppermute | solution.py:80
  184.7 1.6 collective-permute-done.20
  186.8 3.2 %collective-permute-done.23 = f32[516]{0:T(1024)S(1)} collective-permute-done((f32[516]{0:T(1024)S(1)}, f32[516]{0:T(1024)S(1)}, u32[]{:S(2)}, u32[]{:S(2)}) %collective-permute-start.23) | collective-permute-done | bytes 2096 | tf_op jit(solution)/shard_map/ppermute | solution.py:81
  190.4 0.8 slice.265
  (102 shorter events, 9.2 us)
Async XLA Ops:
  2.5 19.3 %collective-permute-start.2 = (bf16[516,512]{1,0:T(8,128)(2,1)}, bf16[516,512]{1,0:T(8,128)(2,1)}, u32[]{:S(2)}, u32[]{:S(2)}) collective-permute-start(bf16[516,512]{1,0:T(8,128)(2,1)} %pad_maximum_fusion.3), channel_id=1, source_target_pairs={{0,6},{1,7},{2,0},{3,1},{4,2},{5,3},{6,4},{7,5},{8,14},{9,15},{10,... | collective-permute-start | bytes 1585160 | tf_op jit(solution)/shard_map/ppermute | solution.py:42
  5.5 15.1 %collective-permute-start.1 = (bf16[516,512]{1,0:T(8,128)(2,1)}, bf16[516,512]{1,0:T(8,128)(2,1)}, u32[]{:S(2)}, u32[]{:S(2)}) collective-permute-start(bf16[516,512]{1,0:T(8,128)(2,1)} %pad_maximum_fusion.3), channel_id=1, source_target_pairs={{0,2},{1,3},{2,4},{3,5},{4,6},{5,7},{6,0},{7,1},{8,10},{9,11},{10,... | collective-permute-start | bytes 1585160 | tf_op jit(solution)/shard_map/ppermute | solution.py:42
  5.5 13.9 %collective-permute-start = (bf16[516,512]{1,0:T(8,128)(2,1)}, bf16[516,512]{1,0:T(8,128)(2,1)}, u32[]{:S(2)}, u32[]{:S(2)}) collective-permute-start(bf16[516,512]{1,0:T(8,128)(2,1)} %pad_maximum_fusion.3), channel_id=1, source_target_pairs={{0,1},{1,0},{2,3},{3,2},{4,5},{5,4},{6,7},{7,6},{8,9},{9,8},{10,11... | collective-permute-start | bytes 1585160 | tf_op jit(solution)/shard_map/ppermute | solution.py:42
  7.0 7.4 %copy-start.14 = (s32[4]{0:T(128)S(1)}, s32[4]{0:T(128)}, u32[]{:S(2)}) copy-start(s32[4]{0:T(128)} %param.15) | copy-start | bytes 52
  14.4 13.3 %copy-start.6 = (bf16[3,512,512]{2,1,0:T(8,128)(2,1)S(1)}, bf16[3,512,512]{2,1,0:T(8,128)(2,1)}, u32[]{:S(2)}) copy-start(bf16[3,512,512]{2,1,0:T(8,128)(2,1)} %get-tuple-element.12) | copy-start | bytes 4718596
  20.4 7.4 %copy-start.1 = (bf16[4,128,512]{2,1,0:T(8,128)(2,1)S(1)}, bf16[4,128,512]{2,1,0:T(8,128)(2,1)}, u32[]{:S(2)}) copy-start(bf16[4,128,512]{2,1,0:T(8,128)(2,1)} %param.8) | copy-start | bytes 1572868
  20.4 7.4 %copy-start.4 = (bf16[3,512,512]{2,1,0:T(8,128)(2,1)S(1)}, bf16[3,512,512]{2,1,0:T(8,128)(2,1)}, u32[]{:S(2)}) copy-start(bf16[3,512,512]{2,1,0:T(8,128)(2,1)} %get-tuple-element.10) | copy-start | bytes 4718596
  20.4 7.4 %copy-start.5 = (bf16[3,512,512]{2,1,0:T(8,128)(2,1)S(1)}, bf16[3,512,512]{2,1,0:T(8,128)(2,1)}, u32[]{:S(2)}) copy-start(bf16[3,512,512]{2,1,0:T(8,128)(2,1)} %get-tuple-element.11) | copy-start | bytes 4718596
  20.4 7.4 %copy-start.10 = (bf16[4,512]{1,0:T(4,128)(2,1)S(1)}, bf16[4,512]{1,0:T(4,128)(2,1)}, u32[]{:S(2)}) copy-start(bf16[4,512]{1,0:T(4,128)(2,1)} %param.9) | copy-start | bytes 12292
  23.0 14.5 %collective-permute-start.5 = (bf16[516,512]{1,0:T(8,128)(2,1)S(1)}, bf16[516,512]{1,0:T(8,128)(2,1)S(1)}, u32[]{:S(2)}, u32[]{:S(2)}) collective-permute-start(bf16[516,512]{1,0:T(8,128)(2,1)S(1)} %get-tuple-element.48), channel_id=1, source_target_pairs={{0,2},{1,3},{2,4},{3,5},{4,6},{5,7},{6,0},{7,1},{8,10},{9,11},{10,... | collective-permute-start | bytes 1585160 | tf_op jit(solution)/shard_map/ppermute | solution.py:42
  23.2 12.6 %collective-permute-start.3 = (bf16[516,512]{1,0:T(8,128)(2,1)S(1)}, bf16[516,512]{1,0:T(8,128)(2,1)S(1)}, u32[]{:S(2)}, u32[]{:S(2)}) collective-permute-start(bf16[516,512]{1,0:T(8,128)(2,1)S(1)} %get-tuple-element.50), channel_id=1, source_target_pairs={{0,1},{1,0},{2,3},{3,2},{4,5},{5,4},{6,7},{7,6},{8,9},{9,8},{10,11... | collective-permute-start | bytes 1585160 | tf_op jit(solution)/shard_map/ppermute | solution.py:42
  24.7 12.7 %collective-permute-start.4 = (bf16[516,512]{1,0:T(8,128)(2,1)S(1)}, bf16[516,512]{1,0:T(8,128)(2,1)S(1)}, u32[]{:S(2)}, u32[]{:S(2)}) collective-permute-start(bf16[516,512]{1,0:T(8,128)(2,1)S(1)} %get-tuple-element.49), channel_id=1, source_target_pairs={{0,6},{1,7},{2,0},{3,1},{4,2},{5,3},{6,4},{7,5},{8,14},{9,15},{10,... | collective-permute-start | bytes 1585160 | tf_op jit(solution)/shard_map/ppermute | solution.py:42
  33.2 8.3 %copy-start.3 = (bf16[3,512,512]{2,1,0:T(8,128)(2,1)S(1)}, bf16[3,512,512]{2,1,0:T(8,128)(2,1)}, u32[]{:S(2)}) copy-start(bf16[3,512,512]{2,1,0:T(8,128)(2,1)} %get-tuple-element.14) | copy-start | bytes 4718596
  37.5 8.2 %collective-permute-start.7 = (bf16[516,256]{1,0:T(8,128)(2,1)S(1)}, bf16[516,256]{1,0:T(8,128)(2,1)S(1)}, u32[]{:S(2)}, u32[]{:S(2)}) collective-permute-start(bf16[516,256]{1,0:T(8,128)(2,1)S(1)} %get-tuple-element.44), channel_id=1, source_target_pairs={{0,2},{1,3},{2,4},{3,5},{4,6},{5,7},{6,0},{7,1},{8,10},{9,11},{10,... | collective-permute-start | bytes 792584 | tf_op jit(solution)/shard_map/ppermute | solution.py:42
  39.0 6.7 %collective-permute-start.6 = (bf16[516,256]{1,0:T(8,128)(2,1)S(1)}, bf16[516,256]{1,0:T(8,128)(2,1)S(1)}, u32[]{:S(2)}, u32[]{:S(2)}) collective-permute-start(bf16[516,256]{1,0:T(8,128)(2,1)S(1)} %get-tuple-element.42), channel_id=1, source_target_pairs={{0,6},{1,7},{2,0},{3,1},{4,2},{5,3},{6,4},{7,5},{8,14},{9,15},{10,... | collective-permute-start | bytes 792584 | tf_op jit(solution)/shard_map/ppermute | solution.py:42
  48.4 14.2 %copy-start = (f32[3,516,512]{2,1,0:T(8,128)}, f32[3,516,512]{2,1,0:T(8,128)S(1)}, u32[]{:S(2)}) copy-start(f32[3,516,512]{2,1,0:T(8,128)S(1)} %add_bitcast_fusion.proj_ref) | copy-start | bytes 9510916
  48.4 10.0 %copy-start.12 = (f32[512]{0:T(512)S(1)}, f32[512]{0:T(512)}, u32[]{:S(2)}) copy-start(f32[512]{0:T(512)} %param.13) | copy-start | bytes 6148
  48.4 10.0 %copy-start.13 = (f32[512]{0:T(512)S(1)}, f32[512]{0:T(512)}, u32[]{:S(2)}) copy-start(f32[512]{0:T(512)} %param.12) | copy-start | bytes 6148
  48.7 6.6 %collective-permute-start.10 = (f32[2,516]{1,0:T(2,128)S(1)}, f32[2,516]{1,0:T(2,128)S(1)}, u32[]{:S(2)}, u32[]{:S(2)}) collective-permute-start(f32[2,516]{1,0:T(2,128)S(1)} %pad_maximum_fusion.14), channel_id=1, source_target_pairs={{0,4},{1,5},{2,6},{3,7},{4,0},{5,1},{6,2},{7,3},{8,12},{9,13},{10,... | collective-permute-start | bytes 12392 | tf_op jit(solution)/shard_map/ppermute | solution.py:80
  52.3 3.6 %collective-permute-start.9 = (f32[2,516]{1,0:T(2,128)S(1)}, f32[2,516]{1,0:T(2,128)S(1)}, u32[]{:S(2)}, u32[]{:S(2)}) collective-permute-start(f32[2,516]{1,0:T(2,128)S(1)} %pad_maximum_fusion.14), channel_id=1, source_target_pairs={{0,6},{1,7},{2,0},{3,1},{4,2},{5,3},{6,4},{7,5},{8,14},{9,15},{10,... | collective-permute-start | bytes 12392 | tf_op jit(solution)/shard_map/ppermute | solution.py:80
  52.9 4.8 %collective-permute-start.8 = (f32[2,516]{1,0:T(2,128)S(1)}, f32[2,516]{1,0:T(2,128)S(1)}, u32[]{:S(2)}, u32[]{:S(2)}) collective-permute-start(f32[2,516]{1,0:T(2,128)S(1)} %pad_maximum_fusion.14), channel_id=1, source_target_pairs={{0,2},{1,3},{2,4},{3,5},{4,6},{5,7},{6,0},{7,1},{8,10},{9,11},{10,... | collective-permute-start | bytes 12392 | tf_op jit(solution)/shard_map/ppermute | solution.py:80
  57.8 3.7 %collective-permute-start.11 = (f32[2,516]{1,0:T(2,128)S(1)}, f32[2,516]{1,0:T(2,128)S(1)}, u32[]{:S(2)}, u32[]{:S(2)}) collective-permute-start(f32[2,516]{1,0:T(2,128)S(1)} %add_add_fusion), channel_id=1, source_target_pairs={{0,1},{1,0},{2,3},{3,2},{4,5},{5,4},{6,7},{7,6},{8,9},{9,8},{10,11... | collective-permute-start | bytes 12392 | tf_op jit(solution)/shard_map/ppermute | solution.py:81
  66.6 9.6 %copy-start.9 = (f32[3,4,512]{2,1,0:T(4,128)S(1)}, f32[3,4,512]{2,1,0:T(4,128)}, u32[]{:S(2)}) copy-start(f32[3,4,512]{2,1,0:T(4,128)} %get-tuple-element.5) | copy-start | bytes 73732
  66.6 27.8 %all-to-all-start = ((bf16[16,3,128,128]{3,2,1,0:T(8,128)(2,1)}), bf16[16,3,128,128]{3,2,1,0:T(8,128)(2,1)S(1)}, u32[]{:S(2)}, u32[]{:S(2)}) async-start(bf16[16,3,128,128]{3,2,1,0:T(8,128)(2,1)} %get-tuple-element.4), calls=%async_computation | async-start | bytes 3145728 | tf_op jit(solution)/shard_map/all_to_all | solution.py:201
  116.7 17.1 %all-to-all-start.1 = ((bf16[16,136,128]{2,1,0:T(8,128)(2,1)}), bf16[16,136,128]{2,1,0:T(8,128)(2,1)S(1)}, u32[]{:S(2)}, u32[]{:S(2)}) async-start(bf16[16,136,128]{2,1,0:T(8,128)(2,1)} %pad_maximum_fusion.2), calls=%async_computation.1 | async-start | bytes 1114112 | tf_op jit(solution)/shard_map/all_to_all | solution.py:216
  136.0 10.5 %collective-permute-start.16 = (bf16[516,256]{1,0:T(8,128)(2,1)S(1)}, bf16[516,256]{1,0:T(8,128)(2,1)S(1)}, u32[]{:S(2)}, u32[]{:S(2)}) collective-permute-start(bf16[516,256]{1,0:T(8,128)(2,1)S(1)} %get-tuple-element.40), channel_id=1, source_target_pairs={{0,2},{1,3},{2,4},{3,5},{4,6},{5,7},{6,0},{7,1},{8,10},{9,11},{10,... | collective-permute-start | bytes 792584 | tf_op jit(solution)/shard_map/ppermute | solution.py:61
  136.2 10.3 %collective-permute-start.13 = (bf16[516,256]{1,0:T(8,128)(2,1)S(1)}, bf16[516,256]{1,0:T(8,128)(2,1)S(1)}, u32[]{:S(2)}, u32[]{:S(2)}) collective-permute-start(bf16[516,256]{1,0:T(8,128)(2,1)S(1)} %get-tuple-element.41), channel_id=1, source_target_pairs={{0,6},{1,7},{2,0},{3,1},{4,2},{5,3},{6,4},{7,5},{8,14},{9,15},{10,... | collective-permute-start | bytes 792584 | tf_op jit(solution)/shard_map/ppermute | solution.py:61
  140.4 17.3 %collective-permute-start.12 = (bf16[516,512]{1,0:T(8,128)(2,1)S(1)}, bf16[516,512]{1,0:T(8,128)(2,1)S(1)}, u32[]{:S(2)}, u32[]{:S(2)}) collective-permute-start(bf16[516,512]{1,0:T(8,128)(2,1)S(1)} %pad_maximum_fusion.5), channel_id=1, source_target_pairs={{0,2},{1,3},{2,4},{3,5},{4,6},{5,7},{6,0},{7,1},{8,10},{9,11},{10,... | collective-permute-start | bytes 1585160 | tf_op jit(solution)/shard_map/ppermute | solution.py:61
  146.5 3.2 %copy-start.7 = (bf16[512,512]{1,0:T(8,128)(2,1)S(1)}, bf16[512,512]{1,0:T(8,128)(2,1)}, u32[]{:S(2)}) copy-start(bf16[512,512]{1,0:T(8,128)(2,1)} %get-tuple-element.23) | copy-start | bytes 1572868
  146.5 3.2 %copy-start.8 = (bf16[512,512]{1,0:T(8,128)(2,1)S(1)}, bf16[512,512]{1,0:T(8,128)(2,1)}, u32[]{:S(2)}) copy-start(bf16[512,512]{1,0:T(8,128)(2,1)} %get-tuple-element.24) | copy-start | bytes 1572868
  146.7 14.1 %collective-permute-start.14 = (bf16[516,512]{1,0:T(8,128)(2,1)S(1)}, bf16[516,512]{1,0:T(8,128)(2,1)S(1)}, u32[]{:S(2)}, u32[]{:S(2)}) collective-permute-start(bf16[516,512]{1,0:T(8,128)(2,1)S(1)} %pad_maximum_fusion.6), channel_id=1, source_target_pairs={{0,6},{1,7},{2,0},{3,1},{4,2},{5,3},{6,4},{7,5},{8,14},{9,15},{10,... | collective-permute-start | bytes 1585160 | tf_op jit(solution)/shard_map/ppermute | solution.py:61
  149.6 13.5 %collective-permute-start.17 = (bf16[516,512]{1,0:T(8,128)(2,1)S(1)}, bf16[516,512]{1,0:T(8,128)(2,1)S(1)}, u32[]{:S(2)}, u32[]{:S(2)}) collective-permute-start(bf16[516,512]{1,0:T(8,128)(2,1)S(1)} %pad_maximum_fusion.8), channel_id=1, source_target_pairs={{0,1},{1,0},{2,3},{3,2},{4,5},{5,4},{6,7},{7,6},{8,9},{9,8},{10,11... | collective-permute-start | bytes 1585160 | tf_op jit(solution)/shard_map/ppermute | solution.py:61
  163.7 12.6 %collective-permute-start.19 = (bf16[516,512]{1,0:T(8,128)(2,1)S(1)}, bf16[516,512]{1,0:T(8,128)(2,1)S(1)}, u32[]{:S(2)}, u32[]{:S(2)}) collective-permute-start(bf16[516,512]{1,0:T(8,128)(2,1)S(1)} %pad_maximum_fusion.10), channel_id=1, source_target_pairs={{0,6},{1,7},{2,0},{3,1},{4,2},{5,3},{6,4},{7,5},{8,14},{9,15},{10,... | collective-permute-start | bytes 1585160 | tf_op jit(solution)/shard_map/ppermute | solution.py:61
  165.3 24.7 %copy-start.2 = (bf16[4,128,512]{2,1,0:T(8,128)(2,1)S(1)}, bf16[4,128,512]{2,1,0:T(8,128)(2,1)}, u32[]{:S(2)}) copy-start(bf16[4,128,512]{2,1,0:T(8,128)(2,1)} %param.8) | copy-start | bytes 1572868
  165.3 24.7 %copy-start.11 = (f32[512]{0:T(512)S(1)}, f32[512]{0:T(512)}, u32[]{:S(2)}) copy-start(f32[512]{0:T(512)} %param.14) | copy-start | bytes 6148
  165.4 13.8 %collective-permute-start.18 = (bf16[516,512]{1,0:T(8,128)(2,1)S(1)}, bf16[516,512]{1,0:T(8,128)(2,1)S(1)}, u32[]{:S(2)}, u32[]{:S(2)}) collective-permute-start(bf16[516,512]{1,0:T(8,128)(2,1)S(1)} %pad_maximum_fusion.9), channel_id=1, source_target_pairs={{0,2},{1,3},{2,4},{3,5},{4,6},{5,7},{6,0},{7,1},{8,10},{9,11},{10,... | collective-permute-start | bytes 1585160 | tf_op jit(solution)/shard_map/ppermute | solution.py:61
  166.0 13.2 %collective-permute-start.15 = (bf16[516,512]{1,0:T(8,128)(2,1)S(1)}, bf16[516,512]{1,0:T(8,128)(2,1)S(1)}, u32[]{:S(2)}, u32[]{:S(2)}) collective-permute-start(bf16[516,512]{1,0:T(8,128)(2,1)S(1)} %pad_maximum_fusion.7), channel_id=1, source_target_pairs={{0,1},{1,0},{2,3},{3,2},{4,5},{5,4},{6,7},{7,6},{8,9},{9,8},{10,11... | collective-permute-start | bytes 1585160 | tf_op jit(solution)/shard_map/ppermute | solution.py:61
  179.5 5.2 %collective-permute-start.22 = (f32[516]{0:T(1024)S(1)}, f32[516]{0:T(1024)S(1)}, u32[]{:S(2)}, u32[]{:S(2)}) collective-permute-start(f32[516]{0:T(1024)S(1)} %multiply_reduce_fusion), channel_id=1, source_target_pairs={{0,4},{1,5},{2,6},{3,7},{4,0},{5,1},{6,2},{7,3},{8,12},{9,13},{10,... | collective-permute-start | bytes 6200 | tf_op jit(solution)/shard_map/ppermute | solution.py:80
  180.0 4.7 %collective-permute-start.21 = (f32[516]{0:T(1024)S(1)}, f32[516]{0:T(1024)S(1)}, u32[]{:S(2)}, u32[]{:S(2)}) collective-permute-start(f32[516]{0:T(1024)S(1)} %multiply_reduce_fusion), channel_id=1, source_target_pairs={{0,6},{1,7},{2,0},{3,1},{4,2},{5,3},{6,4},{7,5},{8,14},{9,15},{10,... | collective-permute-start | bytes 6200 | tf_op jit(solution)/shard_map/ppermute | solution.py:80
  181.6 4.8 %collective-permute-start.20 = (f32[516]{0:T(1024)S(1)}, f32[516]{0:T(1024)S(1)}, u32[]{:S(2)}, u32[]{:S(2)}) collective-permute-start(f32[516]{0:T(1024)S(1)} %multiply_reduce_fusion), channel_id=1, source_target_pairs={{0,2},{1,3},{2,4},{3,5},{4,6},{5,7},{6,0},{7,1},{8,10},{9,11},{10,... | collective-permute-start | bytes 6200 | tf_op jit(solution)/shard_map/ppermute | solution.py:80
  186.4 3.6 %collective-permute-start.23 = (f32[516]{0:T(1024)S(1)}, f32[516]{0:T(1024)S(1)}, u32[]{:S(2)}, u32[]{:S(2)}) collective-permute-start(f32[516]{0:T(1024)S(1)} %add_add_fusion.1), channel_id=1, source_target_pairs={{0,1},{1,0},{2,3},{3,2},{4,5},{5,4},{6,7},{7,6},{8,9},{9,8},{10,11... | collective-permute-start | bytes 6200 | tf_op jit(solution)/shard_map/ppermute | solution.py:81

commit v2 on v1

--- a/solution.py
+++ b/solution.py
@@ -113,7 +113,7 @@
 def attend_pair(q_all, k_all, v_all, q_new, k_new, v_new, length):
     count = q_all.shape[0]
     scale = HD ** (-0.5)
-    bounds = (0, count // 2, count)
+    bounds = (0, count // 2, count * 3 // 4, count)
     outs = []
     for begin, stop in zip(bounds[:-1], bounds[1:]):
         scores = (

time: 192 us -> 191 us (level)
  waiting for transfers between devices: 74.6 us -> 71.2 us
  other arithmetic: 17.7 us -> 20.6 us
    all_to_all x1, waiting for transfers between devices: 16.9 us -> 13.4 us  [body(): got = lax.all_to_all(qkv, 'seq', 0, 0, tiled=True)]
    lt x2 -> x3, other arithmetic: 1.3 us -> 3.66 us  [attend_pair(): valid = (key_pos <= query_pos) & (key_pos < length)]
    reduce_sum x2 -> x3, other arithmetic: 6.03 us -> 4.75 us  [attend_pair(): total = jnp.sum(weights, -1, keepdims=True)]
    dot_general x2 -> x3, matrix products: 4.69 us -> 3.5 us  [attend_pair(): jnp.dot(weights.astype(jnp.bfloat16), v_all[:stop], preferred_element_typ...]
    dot_general x2 -> x3, matrix products: 5.53 us -> 4.96 us  [attend_pair(): jnp.dot(q_all[begin:stop], k_all[:stop].T, preferred_element_type=jnp.flo...]
  transfers between devices with their start and end apart: 26 -> 26, of which waited for: 19 -> 19; matrix products, arithmetic and copies ran while one was open for 15% -> 17% of each run, Pallas kernels for 0% -> 0%
where the time goes in v2:
time: 191 us
  waiting for transfers between devices  71.2 us (37%)
  starting transfers between devices  47.4 us (25%)
  matrix products  23.6 us (12%)
  other arithmetic  20.6 us (11%)
  local copies, waits for them, and re-layouts  20.3 us (11%)
  Pallas kernels  4.11 us (2%)
  between operations  3.36 us (2%)
    ppermute x8, waiting for transfers between devices, tp_reduce_scatter(): lax.ppermute(value.astype(jnp.bfloat16), 'tp', perm).astype(jnp.float32)  30.7 us
    all_to_all x1, waiting for transfers between devices, body(): got = lax.all_to_all(qkv, 'seq', 0, 0, tiled=True)  13.4 us
    ppermute x8, starting transfers between devices, tp_gather(): send = lambda value, perm: lax.ppermute(value, 'tp', perm)  13.3 us
    dot_general x3, matrix products, body(): jnp.einsum('tn,cnf->ctf', jnp.concatenate(blocks, 1), jnp.concatenate(w_b...  11 us
    dynamic_slice x2, local copies, waits for them, and re-layouts, in_relative_order(): lax.dynamic_slice_in_dim(weight, order[name] * width_local, width_local,...  10.8 us
    ppermute x8, waiting for transfers between devices, tp_gather(): send = lambda value, perm: lax.ppermute(value, 'tp', perm)  9.44 us
    ppermute x8, starting transfers between devices, tp_reduce_scatter(): lax.ppermute(value.astype(jnp.bfloat16), 'tp', perm).astype(jnp.float32)  8.82 us
    ppermute x6, starting transfers between devices, tp_sum(): lax.ppermute(values, 'tp', [(i, (i + shift) % size) for i in range(size)])  8.39 us
  transfers between devices with their start and end apart: 26, of which 19 were waited for; matrix products, arithmetic and copies ran while one was open for 17% of the time, Pallas kernels for 0%

profile of v2, /device:TPU:32, one launch (start us, length us, event | category | flops | bytes accessed | tf_op | source)
XLA Modules:
  0.0 190.7 jit_solution(15925985398091348708)
XLA Ops:
  0.6 1.9 pad_maximum_fusion.3
  2.5 3.0 %collective-permute-start.2 = (bf16[516,512]{1,0:T(8,128)(2,1)}, bf16[516,512]{1,0:T(8,128)(2,1)}, u32[]{:S(2)}, u32[]{:S(2)}) collective-permute-start(bf16[516,512]{1,0:T(8,128)(2,1)} %pad_maximum_fusion.3), channel_id=1, source_target_pairs={{0,6},{1,7},{2,0},{3,1},{4,2},{5,3},{6,4},{7,5},{8,14},{9,15},{10,... | collective-permute-start | bytes 1585160 | tf_op jit(solution)/shard_map/ppermute | solution.py:42
  5.5 1.5 collective-permute-start
  7.0 7.4 %constant_dynamic-slice_fusion.12 = (bf16[3,512,512]{2,1,0:T(8,128)(2,1)S(1)}, bf16[3,512,512]{2,1,0:T(8,128)(2,1)S(1)}, bf16[3,512,512]{2,1,0:T(8,128)(2,1)}, b...) fusion(bf16[3,4096,512]{2,1,0:T(8,128)(2,1)} %param.10, ...), kind=kLoop, calls=%fused_computation.150 | loop fusion | bytes 22020124 | tf_op jit(solution)/shard_map/dynamic_slice | solution.py:164
  14.5 1.0 fusion.91
  15.5 3.9 %collective-permute-done = bf16[516,512]{1,0:T(8,128)(2,1)} collective-permute-done((bf16[516,512]{1,0:T(8,128)(2,1)}, bf16[516,512]{1,0:T(8,128)(2,1)}, u32[]{:S(2)}, u32[]{:S(2)}) %collective-permute-start) | collective-permute-done | bytes 528416 | tf_op jit(solution)/shard_map/ppermute | solution.py:42
  19.4 1.0 slice.254
  20.6 1.2 fusion.125
  21.9 1.0 slice.251
  23.2 1.5 collective-permute-start.3
  24.7 3.1 %collective-permute-start.4 = (bf16[516,512]{1,0:T(8,128)(2,1)S(1)}, bf16[516,512]{1,0:T(8,128)(2,1)S(1)}, u32[]{:S(2)}, u32[]{:S(2)}) collective-permute-start(bf16[516,512]{1,0:T(8,128)(2,1)S(1)} %get-tuple-element.52), channel_id=1, source_target_pairs={{0,6},{1,7},{2,0},{3,1},{4,2},{5,3},{6,4},{7,5},{8,14},{9,15},{10,... | collective-permute-start | bytes 1585160 | tf_op jit(solution)/shard_map/ppermute | solution.py:42
  27.8 5.4 %fusion = f32[3,512,516]{1,2,0:T(8,128)S(1)} fusion(bf16[3,512,512]{2,1,0:T(8,128)(2,1)S(1)} %copy-done.4, bf16[3,512,512]{2,1,0:T(8,128)(2,1)S(1)} %copy-done.5, bf16[3,512,512]{2,1,0:T(8,128)(2,1)S(1)} %copy-done.6, bf16[3,512,512]{2,1,0:T(8,128)(2,1)} %get-tuple-element.13, bf16[516,512]{1,0:T(8,128)(2,1)} %collective-permute-done.2, ...), kind=kOutput, calls=%fused_computation | convolution fusion | flops 3282124800 | bytes 11575296 | tf_op jit(solution)/shard_map/tn,cnf->ctf/dot_general | solution.py:172
  33.3 2.5 %collective-permute-done.3 = bf16[516,512]{1,0:T(8,128)(2,1)S(1)} collective-permute-done((bf16[516,512]{1,0:T(8,128)(2,1)S(1)}, bf16[516,512]{1,0:T(8,128)(2,1)S(1)}, u32[]{:S(2)}, u32[]{:S(2)}) %collective-permute-start.3) | collective-permute-done | bytes 528416 | tf_op jit(solution)/shard_map/ppermute | solution.py:42
  35.8 1.6 collective-permute-done.4
  37.5 1.5 collective-permute-start.7
  39.0 2.6 %collective-permute-start.6 = (bf16[516,256]{1,0:T(8,128)(2,1)S(1)}, bf16[516,256]{1,0:T(8,128)(2,1)S(1)}, u32[]{:S(2)}, u32[]{:S(2)}) collective-permute-start(bf16[516,256]{1,0:T(8,128)(2,1)S(1)} %get-tuple-element.45), channel_id=1, source_target_pairs={{0,6},{1,7},{2,0},{3,1},{4,2},{5,3},{6,4},{7,5},{8,14},{9,15},{10,... | collective-permute-start | bytes 792584 | tf_op jit(solution)/shard_map/ppermute | solution.py:42
  41.6 2.8 %fusion.8 = f32[3,512,516]{1,2,0:T(8,128)S(1)} fusion(bf16[3,512,512]{2,1,0:T(8,128)(2,1)S(1)} %copy-done.3, bf16[3,512,512]{2,1,0:T(8,128)(2,1)S(1)} %get-tuple-element.9, bf16[3,512,512]{2,1,0:T(8,128)(2,1)S(1)} %get-tuple-element.8, bf16[516,1536]{1,0:T(8,128)(2,1)S(1)} %slice_dynamic-update-slice_fusion), kind=kOutput, calls=%fused_computation.8 | convolution fusion | flops 2448949248 | bytes 9474048 | tf_op jit(solution)/shard_map/tn,cnf->ctf/dot_general | solution.py:172
  44.4 1.2 collective-permute-done.7
  45.7 2.7 %add_bitcast_fusion.proj_ref = f32[3,516,512]{2,1,0:T(8,128)S(1)} fusion(f32[3,512,516]{1,2,0:T(8,128)S(1)} %fusion, f32[3,512,516]{1,2,0:T(8,128)S(1)} %fusion.8, bf16[3,4096,512]{2,1,0:T(8,128)(2,1)} %param.10, s32[]{:T(128)S(6)} %select_n.121, bf16[516,256]{1,0:T(8,128)(2,1)S(1)} %collective-permute-done.7, bf16[516,256]{1,0:T(8,128)(2,1)S(1)} %collective-permute-done.6), kind=kOutput, calls=%fused_computation.25 | convolution fusion | flops 814239744 | bytes 11612164 | tf_op jit(solution)/shard_map/tn,cnf->ctf/dot_general | solution.py:172
  48.7 3.6 %collective-permute-start.10 = (f32[2,516]{1,0:T(2,128)S(1)}, f32[2,516]{1,0:T(2,128)S(1)}, u32[]{:S(2)}, u32[]{:S(2)}) collective-permute-start(f32[2,516]{1,0:T(2,128)S(1)} %pad_maximum_fusion.14), channel_id=1, source_target_pairs={{0,4},{1,5},{2,6},{3,7},{4,0},{5,1},{6,2},{7,3},{8,12},{9,13},{10,... | collective-permute-start | bytes 12392 | tf_op jit(solution)/shard_map/ppermute | solution.py:80
  52.9 1.4 collective-permute-start.8
  54.3 1.0 pad_maximum_fusion.12
  55.9 1.9 collective-permute-done.8
  59.0 2.5 %collective-permute-done.11 = f32[2,516]{1,0:T(2,128)S(1)} collective-permute-done((f32[2,516]{1,0:T(2,128)S(1)}, f32[2,516]{1,0:T(2,128)S(1)}, u32[]{:S(2)}, u32[]{:S(2)}) %collective-permute-start.11) | collective-permute-done | bytes 4160 | tf_op jit(solution)/shard_map/ppermute | solution.py:81
  61.5 1.1 copy.10.square_ref
  62.6 4.1 %shard_map.95 = (bf16[16,3,128,128]{3,2,1,0:T(8,128)(2,1)}, f32[3,4,512]{2,1,0:T(4,128)}) custom-call(f32[3,516,512]{2,1,0:T(8,128)} %copy-done, f32[2,516,1]{2,1,0:T(8,128)} %copy.10.square_ref, f32[2,1,512]{2,1,0:T(1,128)} %broadcast_in_dim.54.gain_ref, f32[516,128]{1,0:T(8,128)} %get-tuple-element.69.cos_ref, f32[516,128]{1,0:T(8,128)} %get-tuple-element.70.sin_ref), custom_call_target="tpu_custom_call" | custom-call | tf_op jit(solution)/shard_map/pallas_call | solution.py:104
  66.7 7.7 %all-to-all-start = ((bf16[16,3,128,128]{3,2,1,0:T(8,128)(2,1)}), bf16[16,3,128,128]{3,2,1,0:T(8,128)(2,1)S(1)}, u32[]{:S(2)}, u32[]{:S(2)}) async-start(bf16[16,3,128,128]{3,2,1,0:T(8,128)(2,1)} %get-tuple-element.4), calls=%async_computation | async-start | bytes 3145728 | tf_op jit(solution)/shard_map/all_to_all | solution.py:201
  75.0 1.2 iota_compare_fusion.5
  76.2 1.2 iota_compare_fusion.3
  78.0 1.2 iota_compare_fusion.4
  81.1 13.4 %all-to-all-done = bf16[16,3,128,128]{3,2,1,0:T(8,128)(2,1)S(1)} async-done(((bf16[16,3,128,128]{3,2,1,0:T(8,128)(2,1)}), bf16[16,3,128,128]{3,2,1,0:T(8,128)(2,1)S(1)}, u32[]{:S(2)}, u32[]{:S(2)}) %all-to-all-start) | async-done | bytes 1572896 | tf_op jit(solution)/shard_map/all_to_all | solution.py:201
  94.8 1.3 fusion.92
  96.8 1.9 %fusion.95 = (f32[]{:T(128)}, bf16[2048]{0:T(1024)(128)(2,1)}) fusion(f32[2048]{0:T(1024)S(1)} %bitcast.110, f32[]{:T(128)S(6)} %max.3, s32[]{:T(128)} %bitcast.1), kind=kLoop, calls=%fused_computation.155 | loop fusion | flops 14335 | bytes 12300 | tf_op jit(solution)/shard_map/reduce_sum | solution.py:142
  99.4 0.9 fusion.118
  101.1 2.3 %fusion.126 = (f32[512]{0:T(512)S(1)}, f32[512,2048]{1,0:T(8,128)S(1)}) fusion(bf16[512,128]{1,0:T(8,128)(2,1)} %bitcast.108, bf16[2048,128]{1,0:T(8,128)(2,1)S(1)} %bitcast.100, pred[2048]{0:T(1024)(128)(4,1)} %iota_compare_fusion.3, s32[512]{0:T(512)} %iota_add_fusion), kind=kOutput, calls=%fused_computation.197 | convolution fusion | flops 273677824 | bytes 4855808 | tf_op jit(solution)/shard_map/dot_general | solution.py:120
  103.4 1.5 fusion.19
  104.9 1.3 fusion.78
  106.3 1.1 fusion.127
  107.3 1.2 fusion.21
  108.5 1.0 fusion.72
  109.6 1.6 fusion.17
  111.2 2.1 %fusion.81 = f32[1024]{0:T(1024)S(1)} fusion(f32[1024]{0:T(1024)S(1)} %get-tuple-element.63, f32[1024,1024]{0,1:T(8,128)S(1)} %get-tuple-element.64, pred[1024]{0:T(1024)(128)(4,1)S(1)} %copy-done.22), kind=kLoop, calls=%fused_computation.83 | loop fusion | flops 7339008 | bytes 4203520 | tf_op jit(solution)/shard_map/reduce_sum | solution.py:129
  113.3 1.1 fusion.59
  114.7 0.8 pad_maximum_fusion.2
  115.5 8.0 %all-to-all-start.1 = ((bf16[16,136,128]{2,1,0:T(8,128)(2,1)}), bf16[16,136,128]{2,1,0:T(8,128)(2,1)S(1)}, u32[]{:S(2)}, u32[]{:S(2)}) async-start(bf16[16,136,128]{2,1,0:T(8,128)(2,1)} %pad_maximum_fusion.2), calls=%async_computation.1 | async-start | bytes 1114112 | tf_op jit(solution)/shard_map/all_to_all | solution.py:216
  123.6 3.4 %constant_dynamic-slice_fusion.6 = (bf16[512,512]{1,0:T(8,128)(2,1)S(1)}, bf16[512,512]{1,0:T(8,128)(2,1)S(1)}, bf16[512,512]{1,0:T(8,128)(2,1)S(1)}, bf16[512,5...) fusion(bf16[512,4096]{1,0:T(8,128)(2,1)} %param.11, ...), kind=kLoop, calls=%fused_computation.143 | loop fusion | bytes 7340060 | tf_op jit(solution)/shard_map/dynamic_slice | solution.py:164
  127.0 5.7 %all-to-all-done.1 = bf16[16,136,128]{2,1,0:T(8,128)(2,1)S(1)} async-done(((bf16[16,136,128]{2,1,0:T(8,128)(2,1)}), bf16[16,136,128]{2,1,0:T(8,128)(2,1)S(1)}, u32[]{:S(2)}, u32[]{:S(2)}) %all-to-all-start.1) | async-done | bytes 557088 | tf_op jit(solution)/shard_map/all_to_all | solution.py:216
  133.2 1.5 convolution_convert_fusion
  135.0 3.1 %collective-permute-start.13 = (bf16[516,256]{1,0:T(8,128)(2,1)S(1)}, bf16[516,256]{1,0:T(8,128)(2,1)S(1)}, u32[]{:S(2)}, u32[]{:S(2)}) collective-permute-start(bf16[516,256]{1,0:T(8,128)(2,1)S(1)} %get-tuple-element.44), channel_id=1, source_target_pairs={{0,6},{1,7},{2,0},{3,1},{4,2},{5,3},{6,4},{7,5},{8,14},{9,15},{10,... | collective-permute-start | bytes 792584 | tf_op jit(solution)/shard_map/ppermute | solution.py:61
  138.1 1.0 fusion.128
  139.3 6.0 %collective-permute-done.16 = bf16[516,256]{1,0:T(8,128)(2,1)S(1)} collective-permute-done((bf16[516,256]{1,0:T(8,128)(2,1)S(1)}, bf16[516,256]{1,0:T(8,128)(2,1)S(1)}, u32[]{:S(2)}, u32[]{:S(2)}) %collective-permute-start.16) | collective-permute-done | bytes 264224 | tf_op jit(solution)/shard_map/ppermute | solution.py:61
  145.5 2.8 %collective-permute-start.14 = (bf16[516,512]{1,0:T(8,128)(2,1)S(1)}, bf16[516,512]{1,0:T(8,128)(2,1)S(1)}, u32[]{:S(2)}, u32[]{:S(2)}) collective-permute-start(bf16[516,512]{1,0:T(8,128)(2,1)S(1)} %pad_maximum_fusion.6), channel_id=1, source_target_pairs={{0,6},{1,7},{2,0},{3,1},{4,2},{5,3},{6,4},{7,5},{8,14},{9,15},{10,... | collective-permute-start | bytes 1585160 | tf_op jit(solution)/shard_map/ppermute | solution.py:61
  148.5 1.3 fusion.129
  149.8 6.7 %collective-permute-done.12 = bf16[516,512]{1,0:T(8,128)(2,1)S(1)} collective-permute-done((bf16[516,512]{1,0:T(8,128)(2,1)S(1)}, bf16[516,512]{1,0:T(8,128)(2,1)S(1)}, u32[]{:S(2)}, u32[]{:S(2)}) %collective-permute-start.12) | collective-permute-done | bytes 528416 | tf_op jit(solution)/shard_map/ppermute | solution.py:61
  156.6 2.9 %collective-permute-done.14 = bf16[516,512]{1,0:T(8,128)(2,1)S(1)} collective-permute-done((bf16[516,512]{1,0:T(8,128)(2,1)S(1)}, bf16[516,512]{1,0:T(8,128)(2,1)S(1)}, u32[]{:S(2)}, u32[]{:S(2)}) %collective-permute-start.14) | collective-permute-done | bytes 528416 | tf_op jit(solution)/shard_map/ppermute | solution.py:61
  159.7 2.2 %collective-permute-done.17 = bf16[516,512]{1,0:T(8,128)(2,1)S(1)} collective-permute-done((bf16[516,512]{1,0:T(8,128)(2,1)S(1)}, bf16[516,512]{1,0:T(8,128)(2,1)S(1)}, u32[]{:S(2)}, u32[]{:S(2)}) %collective-permute-start.17) | collective-permute-done | bytes 528416 | tf_op jit(solution)/shard_map/ppermute | solution.py:61
  162.5 1.6 collective-permute-start.19
  165.1 9.9 %collective-permute-done.19 = bf16[516,512]{1,0:T(8,128)(2,1)S(1)} collective-permute-done((bf16[516,512]{1,0:T(8,128)(2,1)S(1)}, bf16[516,512]{1,0:T(8,128)(2,1)S(1)}, u32[]{:S(2)}, u32[]{:S(2)}) %collective-permute-start.19) | collective-permute-done | bytes 528416 | tf_op jit(solution)/shard_map/ppermute | solution.py:61
  175.1 2.9 %collective-permute-done.18 = bf16[516,512]{1,0:T(8,128)(2,1)S(1)} collective-permute-done((bf16[516,512]{1,0:T(8,128)(2,1)S(1)}, bf16[516,512]{1,0:T(8,128)(2,1)S(1)}, u32[]{:S(2)}, u32[]{:S(2)}) %collective-permute-start.18) | collective-permute-done | bytes 528416 | tf_op jit(solution)/shard_map/ppermute | solution.py:61
  178.8 1.6 collective-permute-start.21
  181.1 2.4 %collective-permute-done.22 = f32[516]{0:T(1024)S(1)} collective-permute-done((f32[516]{0:T(1024)S(1)}, f32[516]{0:T(1024)S(1)}, u32[]{:S(2)}, u32[]{:S(2)}) %collective-permute-start.22) | collective-permute-done | bytes 2096 | tf_op jit(solution)/shard_map/ppermute | solution.py:80
  183.5 1.6 collective-permute-done.20
  185.6 3.2 %collective-permute-done.23 = f32[516]{0:T(1024)S(1)} collective-permute-done((f32[516]{0:T(1024)S(1)}, f32[516]{0:T(1024)S(1)}, u32[]{:S(2)}, u32[]{:S(2)}) %collective-permute-start.23) | collective-permute-done | bytes 2096 | tf_op jit(solution)/shard_map/ppermute | solution.py:81
  189.2 0.8 slice.295
  (127 shorter events, 13.5 us)
Async XLA Ops:
  2.5 19.3 %collective-permute-start.2 = (bf16[516,512]{1,0:T(8,128)(2,1)}, bf16[516,512]{1,0:T(8,128)(2,1)}, u32[]{:S(2)}, u32[]{:S(2)}) collective-permute-start(bf16[516,512]{1,0:T(8,128)(2,1)} %pad_maximum_fusion.3), channel_id=1, source_target_pairs={{0,6},{1,7},{2,0},{3,1},{4,2},{5,3},{6,4},{7,5},{8,14},{9,15},{10,... | collective-permute-start | bytes 1585160 | tf_op jit(solution)/shard_map/ppermute | solution.py:42
  5.5 15.1 %collective-permute-start.1 = (bf16[516,512]{1,0:T(8,128)(2,1)}, bf16[516,512]{1,0:T(8,128)(2,1)}, u32[]{:S(2)}, u32[]{:S(2)}) collective-permute-start(bf16[516,512]{1,0:T(8,128)(2,1)} %pad_maximum_fusion.3), channel_id=1, source_target_pairs={{0,2},{1,3},{2,4},{3,5},{4,6},{5,7},{6,0},{7,1},{8,10},{9,11},{10,... | collective-permute-start | bytes 1585160 | tf_op jit(solution)/shard_map/ppermute | solution.py:42
  5.5 13.9 %collective-permute-start = (bf16[516,512]{1,0:T(8,128)(2,1)}, bf16[516,512]{1,0:T(8,128)(2,1)}, u32[]{:S(2)}, u32[]{:S(2)}) collective-permute-start(bf16[516,512]{1,0:T(8,128)(2,1)} %pad_maximum_fusion.3), channel_id=1, source_target_pairs={{0,1},{1,0},{2,3},{3,2},{4,5},{5,4},{6,7},{7,6},{8,9},{9,8},{10,11... | collective-permute-start | bytes 1585160 | tf_op jit(solution)/shard_map/ppermute | solution.py:42
  7.0 7.4 %copy-start.23 = (s32[4]{0:T(128)S(1)}, s32[4]{0:T(128)}, u32[]{:S(2)}) copy-start(s32[4]{0:T(128)} %param.15) | copy-start | bytes 52
  14.5 13.3 %copy-start.6 = (bf16[3,512,512]{2,1,0:T(8,128)(2,1)S(1)}, bf16[3,512,512]{2,1,0:T(8,128)(2,1)}, u32[]{:S(2)}) copy-start(bf16[3,512,512]{2,1,0:T(8,128)(2,1)} %get-tuple-element.12) | copy-start | bytes 4718596
  20.4 7.4 %copy-start.1 = (bf16[4,128,512]{2,1,0:T(8,128)(2,1)S(1)}, bf16[4,128,512]{2,1,0:T(8,128)(2,1)}, u32[]{:S(2)}) copy-start(bf16[4,128,512]{2,1,0:T(8,128)(2,1)} %param.8) | copy-start | bytes 1572868
  20.4 7.4 %copy-start.4 = (bf16[3,512,512]{2,1,0:T(8,128)(2,1)S(1)}, bf16[3,512,512]{2,1,0:T(8,128)(2,1)}, u32[]{:S(2)}) copy-start(bf16[3,512,512]{2,1,0:T(8,128)(2,1)} %get-tuple-element.10) | copy-start | bytes 4718596
  20.4 7.4 %copy-start.5 = (bf16[3,512,512]{2,1,0:T(8,128)(2,1)S(1)}, bf16[3,512,512]{2,1,0:T(8,128)(2,1)}, u32[]{:S(2)}) copy-start(bf16[3,512,512]{2,1,0:T(8,128)(2,1)} %get-tuple-element.11) | copy-start | bytes 4718596
  20.4 7.4 %copy-start.13 = (bf16[4,512]{1,0:T(4,128)(2,1)S(1)}, bf16[4,512]{1,0:T(4,128)(2,1)}, u32[]{:S(2)}) copy-start(bf16[4,512]{1,0:T(4,128)(2,1)} %param.9) | copy-start | bytes 12292
  23.0 14.5 %collective-permute-start.5 = (bf16[516,512]{1,0:T(8,128)(2,1)S(1)}, bf16[516,512]{1,0:T(8,128)(2,1)S(1)}, u32[]{:S(2)}, u32[]{:S(2)}) collective-permute-start(bf16[516,512]{1,0:T(8,128)(2,1)S(1)} %get-tuple-element.51), channel_id=1, source_target_pairs={{0,2},{1,3},{2,4},{3,5},{4,6},{5,7},{6,0},{7,1},{8,10},{9,11},{10,... | collective-permute-start | bytes 1585160 | tf_op jit(solution)/shard_map/ppermute | solution.py:42
  23.2 12.6 %collective-permute-start.3 = (bf16[516,512]{1,0:T(8,128)(2,1)S(1)}, bf16[516,512]{1,0:T(8,128)(2,1)S(1)}, u32[]{:S(2)}, u32[]{:S(2)}) collective-permute-start(bf16[516,512]{1,0:T(8,128)(2,1)S(1)} %get-tuple-element.53), channel_id=1, source_target_pairs={{0,1},{1,0},{2,3},{3,2},{4,5},{5,4},{6,7},{7,6},{8,9},{9,8},{10,11... | collective-permute-start | bytes 1585160 | tf_op jit(solution)/shard_map/ppermute | solution.py:42
  24.7 12.7 %collective-permute-start.4 = (bf16[516,512]{1,0:T(8,128)(2,1)S(1)}, bf16[516,512]{1,0:T(8,128)(2,1)S(1)}, u32[]{:S(2)}, u32[]{:S(2)}) collective-permute-start(bf16[516,512]{1,0:T(8,128)(2,1)S(1)} %get-tuple-element.52), channel_id=1, source_target_pairs={{0,6},{1,7},{2,0},{3,1},{4,2},{5,3},{6,4},{7,5},{8,14},{9,15},{10,... | collective-permute-start | bytes 1585160 | tf_op jit(solution)/shard_map/ppermute | solution.py:42
  33.3 8.3 %copy-start.3 = (bf16[3,512,512]{2,1,0:T(8,128)(2,1)S(1)}, bf16[3,512,512]{2,1,0:T(8,128)(2,1)}, u32[]{:S(2)}) copy-start(bf16[3,512,512]{2,1,0:T(8,128)(2,1)} %get-tuple-element.14) | copy-start | bytes 4718596
  37.5 8.2 %collective-permute-start.7 = (bf16[516,256]{1,0:T(8,128)(2,1)S(1)}, bf16[516,256]{1,0:T(8,128)(2,1)S(1)}, u32[]{:S(2)}, u32[]{:S(2)}) collective-permute-start(bf16[516,256]{1,0:T(8,128)(2,1)S(1)} %get-tuple-element.47), channel_id=1, source_target_pairs={{0,2},{1,3},{2,4},{3,5},{4,6},{5,7},{6,0},{7,1},{8,10},{9,11},{10,... | collective-permute-start | bytes 792584 | tf_op jit(solution)/shard_map/ppermute | solution.py:42
  39.0 6.7 %collective-permute-start.6 = (bf16[516,256]{1,0:T(8,128)(2,1)S(1)}, bf16[516,256]{1,0:T(8,128)(2,1)S(1)}, u32[]{:S(2)}, u32[]{:S(2)}) collective-permute-start(bf16[516,256]{1,0:T(8,128)(2,1)S(1)} %get-tuple-element.45), channel_id=1, source_target_pairs={{0,6},{1,7},{2,0},{3,1},{4,2},{5,3},{6,4},{7,5},{8,14},{9,15},{10,... | collective-permute-start | bytes 792584 | tf_op jit(solution)/shard_map/ppermute | solution.py:42
  48.4 14.2 %copy-start = (f32[3,516,512]{2,1,0:T(8,128)}, f32[3,516,512]{2,1,0:T(8,128)S(1)}, u32[]{:S(2)}) copy-start(f32[3,516,512]{2,1,0:T(8,128)S(1)} %add_bitcast_fusion.proj_ref) | copy-start | bytes 9510916
  48.4 10.0 %copy-start.20 = (f32[512]{0:T(512)S(1)}, f32[512]{0:T(512)}, u32[]{:S(2)}) copy-start(f32[512]{0:T(512)} %param.13) | copy-start | bytes 6148
  48.4 10.0 %copy-start.21 = (f32[512]{0:T(512)S(1)}, f32[512]{0:T(512)}, u32[]{:S(2)}) copy-start(f32[512]{0:T(512)} %param.12) | copy-start | bytes 6148
  48.7 6.6 %collective-permute-start.10 = (f32[2,516]{1,0:T(2,128)S(1)}, f32[2,516]{1,0:T(2,128)S(1)}, u32[]{:S(2)}, u32[]{:S(2)}) collective-permute-start(f32[2,516]{1,0:T(2,128)S(1)} %pad_maximum_fusion.14), channel_id=1, source_target_pairs={{0,4},{1,5},{2,6},{3,7},{4,0},{5,1},{6,2},{7,3},{8,12},{9,13},{10,... | collective-permute-start | bytes 12392 | tf_op jit(solution)/shard_map/ppermute | solution.py:80
  52.3 3.6 %collective-permute-start.9 = (f32[2,516]{1,0:T(2,128)S(1)}, f32[2,516]{1,0:T(2,128)S(1)}, u32[]{:S(2)}, u32[]{:S(2)}) collective-permute-start(f32[2,516]{1,0:T(2,128)S(1)} %pad_maximum_fusion.14), channel_id=1, source_target_pairs={{0,6},{1,7},{2,0},{3,1},{4,2},{5,3},{6,4},{7,5},{8,14},{9,15},{10,... | collective-permute-start | bytes 12392 | tf_op jit(solution)/shard_map/ppermute | solution.py:80
  52.9 4.8 %collective-permute-start.8 = (f32[2,516]{1,0:T(2,128)S(1)}, f32[2,516]{1,0:T(2,128)S(1)}, u32[]{:S(2)}, u32[]{:S(2)}) collective-permute-start(f32[2,516]{1,0:T(2,128)S(1)} %pad_maximum_fusion.14), channel_id=1, source_target_pairs={{0,2},{1,3},{2,4},{3,5},{4,6},{5,7},{6,0},{7,1},{8,10},{9,11},{10,... | collective-permute-start | bytes 12392 | tf_op jit(solution)/shard_map/ppermute | solution.py:80
  57.8 3.7 %collective-permute-start.11 = (f32[2,516]{1,0:T(2,128)S(1)}, f32[2,516]{1,0:T(2,128)S(1)}, u32[]{:S(2)}, u32[]{:S(2)}) collective-permute-start(f32[2,516]{1,0:T(2,128)S(1)} %add_add_fusion), channel_id=1, source_target_pairs={{0,1},{1,0},{2,3},{3,2},{4,5},{5,4},{6,7},{7,6},{8,9},{9,8},{10,11... | collective-permute-start | bytes 12392 | tf_op jit(solution)/shard_map/ppermute | solution.py:81
  66.7 13.2 %copy-start.12 = (f32[3,4,512]{2,1,0:T(4,128)S(1)}, f32[3,4,512]{2,1,0:T(4,128)}, u32[]{:S(2)}) copy-start(f32[3,4,512]{2,1,0:T(4,128)} %get-tuple-element.5) | copy-start | bytes 73732
  66.7 27.8 %all-to-all-start = ((bf16[16,3,128,128]{3,2,1,0:T(8,128)(2,1)}), bf16[16,3,128,128]{3,2,1,0:T(8,128)(2,1)S(1)}, u32[]{:S(2)}, u32[]{:S(2)}) async-start(bf16[16,3,128,128]{3,2,1,0:T(8,128)(2,1)} %get-tuple-element.4), calls=%async_computation | async-start | bytes 3145728 | tf_op jit(solution)/shard_map/all_to_all | solution.py:201
  98.7 1.6 copy-start.14
  101.1 2.3 %copy-start.16 = (pred[2048]{0:T(1024)(128)(4,1)S(1)}, pred[2048]{0:T(1024)(128)(4,1)}, u32[]{:S(2)}) copy-start(pred[2048]{0:T(1024)(128)(4,1)} %iota_compare_fusion.3) | copy-start | bytes 6148
  101.1 2.3 %copy-start.18 = (s32[512]{0:T(512)S(1)}, s32[512]{0:T(512)}, u32[]{:S(2)}) copy-start(s32[512]{0:T(512)} %iota_add_fusion) | copy-start | bytes 6148
  104.9 1.4 copy-start.15
  104.9 1.4 copy-start.17
  108.5 1.1 copy-start.10
  108.5 1.1 copy-start.11
  108.5 1.1 copy-start.22
  111.2 2.1 %copy-start.9 = (bf16[1,8,128,128]{3,2,0,1:T(8,128)(2,1)S(1)}, bf16[1,8,128,128]{3,2,0,1:T(8,128)(2,1)}, u32[]{:S(2)}) copy-start(bf16[1,8,128,128]{3,2,0,1:T(8,128)(2,1)} %get-tuple-element.35) | copy-start | bytes 786436
  115.5 17.1 %all-to-all-start.1 = ((bf16[16,136,128]{2,1,0:T(8,128)(2,1)}), bf16[16,136,128]{2,1,0:T(8,128)(2,1)S(1)}, u32[]{:S(2)}, u32[]{:S(2)}) async-start(bf16[16,136,128]{2,1,0:T(8,128)(2,1)} %pad_maximum_fusion.2), calls=%async_computation.1 | async-start | bytes 1114112 | tf_op jit(solution)/shard_map/all_to_all | solution.py:216
  134.8 10.5 %collective-permute-start.16 = (bf16[516,256]{1,0:T(8,128)(2,1)S(1)}, bf16[516,256]{1,0:T(8,128)(2,1)S(1)}, u32[]{:S(2)}, u32[]{:S(2)}) collective-permute-start(bf16[516,256]{1,0:T(8,128)(2,1)S(1)} %get-tuple-element.43), channel_id=1, source_target_pairs={{0,2},{1,3},{2,4},{3,5},{4,6},{5,7},{6,0},{7,1},{8,10},{9,11},{10,... | collective-permute-start | bytes 792584 | tf_op jit(solution)/shard_map/ppermute | solution.py:61
  135.0 10.3 %collective-permute-start.13 = (bf16[516,256]{1,0:T(8,128)(2,1)S(1)}, bf16[516,256]{1,0:T(8,128)(2,1)S(1)}, u32[]{:S(2)}, u32[]{:S(2)}) collective-permute-start(bf16[516,256]{1,0:T(8,128)(2,1)S(1)} %get-tuple-element.44), channel_id=1, source_target_pairs={{0,6},{1,7},{2,0},{3,1},{4,2},{5,3},{6,4},{7,5},{8,14},{9,15},{10,... | collective-permute-start | bytes 792584 | tf_op jit(solution)/shard_map/ppermute | solution.py:61
  139.2 17.3 %collective-permute-start.12 = (bf16[516,512]{1,0:T(8,128)(2,1)S(1)}, bf16[516,512]{1,0:T(8,128)(2,1)S(1)}, u32[]{:S(2)}, u32[]{:S(2)}) collective-permute-start(bf16[516,512]{1,0:T(8,128)(2,1)S(1)} %pad_maximum_fusion.5), channel_id=1, source_target_pairs={{0,2},{1,3},{2,4},{3,5},{4,6},{5,7},{6,0},{7,1},{8,10},{9,11},{10,... | collective-permute-start | bytes 1585160 | tf_op jit(solution)/shard_map/ppermute | solution.py:61
  145.3 3.2 %copy-start.7 = (bf16[512,512]{1,0:T(8,128)(2,1)S(1)}, bf16[512,512]{1,0:T(8,128)(2,1)}, u32[]{:S(2)}) copy-start(bf16[512,512]{1,0:T(8,128)(2,1)} %get-tuple-element.23) | copy-start | bytes 1572868
  145.3 3.2 %copy-start.8 = (bf16[512,512]{1,0:T(8,128)(2,1)S(1)}, bf16[512,512]{1,0:T(8,128)(2,1)}, u32[]{:S(2)}) copy-start(bf16[512,512]{1,0:T(8,128)(2,1)} %get-tuple-element.24) | copy-start | bytes 1572868
  145.5 14.1 %collective-permute-start.14 = (bf16[516,512]{1,0:T(8,128)(2,1)S(1)}, bf16[516,512]{1,0:T(8,128)(2,1)S(1)}, u32[]{:S(2)}, u32[]{:S(2)}) collective-permute-start(bf16[516,512]{1,0:T(8,128)(2,1)S(1)} %pad_maximum_fusion.6), channel_id=1, source_target_pairs={{0,6},{1,7},{2,0},{3,1},{4,2},{5,3},{6,4},{7,5},{8,14},{9,15},{10,... | collective-permute-start | bytes 1585160 | tf_op jit(solution)/shard_map/ppermute | solution.py:61
  148.4 13.5 %collective-permute-start.17 = (bf16[516,512]{1,0:T(8,128)(2,1)S(1)}, bf16[516,512]{1,0:T(8,128)(2,1)S(1)}, u32[]{:S(2)}, u32[]{:S(2)}) collective-permute-start(bf16[516,512]{1,0:T(8,128)(2,1)S(1)} %pad_maximum_fusion.8), channel_id=1, source_target_pairs={{0,1},{1,0},{2,3},{3,2},{4,5},{5,4},{6,7},{7,6},{8,9},{9,8},{10,11... | collective-permute-start | bytes 1585160 | tf_op jit(solution)/shard_map/ppermute | solution.py:61
  162.5 12.6 %collective-permute-start.19 = (bf16[516,512]{1,0:T(8,128)(2,1)S(1)}, bf16[516,512]{1,0:T(8,128)(2,1)S(1)}, u32[]{:S(2)}, u32[]{:S(2)}) collective-permute-start(bf16[516,512]{1,0:T(8,128)(2,1)S(1)} %pad_maximum_fusion.10), channel_id=1, source_target_pairs={{0,6},{1,7},{2,0},{3,1},{4,2},{5,3},{6,4},{7,5},{8,14},{9,15},{10,... | collective-permute-start | bytes 1585160 | tf_op jit(solution)/shard_map/ppermute | solution.py:61
  164.1 24.7 %copy-start.2 = (bf16[4,128,512]{2,1,0:T(8,128)(2,1)S(1)}, bf16[4,128,512]{2,1,0:T(8,128)(2,1)}, u32[]{:S(2)}) copy-start(bf16[4,128,512]{2,1,0:T(8,128)(2,1)} %param.8) | copy-start | bytes 1572868
  164.1 24.7 %copy-start.19 = (f32[512]{0:T(512)S(1)}, f32[512]{0:T(512)}, u32[]{:S(2)}) copy-start(f32[512]{0:T(512)} %param.14) | copy-start | bytes 6148
  164.1 13.8 %collective-permute-start.18 = (bf16[516,512]{1,0:T(8,128)(2,1)S(1)}, bf16[516,512]{1,0:T(8,128)(2,1)S(1)}, u32[]{:S(2)}, u32[]{:S(2)}) collective-permute-start(bf16[516,512]{1,0:T(8,128)(2,1)S(1)} %pad_maximum_fusion.9), channel_id=1, source_target_pairs={{0,2},{1,3},{2,4},{3,5},{4,6},{5,7},{6,0},{7,1},{8,10},{9,11},{10,... | collective-permute-start | bytes 1585160 | tf_op jit(solution)/shard_map/ppermute | solution.py:61
  164.8 13.2 %collective-permute-start.15 = (bf16[516,512]{1,0:T(8,128)(2,1)S(1)}, bf16[516,512]{1,0:T(8,128)(2,1)S(1)}, u32[]{:S(2)}, u32[]{:S(2)}) collective-permute-start(bf16[516,512]{1,0:T(8,128)(2,1)S(1)} %pad_maximum_fusion.7), channel_id=1, source_target_pairs={{0,1},{1,0},{2,3},{3,2},{4,5},{5,4},{6,7},{7,6},{8,9},{9,8},{10,11... | collective-permute-start | bytes 1585160 | tf_op jit(solution)/shard_map/ppermute | solution.py:61
  178.3 5.2 %collective-permute-start.22 = (f32[516]{0:T(1024)S(1)}, f32[516]{0:T(1024)S(1)}, u32[]{:S(2)}, u32[]{:S(2)}) collective-permute-start(f32[516]{0:T(1024)S(1)} %multiply_reduce_fusion), channel_id=1, source_target_pairs={{0,4},{1,5},{2,6},{3,7},{4,0},{5,1},{6,2},{7,3},{8,12},{9,13},{10,... | collective-permute-start | bytes 6200 | tf_op jit(solution)/shard_map/ppermute | solution.py:80
  178.8 4.7 %collective-permute-start.21 = (f32[516]{0:T(1024)S(1)}, f32[516]{0:T(1024)S(1)}, u32[]{:S(2)}, u32[]{:S(2)}) collective-permute-start(f32[516]{0:T(1024)S(1)} %multiply_reduce_fusion), channel_id=1, source_target_pairs={{0,6},{1,7},{2,0},{3,1},{4,2},{5,3},{6,4},{7,5},{8,14},{9,15},{10,... | collective-permute-start | bytes 6200 | tf_op jit(solution)/shard_map/ppermute | solution.py:80
  180.4 4.8 %collective-permute-start.20 = (f32[516]{0:T(1024)S(1)}, f32[516]{0:T(1024)S(1)}, u32[]{:S(2)}, u32[]{:S(2)}) collective-permute-start(f32[516]{0:T(1024)S(1)} %multiply_reduce_fusion), channel_id=1, source_target_pairs={{0,2},{1,3},{2,4},{3,5},{4,6},{5,7},{6,0},{7,1},{8,10},{9,11},{10,... | collective-permute-start | bytes 6200 | tf_op jit(solution)/shard_map/ppermute | solution.py:80
  185.2 3.6 %collective-permute-start.23 = (f32[516]{0:T(1024)S(1)}, f32[516]{0:T(1024)S(1)}, u32[]{:S(2)}, u32[]{:S(2)}) collective-permute-start(f32[516]{0:T(1024)S(1)} %add_add_fusion.1), channel_id=1, source_target_pairs={{0,1},{1,0},{2,3},{3,2},{4,5},{5,4},{6,7},{7,6},{8,9},{9,8},{10,11... | collective-permute-start | bytes 6200 | tf_op jit(solution)/shard_map/ppermute | solution.py:81

commit v3 on v2

--- a/solution.py
+++ b/solution.py
@@ -113,7 +113,7 @@
 def attend_pair(q_all, k_all, v_all, q_new, k_new, v_new, length):
     count = q_all.shape[0]
     scale = HD ** (-0.5)
-    bounds = (0, count // 2, count * 3 // 4, count)
+    bounds = (0, count * 7 // 16, count * 3 // 4, count)
     outs = []
     for begin, stop in zip(bounds[:-1], bounds[1:]):
         scores = (

time: 191 us -> 190 us (level)
  no operation moved by 1% of the time
where the time goes in v3:
time: 190 us
  waiting for transfers between devices  71.2 us (37%)
  starting transfers between devices  47.4 us (25%)
  matrix products  23.5 us (12%)
  local copies, waits for them, and re-layouts  20.6 us (11%)
  other arithmetic  19.3 us (10%)
  Pallas kernels  4.11 us (2%)
  between operations  3.32 us (2%)
    ppermute x8, waiting for transfers between devices, tp_reduce_scatter(): lax.ppermute(value.astype(jnp.bfloat16), 'tp', perm).astype(jnp.float32)  30.7 us
    all_to_all x1, waiting for transfers between devices, body(): got = lax.all_to_all(qkv, 'seq', 0, 0, tiled=True)  13.3 us
    ppermute x8, starting transfers between devices, tp_gather(): send = lambda value, perm: lax.ppermute(value, 'tp', perm)  13.3 us
    dot_general x3, matrix products, body(): jnp.einsum('tn,cnf->ctf', jnp.concatenate(blocks, 1), jnp.concatenate(w_b...  11 us
    dynamic_slice x2, local copies, waits for them, and re-layouts, in_relative_order(): lax.dynamic_slice_in_dim(weight, order[name] * width_local, width_local,...  10.8 us
    ppermute x8, waiting for transfers between devices, tp_gather(): send = lambda value, perm: lax.ppermute(value, 'tp', perm)  9.44 us
    ppermute x8, starting transfers between devices, tp_reduce_scatter(): lax.ppermute(value.astype(jnp.bfloat16), 'tp', perm).astype(jnp.float32)  8.82 us
    ppermute x6, starting transfers between devices, tp_sum(): lax.ppermute(values, 'tp', [(i, (i + shift) % size) for i in range(size)])  8.39 us
  transfers between devices with their start and end apart: 26, of which 19 were waited for; matrix products, arithmetic and copies ran while one was open for 17% of the time, Pallas kernels for 0%

profile of v3, /device:TPU:32, one launch (start us, length us, event | category | flops | bytes accessed | tf_op | source)
XLA Modules:
  0.0 189.5 jit_solution(14717120428798347715)
XLA Ops:
  0.6 1.9 %pad_maximum_fusion.3 = bf16[516,512]{1,0:T(8,128)(2,1)} fusion(bf16[4,512]{1,0:T(4,128)(2,1)} %param.9, bf16[512,512]{1,0:T(8,128)(2,1)} %bitcast.93), kind=kLoop, calls=%fused_computation.100 | loop fusion | flops 1056768 | bytes 1056768 | tf_op jit(solution)/shard_map/concatenate | solution.py:159
  2.5 3.0 %collective-permute-start.2 = (bf16[516,512]{1,0:T(8,128)(2,1)}, bf16[516,512]{1,0:T(8,128)(2,1)}, u32[]{:S(2)}, u32[]{:S(2)}) collective-permute-start(bf16[516,512]{1,0:T(8,128)(2,1)} %pad_maximum_fusion.3), channel_id=1, source_target_pairs={{0,6},{1,7},{2,0},{3,1},{4,2},{5,3},{6,4},{7,5},{8,14},{9,15},{10,... | collective-permute-start | bytes 1585160 | tf_op jit(solution)/shard_map/ppermute | solution.py:42
  5.5 1.5 collective-permute-start
  7.0 7.4 %constant_dynamic-slice_fusion.12 = (bf16[3,512,512]{2,1,0:T(8,128)(2,1)S(1)}, bf16[3,512,512]{2,1,0:T(8,128)(2,1)S(1)}, bf16[3,512,512]{2,1,0:T(8,128)(2,1)}, b...) fusion(bf16[3,4096,512]{2,1,0:T(8,128)(2,1)} %param.10, ...), kind=kLoop, calls=%fused_computation.149 | loop fusion | bytes 22020124 | tf_op jit(solution)/shard_map/dynamic_slice | solution.py:164
  14.5 1.0 fusion.90
  15.5 3.9 %collective-permute-done = bf16[516,512]{1,0:T(8,128)(2,1)} collective-permute-done((bf16[516,512]{1,0:T(8,128)(2,1)}, bf16[516,512]{1,0:T(8,128)(2,1)}, u32[]{:S(2)}, u32[]{:S(2)}) %collective-permute-start) | collective-permute-done | bytes 528416 | tf_op jit(solution)/shard_map/ppermute | solution.py:42
  19.4 1.0 slice.254
  20.6 1.2 fusion.123
  21.9 1.0 slice.251
  23.2 1.5 collective-permute-start.3
  24.7 3.1 %collective-permute-start.4 = (bf16[516,512]{1,0:T(8,128)(2,1)S(1)}, bf16[516,512]{1,0:T(8,128)(2,1)S(1)}, u32[]{:S(2)}, u32[]{:S(2)}) collective-permute-start(bf16[516,512]{1,0:T(8,128)(2,1)S(1)} %get-tuple-element.50), channel_id=1, source_target_pairs={{0,6},{1,7},{2,0},{3,1},{4,2},{5,3},{6,4},{7,5},{8,14},{9,15},{10,... | collective-permute-start | bytes 1585160 | tf_op jit(solution)/shard_map/ppermute | solution.py:42
  27.8 5.4 %fusion = f32[3,512,516]{1,2,0:T(8,128)S(1)} fusion(bf16[3,512,512]{2,1,0:T(8,128)(2,1)S(1)} %copy-done.4, bf16[3,512,512]{2,1,0:T(8,128)(2,1)S(1)} %copy-done.5, bf16[3,512,512]{2,1,0:T(8,128)(2,1)S(1)} %copy-done.6, bf16[3,512,512]{2,1,0:T(8,128)(2,1)} %get-tuple-element.13, bf16[516,512]{1,0:T(8,128)(2,1)} %collective-permute-done.2, ...), kind=kOutput, calls=%fused_computation | convolution fusion | flops 3282124800 | bytes 11575296 | tf_op jit(solution)/shard_map/tn,cnf->ctf/dot_general | solution.py:172
  33.3 2.5 %collective-permute-done.3 = bf16[516,512]{1,0:T(8,128)(2,1)S(1)} collective-permute-done((bf16[516,512]{1,0:T(8,128)(2,1)S(1)}, bf16[516,512]{1,0:T(8,128)(2,1)S(1)}, u32[]{:S(2)}, u32[]{:S(2)}) %collective-permute-start.3) | collective-permute-done | bytes 528416 | tf_op jit(solution)/shard_map/ppermute | solution.py:42
  35.8 1.6 collective-permute-done.4
  37.5 1.5 collective-permute-start.7
  39.0 2.6 %collective-permute-start.6 = (bf16[516,256]{1,0:T(8,128)(2,1)S(1)}, bf16[516,256]{1,0:T(8,128)(2,1)S(1)}, u32[]{:S(2)}, u32[]{:S(2)}) collective-permute-start(bf16[516,256]{1,0:T(8,128)(2,1)S(1)} %get-tuple-element.43), channel_id=1, source_target_pairs={{0,6},{1,7},{2,0},{3,1},{4,2},{5,3},{6,4},{7,5},{8,14},{9,15},{10,... | collective-permute-start | bytes 792584 | tf_op jit(solution)/shard_map/ppermute | solution.py:42
  41.6 2.8 %fusion.8 = f32[3,512,516]{1,2,0:T(8,128)S(1)} fusion(bf16[3,512,512]{2,1,0:T(8,128)(2,1)S(1)} %copy-done.3, bf16[3,512,512]{2,1,0:T(8,128)(2,1)S(1)} %get-tuple-element.9, bf16[3,512,512]{2,1,0:T(8,128)(2,1)S(1)} %get-tuple-element.8, bf16[516,1536]{1,0:T(8,128)(2,1)S(1)} %slice_dynamic-update-slice_fusion), kind=kOutput, calls=%fused_computation.8 | convolution fusion | flops 2448949248 | bytes 9474048 | tf_op jit(solution)/shard_map/tn,cnf->ctf/dot_general | solution.py:172
  44.4 1.2 collective-permute-done.7
  45.7 2.7 %add_bitcast_fusion.proj_ref = f32[3,516,512]{2,1,0:T(8,128)S(1)} fusion(f32[3,512,516]{1,2,0:T(8,128)S(1)} %fusion, f32[3,512,516]{1,2,0:T(8,128)S(1)} %fusion.8, bf16[3,4096,512]{2,1,0:T(8,128)(2,1)} %param.10, s32[]{:T(128)S(6)} %select_n.121, bf16[516,256]{1,0:T(8,128)(2,1)S(1)} %collective-permute-done.7, bf16[516,256]{1,0:T(8,128)(2,1)S(1)} %collective-permute-done.6), kind=kOutput, calls=%fused_computation.26 | convolution fusion | flops 814239744 | bytes 11612164 | tf_op jit(solution)/shard_map/tn,cnf->ctf/dot_general | solution.py:172
  48.7 3.6 %collective-permute-start.10 = (f32[2,516]{1,0:T(2,128)S(1)}, f32[2,516]{1,0:T(2,128)S(1)}, u32[]{:S(2)}, u32[]{:S(2)}) collective-permute-start(f32[2,516]{1,0:T(2,128)S(1)} %pad_maximum_fusion.14), channel_id=1, source_target_pairs={{0,4},{1,5},{2,6},{3,7},{4,0},{5,1},{6,2},{7,3},{8,12},{9,13},{10,... | collective-permute-start | bytes 12392 | tf_op jit(solution)/shard_map/ppermute | solution.py:80
  52.9 1.4 collective-permute-start.8
  54.3 1.0 pad_maximum_fusion.12
  55.9 1.9 collective-permute-done.8
  59.0 2.5 %collective-permute-done.11 = f32[2,516]{1,0:T(2,128)S(1)} collective-permute-done((f32[2,516]{1,0:T(2,128)S(1)}, f32[2,516]{1,0:T(2,128)S(1)}, u32[]{:S(2)}, u32[]{:S(2)}) %collective-permute-start.11) | collective-permute-done | bytes 4160 | tf_op jit(solution)/shard_map/ppermute | solution.py:81
  61.5 1.1 copy.10.square_ref
  62.6 4.1 %shard_map.95 = (bf16[16,3,128,128]{3,2,1,0:T(8,128)(2,1)}, f32[3,4,512]{2,1,0:T(4,128)}) custom-call(f32[3,516,512]{2,1,0:T(8,128)} %copy-done, f32[2,516,1]{2,1,0:T(8,128)} %copy.10.square_ref, f32[2,1,512]{2,1,0:T(1,128)} %broadcast_in_dim.54.gain_ref, f32[516,128]{1,0:T(8,128)} %get-tuple-element.67.cos_ref, f32[516,128]{1,0:T(8,128)} %get-tuple-element.68.sin_ref), custom_call_target="tpu_custom_call" | custom-call | tf_op jit(solution)/shard_map/pallas_call | solution.py:104
  66.7 7.7 %all-to-all-start = ((bf16[16,3,128,128]{3,2,1,0:T(8,128)(2,1)}), bf16[16,3,128,128]{3,2,1,0:T(8,128)(2,1)S(1)}, u32[]{:S(2)}, u32[]{:S(2)}) async-start(bf16[16,3,128,128]{3,2,1,0:T(8,128)(2,1)} %get-tuple-element.4), calls=%async_computation | async-start | bytes 3145728 | tf_op jit(solution)/shard_map/all_to_all | solution.py:201
  75.0 1.2 iota_compare_fusion.5
  76.2 1.2 iota_compare_fusion.3
  78.0 1.2 iota_compare_fusion.4
  81.2 13.3 %all-to-all-done = bf16[16,3,128,128]{3,2,1,0:T(8,128)(2,1)S(1)} async-done(((bf16[16,3,128,128]{3,2,1,0:T(8,128)(2,1)}), bf16[16,3,128,128]{3,2,1,0:T(8,128)(2,1)S(1)}, u32[]{:S(2)}, u32[]{:S(2)}) %all-to-all-start) | async-done | bytes 1572896 | tf_op jit(solution)/shard_map/all_to_all | solution.py:201
  94.8 1.3 fusion.91
  96.8 1.9 fusion.94
  99.4 0.9 fusion.117
  101.0 2.1 %fusion.124 = (f32[512]{0:T(512)S(1)}, f32[512,2048]{1,0:T(8,128)S(1)}) fusion(bf16[512,128]{1,0:T(8,128)(2,1)S(1)} %bitcast.109, bf16[2048,128]{1,0:T(8,128)(2,1)S(1)} %bitcast.101, pred[2048]{0:T(1024)(128)(4,1)} %iota_compare_fusion.3, s32[512]{0:T(512)} %iota_add_fusion.1), kind=kOutput, calls=%fused_computation.195 | convolution fusion | flops 273677824 | bytes 4855808 | tf_op jit(solution)/shard_map/dot_general | solution.py:120
  103.1 1.5 fusion.17
  104.6 1.3 fusion.71
  106.0 1.3 fusion.125
  107.3 1.4 fusion.19
  108.7 1.3 fusion.77
  110.0 1.3 fusion.21
  112.3 1.0 fusion.58
  113.6 0.8 pad_maximum_fusion.2
  114.4 8.0 %all-to-all-start.1 = ((bf16[16,136,128]{2,1,0:T(8,128)(2,1)}), bf16[16,136,128]{2,1,0:T(8,128)(2,1)S(1)}, u32[]{:S(2)}, u32[]{:S(2)}) async-start(bf16[16,136,128]{2,1,0:T(8,128)(2,1)} %pad_maximum_fusion.2), calls=%async_computation.1 | async-start | bytes 1114112 | tf_op jit(solution)/shard_map/all_to_all | solution.py:216
  122.4 3.4 %constant_dynamic-slice_fusion.6 = (bf16[512,512]{1,0:T(8,128)(2,1)S(1)}, bf16[512,512]{1,0:T(8,128)(2,1)S(1)}, bf16[512,512]{1,0:T(8,128)(2,1)S(1)}, bf16[512,5...) fusion(bf16[512,4096]{1,0:T(8,128)(2,1)} %param.11, ...), kind=kLoop, calls=%fused_computation.142 | loop fusion | bytes 7340060 | tf_op jit(solution)/shard_map/dynamic_slice | solution.py:164
  125.9 5.7 %all-to-all-done.1 = bf16[16,136,128]{2,1,0:T(8,128)(2,1)S(1)} async-done(((bf16[16,136,128]{2,1,0:T(8,128)(2,1)}), bf16[16,136,128]{2,1,0:T(8,128)(2,1)S(1)}, u32[]{:S(2)}, u32[]{:S(2)}) %all-to-all-start.1) | async-done | bytes 557088 | tf_op jit(solution)/shard_map/all_to_all | solution.py:216
  132.1 1.5 convolution_convert_fusion
  133.8 3.1 %collective-permute-start.13 = (bf16[516,256]{1,0:T(8,128)(2,1)S(1)}, bf16[516,256]{1,0:T(8,128)(2,1)S(1)}, u32[]{:S(2)}, u32[]{:S(2)}) collective-permute-start(bf16[516,256]{1,0:T(8,128)(2,1)S(1)} %get-tuple-element.42), channel_id=1, source_target_pairs={{0,6},{1,7},{2,0},{3,1},{4,2},{5,3},{6,4},{7,5},{8,14},{9,15},{10,... | collective-permute-start | bytes 792584 | tf_op jit(solution)/shard_map/ppermute | solution.py:61
  136.9 1.0 fusion.126
  138.1 6.0 %collective-permute-done.16 = bf16[516,256]{1,0:T(8,128)(2,1)S(1)} collective-permute-done((bf16[516,256]{1,0:T(8,128)(2,1)S(1)}, bf16[516,256]{1,0:T(8,128)(2,1)S(1)}, u32[]{:S(2)}, u32[]{:S(2)}) %collective-permute-start.16) | collective-permute-done | bytes 264224 | tf_op jit(solution)/shard_map/ppermute | solution.py:61
  144.4 2.8 %collective-permute-start.14 = (bf16[516,512]{1,0:T(8,128)(2,1)S(1)}, bf16[516,512]{1,0:T(8,128)(2,1)S(1)}, u32[]{:S(2)}, u32[]{:S(2)}) collective-permute-start(bf16[516,512]{1,0:T(8,128)(2,1)S(1)} %pad_maximum_fusion.6), channel_id=1, source_target_pairs={{0,6},{1,7},{2,0},{3,1},{4,2},{5,3},{6,4},{7,5},{8,14},{9,15},{10,... | collective-permute-start | bytes 1585160 | tf_op jit(solution)/shard_map/ppermute | solution.py:61
  147.4 1.3 fusion.127
  148.7 6.7 %collective-permute-done.12 = bf16[516,512]{1,0:T(8,128)(2,1)S(1)} collective-permute-done((bf16[516,512]{1,0:T(8,128)(2,1)S(1)}, bf16[516,512]{1,0:T(8,128)(2,1)S(1)}, u32[]{:S(2)}, u32[]{:S(2)}) %collective-permute-start.12) | collective-permute-done | bytes 528416 | tf_op jit(solution)/shard_map/ppermute | solution.py:61
  155.5 2.9 %collective-permute-done.14 = bf16[516,512]{1,0:T(8,128)(2,1)S(1)} collective-permute-done((bf16[516,512]{1,0:T(8,128)(2,1)S(1)}, bf16[516,512]{1,0:T(8,128)(2,1)S(1)}, u32[]{:S(2)}, u32[]{:S(2)}) %collective-permute-start.14) | collective-permute-done | bytes 528416 | tf_op jit(solution)/shard_map/ppermute | solution.py:61
  158.6 2.2 %collective-permute-done.17 = bf16[516,512]{1,0:T(8,128)(2,1)S(1)} collective-permute-done((bf16[516,512]{1,0:T(8,128)(2,1)S(1)}, bf16[516,512]{1,0:T(8,128)(2,1)S(1)}, u32[]{:S(2)}, u32[]{:S(2)}) %collective-permute-start.17) | collective-permute-done | bytes 528416 | tf_op jit(solution)/shard_map/ppermute | solution.py:61
  161.4 1.6 collective-permute-start.19
  164.0 9.9 %collective-permute-done.19 = bf16[516,512]{1,0:T(8,128)(2,1)S(1)} collective-permute-done((bf16[516,512]{1,0:T(8,128)(2,1)S(1)}, bf16[516,512]{1,0:T(8,128)(2,1)S(1)}, u32[]{:S(2)}, u32[]{:S(2)}) %collective-permute-start.19) | collective-permute-done | bytes 528416 | tf_op jit(solution)/shard_map/ppermute | solution.py:61
  173.9 2.9 %collective-permute-done.18 = bf16[516,512]{1,0:T(8,128)(2,1)S(1)} collective-permute-done((bf16[516,512]{1,0:T(8,128)(2,1)S(1)}, bf16[516,512]{1,0:T(8,128)(2,1)S(1)}, u32[]{:S(2)}, u32[]{:S(2)}) %collective-permute-start.18) | collective-permute-done | bytes 528416 | tf_op jit(solution)/shard_map/ppermute | solution.py:61
  177.7 1.6 collective-permute-start.21
  179.2 0.8 collective-permute-start.20
  180.0 2.4 %collective-permute-done.22 = f32[516]{0:T(1024)S(1)} collective-permute-done((f32[516]{0:T(1024)S(1)}, f32[516]{0:T(1024)S(1)}, u32[]{:S(2)}, u32[]{:S(2)}) %collective-permute-start.22) | collective-permute-done | bytes 2096 | tf_op jit(solution)/shard_map/ppermute | solution.py:80
  182.4 1.6 collective-permute-done.20
  184.5 3.2 %collective-permute-done.23 = f32[516]{0:T(1024)S(1)} collective-permute-done((f32[516]{0:T(1024)S(1)}, f32[516]{0:T(1024)S(1)}, u32[]{:S(2)}, u32[]{:S(2)}) %collective-permute-start.23) | collective-permute-done | bytes 2096 | tf_op jit(solution)/shard_map/ppermute | solution.py:81
  188.1 0.8 slice.295
  (130 shorter events, 13.7 us)
Async XLA Ops:
  2.5 19.3 %collective-permute-start.2 = (bf16[516,512]{1,0:T(8,128)(2,1)}, bf16[516,512]{1,0:T(8,128)(2,1)}, u32[]{:S(2)}, u32[]{:S(2)}) collective-permute-start(bf16[516,512]{1,0:T(8,128)(2,1)} %pad_maximum_fusion.3), channel_id=1, source_target_pairs={{0,6},{1,7},{2,0},{3,1},{4,2},{5,3},{6,4},{7,5},{8,14},{9,15},{10,... | collective-permute-start | bytes 1585160 | tf_op jit(solution)/shard_map/ppermute | solution.py:42
  5.5 15.1 %collective-permute-start.1 = (bf16[516,512]{1,0:T(8,128)(2,1)}, bf16[516,512]{1,0:T(8,128)(2,1)}, u32[]{:S(2)}, u32[]{:S(2)}) collective-permute-start(bf16[516,512]{1,0:T(8,128)(2,1)} %pad_maximum_fusion.3), channel_id=1, source_target_pairs={{0,2},{1,3},{2,4},{3,5},{4,6},{5,7},{6,0},{7,1},{8,10},{9,11},{10,... | collective-permute-start | bytes 1585160 | tf_op jit(solution)/shard_map/ppermute | solution.py:42
  5.5 13.9 %collective-permute-start = (bf16[516,512]{1,0:T(8,128)(2,1)}, bf16[516,512]{1,0:T(8,128)(2,1)}, u32[]{:S(2)}, u32[]{:S(2)}) collective-permute-start(bf16[516,512]{1,0:T(8,128)(2,1)} %pad_maximum_fusion.3), channel_id=1, source_target_pairs={{0,1},{1,0},{2,3},{3,2},{4,5},{5,4},{6,7},{7,6},{8,9},{9,8},{10,11... | collective-permute-start | bytes 1585160 | tf_op jit(solution)/shard_map/ppermute | solution.py:42
  7.0 7.4 %copy-start.24 = (s32[4]{0:T(128)S(1)}, s32[4]{0:T(128)}, u32[]{:S(2)}) copy-start(s32[4]{0:T(128)} %param.15) | copy-start | bytes 52
  14.5 13.3 %copy-start.6 = (bf16[3,512,512]{2,1,0:T(8,128)(2,1)S(1)}, bf16[3,512,512]{2,1,0:T(8,128)(2,1)}, u32[]{:S(2)}) copy-start(bf16[3,512,512]{2,1,0:T(8,128)(2,1)} %get-tuple-element.12) | copy-start | bytes 4718596
  20.4 7.4 %copy-start.1 = (bf16[4,128,512]{2,1,0:T(8,128)(2,1)S(1)}, bf16[4,128,512]{2,1,0:T(8,128)(2,1)}, u32[]{:S(2)}) copy-start(bf16[4,128,512]{2,1,0:T(8,128)(2,1)} %param.8) | copy-start | bytes 1572868
  20.4 7.4 %copy-start.4 = (bf16[3,512,512]{2,1,0:T(8,128)(2,1)S(1)}, bf16[3,512,512]{2,1,0:T(8,128)(2,1)}, u32[]{:S(2)}) copy-start(bf16[3,512,512]{2,1,0:T(8,128)(2,1)} %get-tuple-element.10) | copy-start | bytes 4718596
  20.4 7.4 %copy-start.5 = (bf16[3,512,512]{2,1,0:T(8,128)(2,1)S(1)}, bf16[3,512,512]{2,1,0:T(8,128)(2,1)}, u32[]{:S(2)}) copy-start(bf16[3,512,512]{2,1,0:T(8,128)(2,1)} %get-tuple-element.11) | copy-start | bytes 4718596
  20.4 7.4 %copy-start.14 = (bf16[4,512]{1,0:T(4,128)(2,1)S(1)}, bf16[4,512]{1,0:T(4,128)(2,1)}, u32[]{:S(2)}) copy-start(bf16[4,512]{1,0:T(4,128)(2,1)} %param.9) | copy-start | bytes 12292
  23.0 14.5 %collective-permute-start.5 = (bf16[516,512]{1,0:T(8,128)(2,1)S(1)}, bf16[516,512]{1,0:T(8,128)(2,1)S(1)}, u32[]{:S(2)}, u32[]{:S(2)}) collective-permute-start(bf16[516,512]{1,0:T(8,128)(2,1)S(1)} %get-tuple-element.49), channel_id=1, source_target_pairs={{0,2},{1,3},{2,4},{3,5},{4,6},{5,7},{6,0},{7,1},{8,10},{9,11},{10,... | collective-permute-start | bytes 1585160 | tf_op jit(solution)/shard_map/ppermute | solution.py:42
  23.2 12.6 %collective-permute-start.3 = (bf16[516,512]{1,0:T(8,128)(2,1)S(1)}, bf16[516,512]{1,0:T(8,128)(2,1)S(1)}, u32[]{:S(2)}, u32[]{:S(2)}) collective-permute-start(bf16[516,512]{1,0:T(8,128)(2,1)S(1)} %get-tuple-element.51), channel_id=1, source_target_pairs={{0,1},{1,0},{2,3},{3,2},{4,5},{5,4},{6,7},{7,6},{8,9},{9,8},{10,11... | collective-permute-start | bytes 1585160 | tf_op jit(solution)/shard_map/ppermute | solution.py:42
  24.7 12.7 %collective-permute-start.4 = (bf16[516,512]{1,0:T(8,128)(2,1)S(1)}, bf16[516,512]{1,0:T(8,128)(2,1)S(1)}, u32[]{:S(2)}, u32[]{:S(2)}) collective-permute-start(bf16[516,512]{1,0:T(8,128)(2,1)S(1)} %get-tuple-element.50), channel_id=1, source_target_pairs={{0,6},{1,7},{2,0},{3,1},{4,2},{5,3},{6,4},{7,5},{8,14},{9,15},{10,... | collective-permute-start | bytes 1585160 | tf_op jit(solution)/shard_map/ppermute | solution.py:42
  33.3 8.3 %copy-start.3 = (bf16[3,512,512]{2,1,0:T(8,128)(2,1)S(1)}, bf16[3,512,512]{2,1,0:T(8,128)(2,1)}, u32[]{:S(2)}) copy-start(bf16[3,512,512]{2,1,0:T(8,128)(2,1)} %get-tuple-element.14) | copy-start | bytes 4718596
  37.5 8.2 %collective-permute-start.7 = (bf16[516,256]{1,0:T(8,128)(2,1)S(1)}, bf16[516,256]{1,0:T(8,128)(2,1)S(1)}, u32[]{:S(2)}, u32[]{:S(2)}) collective-permute-start(bf16[516,256]{1,0:T(8,128)(2,1)S(1)} %get-tuple-element.45), channel_id=1, source_target_pairs={{0,2},{1,3},{2,4},{3,5},{4,6},{5,7},{6,0},{7,1},{8,10},{9,11},{10,... | collective-permute-start | bytes 792584 | tf_op jit(solution)/shard_map/ppermute | solution.py:42
  39.0 6.7 %collective-permute-start.6 = (bf16[516,256]{1,0:T(8,128)(2,1)S(1)}, bf16[516,256]{1,0:T(8,128)(2,1)S(1)}, u32[]{:S(2)}, u32[]{:S(2)}) collective-permute-start(bf16[516,256]{1,0:T(8,128)(2,1)S(1)} %get-tuple-element.43), channel_id=1, source_target_pairs={{0,6},{1,7},{2,0},{3,1},{4,2},{5,3},{6,4},{7,5},{8,14},{9,15},{10,... | collective-permute-start | bytes 792584 | tf_op jit(solution)/shard_map/ppermute | solution.py:42
  48.4 14.2 %copy-start = (f32[3,516,512]{2,1,0:T(8,128)}, f32[3,516,512]{2,1,0:T(8,128)S(1)}, u32[]{:S(2)}) copy-start(f32[3,516,512]{2,1,0:T(8,128)S(1)} %add_bitcast_fusion.proj_ref) | copy-start | bytes 9510916
  48.4 10.0 %copy-start.21 = (f32[512]{0:T(512)S(1)}, f32[512]{0:T(512)}, u32[]{:S(2)}) copy-start(f32[512]{0:T(512)} %param.13) | copy-start | bytes 6148
  48.4 10.0 %copy-start.22 = (f32[512]{0:T(512)S(1)}, f32[512]{0:T(512)}, u32[]{:S(2)}) copy-start(f32[512]{0:T(512)} %param.12) | copy-start | bytes 6148
  48.7 6.6 %collective-permute-start.10 = (f32[2,516]{1,0:T(2,128)S(1)}, f32[2,516]{1,0:T(2,128)S(1)}, u32[]{:S(2)}, u32[]{:S(2)}) collective-permute-start(f32[2,516]{1,0:T(2,128)S(1)} %pad_maximum_fusion.14), channel_id=1, source_target_pairs={{0,4},{1,5},{2,6},{3,7},{4,0},{5,1},{6,2},{7,3},{8,12},{9,13},{10,... | collective-permute-start | bytes 12392 | tf_op jit(solution)/shard_map/ppermute | solution.py:80
  52.3 3.6 %collective-permute-start.9 = (f32[2,516]{1,0:T(2,128)S(1)}, f32[2,516]{1,0:T(2,128)S(1)}, u32[]{:S(2)}, u32[]{:S(2)}) collective-permute-start(f32[2,516]{1,0:T(2,128)S(1)} %pad_maximum_fusion.14), channel_id=1, source_target_pairs={{0,6},{1,7},{2,0},{3,1},{4,2},{5,3},{6,4},{7,5},{8,14},{9,15},{10,... | collective-permute-start | bytes 12392 | tf_op jit(solution)/shard_map/ppermute | solution.py:80
  52.9 4.8 %collective-permute-start.8 = (f32[2,516]{1,0:T(2,128)S(1)}, f32[2,516]{1,0:T(2,128)S(1)}, u32[]{:S(2)}, u32[]{:S(2)}) collective-permute-start(f32[2,516]{1,0:T(2,128)S(1)} %pad_maximum_fusion.14), channel_id=1, source_target_pairs={{0,2},{1,3},{2,4},{3,5},{4,6},{5,7},{6,0},{7,1},{8,10},{9,11},{10,... | collective-permute-start | bytes 12392 | tf_op jit(solution)/shard_map/ppermute | solution.py:80
  57.8 3.7 %collective-permute-start.11 = (f32[2,516]{1,0:T(2,128)S(1)}, f32[2,516]{1,0:T(2,128)S(1)}, u32[]{:S(2)}, u32[]{:S(2)}) collective-permute-start(f32[2,516]{1,0:T(2,128)S(1)} %add_add_fusion), channel_id=1, source_target_pairs={{0,1},{1,0},{2,3},{3,2},{4,5},{5,4},{6,7},{7,6},{8,9},{9,8},{10,11... | collective-permute-start | bytes 12392 | tf_op jit(solution)/shard_map/ppermute | solution.py:81
  66.7 13.2 %copy-start.13 = (f32[3,4,512]{2,1,0:T(4,128)S(1)}, f32[3,4,512]{2,1,0:T(4,128)}, u32[]{:S(2)}) copy-start(f32[3,4,512]{2,1,0:T(4,128)} %get-tuple-element.5) | copy-start | bytes 73732
  66.7 27.8 %all-to-all-start = ((bf16[16,3,128,128]{3,2,1,0:T(8,128)(2,1)}), bf16[16,3,128,128]{3,2,1,0:T(8,128)(2,1)S(1)}, u32[]{:S(2)}, u32[]{:S(2)}) async-start(bf16[16,3,128,128]{3,2,1,0:T(8,128)(2,1)} %get-tuple-element.4), calls=%async_computation | async-start | bytes 3145728 | tf_op jit(solution)/shard_map/all_to_all | solution.py:201
  98.6 1.6 copy-start.15
  101.0 2.1 %copy-start.18 = (pred[2048]{0:T(1024)(128)(4,1)S(1)}, pred[2048]{0:T(1024)(128)(4,1)}, u32[]{:S(2)}) copy-start(pred[2048]{0:T(1024)(128)(4,1)} %iota_compare_fusion.3) | copy-start | bytes 6148
  101.0 2.1 %copy-start.19 = (s32[512]{0:T(512)S(1)}, s32[512]{0:T(512)}, u32[]{:S(2)}) copy-start(s32[512]{0:T(512)} %iota_add_fusion.1) | copy-start | bytes 6148
  104.6 1.4 copy-start.12
  104.6 1.4 copy-start.16
  104.6 1.4 copy-start.17
  108.7 1.3 copy-start.10
  108.7 1.3 copy-start.11
  108.7 1.3 copy-start.23
  111.4 0.9 copy-start.9
  114.4 17.1 %all-to-all-start.1 = ((bf16[16,136,128]{2,1,0:T(8,128)(2,1)}), bf16[16,136,128]{2,1,0:T(8,128)(2,1)S(1)}, u32[]{:S(2)}, u32[]{:S(2)}) async-start(bf16[16,136,128]{2,1,0:T(8,128)(2,1)} %pad_maximum_fusion.2), calls=%async_computation.1 | async-start | bytes 1114112 | tf_op jit(solution)/shard_map/all_to_all | solution.py:216
  133.6 10.5 %collective-permute-start.16 = (bf16[516,256]{1,0:T(8,128)(2,1)S(1)}, bf16[516,256]{1,0:T(8,128)(2,1)S(1)}, u32[]{:S(2)}, u32[]{:S(2)}) collective-permute-start(bf16[516,256]{1,0:T(8,128)(2,1)S(1)} %get-tuple-element.41), channel_id=1, source_target_pairs={{0,2},{1,3},{2,4},{3,5},{4,6},{5,7},{6,0},{7,1},{8,10},{9,11},{10,... | collective-permute-start | bytes 792584 | tf_op jit(solution)/shard_map/ppermute | solution.py:61
  133.8 10.3 %collective-permute-start.13 = (bf16[516,256]{1,0:T(8,128)(2,1)S(1)}, bf16[516,256]{1,0:T(8,128)(2,1)S(1)}, u32[]{:S(2)}, u32[]{:S(2)}) collective-permute-start(bf16[516,256]{1,0:T(8,128)(2,1)S(1)} %get-tuple-element.42), channel_id=1, source_target_pairs={{0,6},{1,7},{2,0},{3,1},{4,2},{5,3},{6,4},{7,5},{8,14},{9,15},{10,... | collective-permute-start | bytes 792584 | tf_op jit(solution)/shard_map/ppermute | solution.py:61
  138.0 17.3 %collective-permute-start.12 = (bf16[516,512]{1,0:T(8,128)(2,1)S(1)}, bf16[516,512]{1,0:T(8,128)(2,1)S(1)}, u32[]{:S(2)}, u32[]{:S(2)}) collective-permute-start(bf16[516,512]{1,0:T(8,128)(2,1)S(1)} %pad_maximum_fusion.5), channel_id=1, source_target_pairs={{0,2},{1,3},{2,4},{3,5},{4,6},{5,7},{6,0},{7,1},{8,10},{9,11},{10,... | collective-permute-start | bytes 1585160 | tf_op jit(solution)/shard_map/ppermute | solution.py:61
  144.2 3.2 %copy-start.7 = (bf16[512,512]{1,0:T(8,128)(2,1)S(1)}, bf16[512,512]{1,0:T(8,128)(2,1)}, u32[]{:S(2)}) copy-start(bf16[512,512]{1,0:T(8,128)(2,1)} %get-tuple-element.23) | copy-start | bytes 1572868
  144.2 3.2 %copy-start.8 = (bf16[512,512]{1,0:T(8,128)(2,1)S(1)}, bf16[512,512]{1,0:T(8,128)(2,1)}, u32[]{:S(2)}) copy-start(bf16[512,512]{1,0:T(8,128)(2,1)} %get-tuple-element.24) | copy-start | bytes 1572868
  144.4 14.1 %collective-permute-start.14 = (bf16[516,512]{1,0:T(8,128)(2,1)S(1)}, bf16[516,512]{1,0:T(8,128)(2,1)S(1)}, u32[]{:S(2)}, u32[]{:S(2)}) collective-permute-start(bf16[516,512]{1,0:T(8,128)(2,1)S(1)} %pad_maximum_fusion.6), channel_id=1, source_target_pairs={{0,6},{1,7},{2,0},{3,1},{4,2},{5,3},{6,4},{7,5},{8,14},{9,15},{10,... | collective-permute-start | bytes 1585160 | tf_op jit(solution)/shard_map/ppermute | solution.py:61
  147.3 13.5 %collective-permute-start.17 = (bf16[516,512]{1,0:T(8,128)(2,1)S(1)}, bf16[516,512]{1,0:T(8,128)(2,1)S(1)}, u32[]{:S(2)}, u32[]{:S(2)}) collective-permute-start(bf16[516,512]{1,0:T(8,128)(2,1)S(1)} %pad_maximum_fusion.8), channel_id=1, source_target_pairs={{0,1},{1,0},{2,3},{3,2},{4,5},{5,4},{6,7},{7,6},{8,9},{9,8},{10,11... | collective-permute-start | bytes 1585160 | tf_op jit(solution)/shard_map/ppermute | solution.py:61
  161.4 12.6 %collective-permute-start.19 = (bf16[516,512]{1,0:T(8,128)(2,1)S(1)}, bf16[516,512]{1,0:T(8,128)(2,1)S(1)}, u32[]{:S(2)}, u32[]{:S(2)}) collective-permute-start(bf16[516,512]{1,0:T(8,128)(2,1)S(1)} %pad_maximum_fusion.10), channel_id=1, source_target_pairs={{0,6},{1,7},{2,0},{3,1},{4,2},{5,3},{6,4},{7,5},{8,14},{9,15},{10,... | collective-permute-start | bytes 1585160 | tf_op jit(solution)/shard_map/ppermute | solution.py:61
  163.0 24.7 %copy-start.2 = (bf16[4,128,512]{2,1,0:T(8,128)(2,1)S(1)}, bf16[4,128,512]{2,1,0:T(8,128)(2,1)}, u32[]{:S(2)}) copy-start(bf16[4,128,512]{2,1,0:T(8,128)(2,1)} %param.8) | copy-start | bytes 1572868
  163.0 24.7 %copy-start.20 = (f32[512]{0:T(512)S(1)}, f32[512]{0:T(512)}, u32[]{:S(2)}) copy-start(f32[512]{0:T(512)} %param.14) | copy-start | bytes 6148
  163.0 13.8 %collective-permute-start.18 = (bf16[516,512]{1,0:T(8,128)(2,1)S(1)}, bf16[516,512]{1,0:T(8,128)(2,1)S(1)}, u32[]{:S(2)}, u32[]{:S(2)}) collective-permute-start(bf16[516,512]{1,0:T(8,128)(2,1)S(1)} %pad_maximum_fusion.9), channel_id=1, source_target_pairs={{0,2},{1,3},{2,4},{3,5},{4,6},{5,7},{6,0},{7,1},{8,10},{9,11},{10,... | collective-permute-start | bytes 1585160 | tf_op jit(solution)/shard_map/ppermute | solution.py:61
  163.6 13.2 %collective-permute-start.15 = (bf16[516,512]{1,0:T(8,128)(2,1)S(1)}, bf16[516,512]{1,0:T(8,128)(2,1)S(1)}, u32[]{:S(2)}, u32[]{:S(2)}) collective-permute-start(bf16[516,512]{1,0:T(8,128)(2,1)S(1)} %pad_maximum_fusion.7), channel_id=1, source_target_pairs={{0,1},{1,0},{2,3},{3,2},{4,5},{5,4},{6,7},{7,6},{8,9},{9,8},{10,11... | collective-permute-start | bytes 1585160 | tf_op jit(solution)/shard_map/ppermute | solution.py:61
  177.2 5.2 %collective-permute-start.22 = (f32[516]{0:T(1024)S(1)}, f32[516]{0:T(1024)S(1)}, u32[]{:S(2)}, u32[]{:S(2)}) collective-permute-start(f32[516]{0:T(1024)S(1)} %multiply_reduce_fusion), channel_id=1, source_target_pairs={{0,4},{1,5},{2,6},{3,7},{4,0},{5,1},{6,2},{7,3},{8,12},{9,13},{10,... | collective-permute-start | bytes 6200 | tf_op jit(solution)/shard_map/ppermute | solution.py:80
  177.7 4.7 %collective-permute-start.21 = (f32[516]{0:T(1024)S(1)}, f32[516]{0:T(1024)S(1)}, u32[]{:S(2)}, u32[]{:S(2)}) collective-permute-start(f32[516]{0:T(1024)S(1)} %multiply_reduce_fusion), channel_id=1, source_target_pairs={{0,6},{1,7},{2,0},{3,1},{4,2},{5,3},{6,4},{7,5},{8,14},{9,15},{10,... | collective-permute-start | bytes 6200 | tf_op jit(solution)/shard_map/ppermute | solution.py:80
  179.2 4.8 %collective-permute-start.20 = (f32[516]{0:T(1024)S(1)}, f32[516]{0:T(1024)S(1)}, u32[]{:S(2)}, u32[]{:S(2)}) collective-permute-start(f32[516]{0:T(1024)S(1)} %multiply_reduce_fusion), channel_id=1, source_target_pairs={{0,2},{1,3},{2,4},{3,5},{4,6},{5,7},{6,0},{7,1},{8,10},{9,11},{10,... | collective-permute-start | bytes 6200 | tf_op jit(solution)/shard_map/ppermute | solution.py:80
  184.0 3.6 %collective-permute-start.23 = (f32[516]{0:T(1024)S(1)}, f32[516]{0:T(1024)S(1)}, u32[]{:S(2)}, u32[]{:S(2)}) collective-permute-start(f32[516]{0:T(1024)S(1)} %add_add_fusion.1), channel_id=1, source_target_pairs={{0,1},{1,0},{2,3},{3,2},{4,5},{5,4},{6,7},{7,6},{8,9},{9,8},{10,11... | collective-permute-start | bytes 6200 | tf_op jit(solution)/shard_map/ppermute | solution.py:81

commit v4 on v3

--- a/solution.py
+++ b/solution.py
@@ -99,13 +99,13 @@
                 xh = xh.astype(jnp.bfloat16)
                 for b in range(seqs):
                     pack_ref[b * heads + h, c] = xh[b * pos_dev:(b + 1) * pos_dev]
-                fresh_ref[c, :, h * HD:(h + 1) * HD] = xh[seqs * pos_dev:].astype(jnp.float32)
+                fresh_ref[c, :, h * HD:(h + 1) * HD] = xh[seqs * pos_dev:]
 
     return pl.pallas_call(
         kernel,
         out_shape=(
             jax.ShapeDtypeStruct((seqs * heads, 3, pos_dev, HD), jnp.bfloat16),
-            jax.ShapeDtypeStruct((3, rows - seqs * pos_dev, width), jnp.float32),
+            jax.ShapeDtypeStruct((3, rows - seqs * pos_dev, width), jnp.bfloat16),
         ),
     )(proj, square, gains, cosine, sine)
 
@@ -203,7 +203,7 @@
 
     owner = seq_index
     own_prompt = owner // heads_local
-    fresh = fresh.astype(jnp.bfloat16).reshape(3, pairs, HD)
+    fresh = fresh.reshape(3, pairs, HD)
     new_q, new_k, new_v = fresh[0, owner], fresh[1, owner], fresh[2, owner]
     prompt_out, new_out = attend_pair(
         full[0], full[1], full[2], new_q, new_k, new_v, lengths[own_prompt]

time: 190 us -> 190 us (level)
  no operation moved by 1% of the time
where the time goes in v4:
time: 190 us
  waiting for transfers between devices  71.2 us (37%)
  starting transfers between devices  47.4 us (25%)
  matrix products  23.5 us (12%)
  local copies, waits for them, and re-layouts  20.6 us (11%)
  other arithmetic  19.3 us (10%)
  Pallas kernels  4.11 us (2%)
  between operations  3.31 us (2%)
    ppermute x8, waiting for transfers between devices, tp_reduce_scatter(): lax.ppermute(value.astype(jnp.bfloat16), 'tp', perm).astype(jnp.float32)  30.7 us
    all_to_all x1, waiting for transfers between devices, body(): got = lax.all_to_all(qkv, 'seq', 0, 0, tiled=True)  13.4 us
    ppermute x8, starting transfers between devices, tp_gather(): send = lambda value, perm: lax.ppermute(value, 'tp', perm)  13.3 us
    dot_general x3, matrix products, body(): jnp.einsum('tn,cnf->ctf', jnp.concatenate(blocks, 1), jnp.concatenate(w_b...  11 us
    dynamic_slice x2, local copies, waits for them, and re-layouts, in_relative_order(): lax.dynamic_slice_in_dim(weight, order[name] * width_local, width_local,...  10.8 us
    ppermute x8, waiting for transfers between devices, tp_gather(): send = lambda value, perm: lax.ppermute(value, 'tp', perm)  9.44 us
    ppermute x8, starting transfers between devices, tp_reduce_scatter(): lax.ppermute(value.astype(jnp.bfloat16), 'tp', perm).astype(jnp.float32)  8.82 us
    ppermute x6, starting transfers between devices, tp_sum(): lax.ppermute(values, 'tp', [(i, (i + shift) % size) for i in range(size)])  8.39 us
  transfers between devices with their start and end apart: 26, of which 19 were waited for; matrix products, arithmetic and copies ran while one was open for 17% of the time, Pallas kernels for 0%

profile of v4, /device:TPU:32, one launch (start us, length us, event | category | flops | bytes accessed | tf_op | source)
XLA Modules:
  0.0 189.5 jit_solution(16969151107723697846)
XLA Ops:
  0.6 1.9 %pad_maximum_fusion.3 = bf16[516,512]{1,0:T(8,128)(2,1)} fusion(bf16[4,512]{1,0:T(4,128)(2,1)} %param.9, bf16[512,512]{1,0:T(8,128)(2,1)} %bitcast.93), kind=kLoop, calls=%fused_computation.100 | loop fusion | flops 1056768 | bytes 1056768 | tf_op jit(solution)/shard_map/concatenate | solution.py:159
  2.5 3.0 %collective-permute-start.2 = (bf16[516,512]{1,0:T(8,128)(2,1)}, bf16[516,512]{1,0:T(8,128)(2,1)}, u32[]{:S(2)}, u32[]{:S(2)}) collective-permute-start(bf16[516,512]{1,0:T(8,128)(2,1)} %pad_maximum_fusion.3), channel_id=1, source_target_pairs={{0,6},{1,7},{2,0},{3,1},{4,2},{5,3},{6,4},{7,5},{8,14},{9,15},{10,... | collective-permute-start | bytes 1585160 | tf_op jit(solution)/shard_map/ppermute | solution.py:42
  5.5 1.5 collective-permute-start
  7.0 7.4 %constant_dynamic-slice_fusion.12 = (bf16[3,512,512]{2,1,0:T(8,128)(2,1)S(1)}, bf16[3,512,512]{2,1,0:T(8,128)(2,1)S(1)}, bf16[3,512,512]{2,1,0:T(8,128)(2,1)}, b...) fusion(bf16[3,4096,512]{2,1,0:T(8,128)(2,1)} %param.10, ...), kind=kLoop, calls=%fused_computation.149 | loop fusion | bytes 22020124 | tf_op jit(solution)/shard_map/dynamic_slice | solution.py:164
  14.5 1.0 fusion.90
  15.5 3.9 %collective-permute-done = bf16[516,512]{1,0:T(8,128)(2,1)} collective-permute-done((bf16[516,512]{1,0:T(8,128)(2,1)}, bf16[516,512]{1,0:T(8,128)(2,1)}, u32[]{:S(2)}, u32[]{:S(2)}) %collective-permute-start) | collective-permute-done | bytes 528416 | tf_op jit(solution)/shard_map/ppermute | solution.py:42
  19.4 1.0 slice.254
  20.6 1.2 fusion.123
  21.9 1.0 slice.251
  23.2 1.5 collective-permute-start.3
  24.7 3.1 %collective-permute-start.4 = (bf16[516,512]{1,0:T(8,128)(2,1)S(1)}, bf16[516,512]{1,0:T(8,128)(2,1)S(1)}, u32[]{:S(2)}, u32[]{:S(2)}) collective-permute-start(bf16[516,512]{1,0:T(8,128)(2,1)S(1)} %get-tuple-element.50), channel_id=1, source_target_pairs={{0,6},{1,7},{2,0},{3,1},{4,2},{5,3},{6,4},{7,5},{8,14},{9,15},{10,... | collective-permute-start | bytes 1585160 | tf_op jit(solution)/shard_map/ppermute | solution.py:42
  27.8 5.4 %fusion = f32[3,512,516]{1,2,0:T(8,128)S(1)} fusion(bf16[3,512,512]{2,1,0:T(8,128)(2,1)S(1)} %copy-done.4, bf16[3,512,512]{2,1,0:T(8,128)(2,1)S(1)} %copy-done.5, bf16[3,512,512]{2,1,0:T(8,128)(2,1)S(1)} %copy-done.6, bf16[3,512,512]{2,1,0:T(8,128)(2,1)} %get-tuple-element.13, bf16[516,512]{1,0:T(8,128)(2,1)} %collective-permute-done.2, ...), kind=kOutput, calls=%fused_computation | convolution fusion | flops 3282124800 | bytes 11575296 | tf_op jit(solution)/shard_map/tn,cnf->ctf/dot_general | solution.py:172
  33.3 2.5 %collective-permute-done.3 = bf16[516,512]{1,0:T(8,128)(2,1)S(1)} collective-permute-done((bf16[516,512]{1,0:T(8,128)(2,1)S(1)}, bf16[516,512]{1,0:T(8,128)(2,1)S(1)}, u32[]{:S(2)}, u32[]{:S(2)}) %collective-permute-start.3) | collective-permute-done | bytes 528416 | tf_op jit(solution)/shard_map/ppermute | solution.py:42
  35.8 1.6 collective-permute-done.4
  37.5 1.5 collective-permute-start.7
  39.0 2.6 %collective-permute-start.6 = (bf16[516,256]{1,0:T(8,128)(2,1)S(1)}, bf16[516,256]{1,0:T(8,128)(2,1)S(1)}, u32[]{:S(2)}, u32[]{:S(2)}) collective-permute-start(bf16[516,256]{1,0:T(8,128)(2,1)S(1)} %get-tuple-element.43), channel_id=1, source_target_pairs={{0,6},{1,7},{2,0},{3,1},{4,2},{5,3},{6,4},{7,5},{8,14},{9,15},{10,... | collective-permute-start | bytes 792584 | tf_op jit(solution)/shard_map/ppermute | solution.py:42
  41.6 2.8 %fusion.8 = f32[3,512,516]{1,2,0:T(8,128)S(1)} fusion(bf16[3,512,512]{2,1,0:T(8,128)(2,1)S(1)} %copy-done.3, bf16[3,512,512]{2,1,0:T(8,128)(2,1)S(1)} %get-tuple-element.9, bf16[3,512,512]{2,1,0:T(8,128)(2,1)S(1)} %get-tuple-element.8, bf16[516,1536]{1,0:T(8,128)(2,1)S(1)} %slice_dynamic-update-slice_fusion), kind=kOutput, calls=%fused_computation.8 | convolution fusion | flops 2448949248 | bytes 9474048 | tf_op jit(solution)/shard_map/tn,cnf->ctf/dot_general | solution.py:172
  44.4 1.2 collective-permute-done.7
  45.7 2.7 %add_bitcast_fusion.proj_ref = f32[3,516,512]{2,1,0:T(8,128)S(1)} fusion(f32[3,512,516]{1,2,0:T(8,128)S(1)} %fusion, f32[3,512,516]{1,2,0:T(8,128)S(1)} %fusion.8, bf16[3,4096,512]{2,1,0:T(8,128)(2,1)} %param.10, s32[]{:T(128)S(6)} %select_n.121, bf16[516,256]{1,0:T(8,128)(2,1)S(1)} %collective-permute-done.7, bf16[516,256]{1,0:T(8,128)(2,1)S(1)} %collective-permute-done.6), kind=kOutput, calls=%fused_computation.26 | convolution fusion | flops 814239744 | bytes 11612164 | tf_op jit(solution)/shard_map/tn,cnf->ctf/dot_general | solution.py:172
  48.7 3.6 %collective-permute-start.10 = (f32[2,516]{1,0:T(2,128)S(1)}, f32[2,516]{1,0:T(2,128)S(1)}, u32[]{:S(2)}, u32[]{:S(2)}) collective-permute-start(f32[2,516]{1,0:T(2,128)S(1)} %pad_maximum_fusion.14), channel_id=1, source_target_pairs={{0,4},{1,5},{2,6},{3,7},{4,0},{5,1},{6,2},{7,3},{8,12},{9,13},{10,... | collective-permute-start | bytes 12392 | tf_op jit(solution)/shard_map/ppermute | solution.py:80
  52.9 1.4 collective-permute-start.8
  54.3 1.0 pad_maximum_fusion.12
  55.9 1.9 collective-permute-done.8
  59.0 2.5 %collective-permute-done.11 = f32[2,516]{1,0:T(2,128)S(1)} collective-permute-done((f32[2,516]{1,0:T(2,128)S(1)}, f32[2,516]{1,0:T(2,128)S(1)}, u32[]{:S(2)}, u32[]{:S(2)}) %collective-permute-start.11) | collective-permute-done | bytes 4160 | tf_op jit(solution)/shard_map/ppermute | solution.py:81
  61.5 1.1 copy.10.square_ref
  62.6 4.1 %shard_map.95 = (bf16[16,3,128,128]{3,2,1,0:T(8,128)(2,1)}, bf16[3,4,512]{2,1,0:T(4,128)(2,1)}) custom-call(f32[3,516,512]{2,1,0:T(8,128)} %copy-done, f32[2,516,1]{2,1,0:T(8,128)} %copy.10.square_ref, f32[2,1,512]{2,1,0:T(1,128)} %broadcast_in_dim.54.gain_ref, f32[516,128]{1,0:T(8,128)} %get-tuple-element.67.cos_ref, f32[516,128]{1,0:T(8,128)} %get-tuple-element.68.sin_ref), custom_call_target="tpu_custom_call" | custom-call | tf_op jit(solution)/shard_map/pallas_call | solution.py:104
  66.7 7.7 %all-to-all-start = ((bf16[16,3,128,128]{3,2,1,0:T(8,128)(2,1)}), bf16[16,3,128,128]{3,2,1,0:T(8,128)(2,1)S(1)}, u32[]{:S(2)}, u32[]{:S(2)}) async-start(bf16[16,3,128,128]{3,2,1,0:T(8,128)(2,1)} %get-tuple-element.4), calls=%async_computation | async-start | bytes 3145728 | tf_op jit(solution)/shard_map/all_to_all | solution.py:201
  75.0 1.2 iota_compare_fusion.5
  76.2 1.2 iota_compare_fusion.3
  78.0 1.2 iota_compare_fusion.4
  81.1 13.4 %all-to-all-done = bf16[16,3,128,128]{3,2,1,0:T(8,128)(2,1)S(1)} async-done(((bf16[16,3,128,128]{3,2,1,0:T(8,128)(2,1)}), bf16[16,3,128,128]{3,2,1,0:T(8,128)(2,1)S(1)}, u32[]{:S(2)}, u32[]{:S(2)}) %all-to-all-start) | async-done | bytes 1572896 | tf_op jit(solution)/shard_map/all_to_all | solution.py:201
  94.8 1.3 fusion.91
  96.8 1.9 fusion.94
  99.4 0.9 fusion.117
  101.0 2.1 %fusion.124 = (f32[512]{0:T(512)S(1)}, f32[512,2048]{1,0:T(8,128)S(1)}) fusion(bf16[512,128]{1,0:T(8,128)(2,1)S(1)} %bitcast.109, bf16[2048,128]{1,0:T(8,128)(2,1)S(1)} %bitcast.101, pred[2048]{0:T(1024)(128)(4,1)} %iota_compare_fusion.3, s32[512]{0:T(512)} %iota_add_fusion.1), kind=kOutput, calls=%fused_computation.195 | convolution fusion | flops 273677824 | bytes 4855808 | tf_op jit(solution)/shard_map/dot_general | solution.py:120
  103.1 1.5 fusion.17
  104.6 1.3 fusion.71
  106.0 1.3 fusion.125
  107.3 1.4 fusion.19
  108.7 1.3 fusion.77
  110.0 1.3 fusion.21
  112.3 1.0 fusion.58
  113.6 0.8 pad_maximum_fusion.2
  114.4 8.0 %all-to-all-start.1 = ((bf16[16,136,128]{2,1,0:T(8,128)(2,1)}), bf16[16,136,128]{2,1,0:T(8,128)(2,1)S(1)}, u32[]{:S(2)}, u32[]{:S(2)}) async-start(bf16[16,136,128]{2,1,0:T(8,128)(2,1)} %pad_maximum_fusion.2), calls=%async_computation.1 | async-start | bytes 1114112 | tf_op jit(solution)/shard_map/all_to_all | solution.py:216
  122.4 3.4 %constant_dynamic-slice_fusion.6 = (bf16[512,512]{1,0:T(8,128)(2,1)S(1)}, bf16[512,512]{1,0:T(8,128)(2,1)S(1)}, bf16[512,512]{1,0:T(8,128)(2,1)S(1)}, bf16[512,5...) fusion(bf16[512,4096]{1,0:T(8,128)(2,1)} %param.11, ...), kind=kLoop, calls=%fused_computation.142 | loop fusion | bytes 7340060 | tf_op jit(solution)/shard_map/dynamic_slice | solution.py:164
  125.9 5.7 %all-to-all-done.1 = bf16[16,136,128]{2,1,0:T(8,128)(2,1)S(1)} async-done(((bf16[16,136,128]{2,1,0:T(8,128)(2,1)}), bf16[16,136,128]{2,1,0:T(8,128)(2,1)S(1)}, u32[]{:S(2)}, u32[]{:S(2)}) %all-to-all-start.1) | async-done | bytes 557088 | tf_op jit(solution)/shard_map/all_to_all | solution.py:216
  132.1 1.5 convolution_convert_fusion
  133.8 3.1 %collective-permute-start.13 = (bf16[516,256]{1,0:T(8,128)(2,1)S(1)}, bf16[516,256]{1,0:T(8,128)(2,1)S(1)}, u32[]{:S(2)}, u32[]{:S(2)}) collective-permute-start(bf16[516,256]{1,0:T(8,128)(2,1)S(1)} %get-tuple-element.42), channel_id=1, source_target_pairs={{0,6},{1,7},{2,0},{3,1},{4,2},{5,3},{6,4},{7,5},{8,14},{9,15},{10,... | collective-permute-start | bytes 792584 | tf_op jit(solution)/shard_map/ppermute | solution.py:61
  136.9 1.0 fusion.126
  138.1 6.0 %collective-permute-done.16 = bf16[516,256]{1,0:T(8,128)(2,1)S(1)} collective-permute-done((bf16[516,256]{1,0:T(8,128)(2,1)S(1)}, bf16[516,256]{1,0:T(8,128)(2,1)S(1)}, u32[]{:S(2)}, u32[]{:S(2)}) %collective-permute-start.16) | collective-permute-done | bytes 264224 | tf_op jit(solution)/shard_map/ppermute | solution.py:61
  144.4 2.8 %collective-permute-start.14 = (bf16[516,512]{1,0:T(8,128)(2,1)S(1)}, bf16[516,512]{1,0:T(8,128)(2,1)S(1)}, u32[]{:S(2)}, u32[]{:S(2)}) collective-permute-start(bf16[516,512]{1,0:T(8,128)(2,1)S(1)} %pad_maximum_fusion.6), channel_id=1, source_target_pairs={{0,6},{1,7},{2,0},{3,1},{4,2},{5,3},{6,4},{7,5},{8,14},{9,15},{10,... | collective-permute-start | bytes 1585160 | tf_op jit(solution)/shard_map/ppermute | solution.py:61
  147.4 1.3 fusion.127
  148.7 6.7 %collective-permute-done.12 = bf16[516,512]{1,0:T(8,128)(2,1)S(1)} collective-permute-done((bf16[516,512]{1,0:T(8,128)(2,1)S(1)}, bf16[516,512]{1,0:T(8,128)(2,1)S(1)}, u32[]{:S(2)}, u32[]{:S(2)}) %collective-permute-start.12) | collective-permute-done | bytes 528416 | tf_op jit(solution)/shard_map/ppermute | solution.py:61
  155.5 2.9 %collective-permute-done.14 = bf16[516,512]{1,0:T(8,128)(2,1)S(1)} collective-permute-done((bf16[516,512]{1,0:T(8,128)(2,1)S(1)}, bf16[516,512]{1,0:T(8,128)(2,1)S(1)}, u32[]{:S(2)}, u32[]{:S(2)}) %collective-permute-start.14) | collective-permute-done | bytes 528416 | tf_op jit(solution)/shard_map/ppermute | solution.py:61
  158.6 2.2 %collective-permute-done.17 = bf16[516,512]{1,0:T(8,128)(2,1)S(1)} collective-permute-done((bf16[516,512]{1,0:T(8,128)(2,1)S(1)}, bf16[516,512]{1,0:T(8,128)(2,1)S(1)}, u32[]{:S(2)}, u32[]{:S(2)}) %collective-permute-start.17) | collective-permute-done | bytes 528416 | tf_op jit(solution)/shard_map/ppermute | solution.py:61
  161.4 1.6 collective-permute-start.19
  164.0 9.9 %collective-permute-done.19 = bf16[516,512]{1,0:T(8,128)(2,1)S(1)} collective-permute-done((bf16[516,512]{1,0:T(8,128)(2,1)S(1)}, bf16[516,512]{1,0:T(8,128)(2,1)S(1)}, u32[]{:S(2)}, u32[]{:S(2)}) %collective-permute-start.19) | collective-permute-done | bytes 528416 | tf_op jit(solution)/shard_map/ppermute | solution.py:61
  173.9 2.9 %collective-permute-done.18 = bf16[516,512]{1,0:T(8,128)(2,1)S(1)} collective-permute-done((bf16[516,512]{1,0:T(8,128)(2,1)S(1)}, bf16[516,512]{1,0:T(8,128)(2,1)S(1)}, u32[]{:S(2)}, u32[]{:S(2)}) %collective-permute-start.18) | collective-permute-done | bytes 528416 | tf_op jit(solution)/shard_map/ppermute | solution.py:61
  177.7 1.6 collective-permute-start.21
  179.2 0.8 collective-permute-start.20
  180.0 2.4 %collective-permute-done.22 = f32[516]{0:T(1024)S(1)} collective-permute-done((f32[516]{0:T(1024)S(1)}, f32[516]{0:T(1024)S(1)}, u32[]{:S(2)}, u32[]{:S(2)}) %collective-permute-start.22) | collective-permute-done | bytes 2096 | tf_op jit(solution)/shard_map/ppermute | solution.py:80
  182.4 1.6 collective-permute-done.20
  184.5 3.2 %collective-permute-done.23 = f32[516]{0:T(1024)S(1)} collective-permute-done((f32[516]{0:T(1024)S(1)}, f32[516]{0:T(1024)S(1)}, u32[]{:S(2)}, u32[]{:S(2)}) %collective-permute-start.23) | collective-permute-done | bytes 2096 | tf_op jit(solution)/shard_map/ppermute | solution.py:81
  188.1 0.8 slice.295
  (129 shorter events, 13.7 us)
Async XLA Ops:
  2.5 19.3 %collective-permute-start.2 = (bf16[516,512]{1,0:T(8,128)(2,1)}, bf16[516,512]{1,0:T(8,128)(2,1)}, u32[]{:S(2)}, u32[]{:S(2)}) collective-permute-start(bf16[516,512]{1,0:T(8,128)(2,1)} %pad_maximum_fusion.3), channel_id=1, source_target_pairs={{0,6},{1,7},{2,0},{3,1},{4,2},{5,3},{6,4},{7,5},{8,14},{9,15},{10,... | collective-permute-start | bytes 1585160 | tf_op jit(solution)/shard_map/ppermute | solution.py:42
  5.5 15.1 %collective-permute-start.1 = (bf16[516,512]{1,0:T(8,128)(2,1)}, bf16[516,512]{1,0:T(8,128)(2,1)}, u32[]{:S(2)}, u32[]{:S(2)}) collective-permute-start(bf16[516,512]{1,0:T(8,128)(2,1)} %pad_maximum_fusion.3), channel_id=1, source_target_pairs={{0,2},{1,3},{2,4},{3,5},{4,6},{5,7},{6,0},{7,1},{8,10},{9,11},{10,... | collective-permute-start | bytes 1585160 | tf_op jit(solution)/shard_map/ppermute | solution.py:42
  5.5 13.9 %collective-permute-start = (bf16[516,512]{1,0:T(8,128)(2,1)}, bf16[516,512]{1,0:T(8,128)(2,1)}, u32[]{:S(2)}, u32[]{:S(2)}) collective-permute-start(bf16[516,512]{1,0:T(8,128)(2,1)} %pad_maximum_fusion.3), channel_id=1, source_target_pairs={{0,1},{1,0},{2,3},{3,2},{4,5},{5,4},{6,7},{7,6},{8,9},{9,8},{10,11... | collective-permute-start | bytes 1585160 | tf_op jit(solution)/shard_map/ppermute | solution.py:42
  7.0 7.4 %copy-start.24 = (s32[4]{0:T(128)S(1)}, s32[4]{0:T(128)}, u32[]{:S(2)}) copy-start(s32[4]{0:T(128)} %param.15) | copy-start | bytes 52
  14.5 13.3 %copy-start.6 = (bf16[3,512,512]{2,1,0:T(8,128)(2,1)S(1)}, bf16[3,512,512]{2,1,0:T(8,128)(2,1)}, u32[]{:S(2)}) copy-start(bf16[3,512,512]{2,1,0:T(8,128)(2,1)} %get-tuple-element.12) | copy-start | bytes 4718596
  20.4 7.4 %copy-start.1 = (bf16[4,128,512]{2,1,0:T(8,128)(2,1)S(1)}, bf16[4,128,512]{2,1,0:T(8,128)(2,1)}, u32[]{:S(2)}) copy-start(bf16[4,128,512]{2,1,0:T(8,128)(2,1)} %param.8) | copy-start | bytes 1572868
  20.4 7.4 %copy-start.4 = (bf16[3,512,512]{2,1,0:T(8,128)(2,1)S(1)}, bf16[3,512,512]{2,1,0:T(8,128)(2,1)}, u32[]{:S(2)}) copy-start(bf16[3,512,512]{2,1,0:T(8,128)(2,1)} %get-tuple-element.10) | copy-start | bytes 4718596
  20.4 7.4 %copy-start.5 = (bf16[3,512,512]{2,1,0:T(8,128)(2,1)S(1)}, bf16[3,512,512]{2,1,0:T(8,128)(2,1)}, u32[]{:S(2)}) copy-start(bf16[3,512,512]{2,1,0:T(8,128)(2,1)} %get-tuple-element.11) | copy-start | bytes 4718596
  20.4 7.4 %copy-start.13 = (bf16[4,512]{1,0:T(4,128)(2,1)S(1)}, bf16[4,512]{1,0:T(4,128)(2,1)}, u32[]{:S(2)}) copy-start(bf16[4,512]{1,0:T(4,128)(2,1)} %param.9) | copy-start | bytes 12292
  23.0 14.5 %collective-permute-start.5 = (bf16[516,512]{1,0:T(8,128)(2,1)S(1)}, bf16[516,512]{1,0:T(8,128)(2,1)S(1)}, u32[]{:S(2)}, u32[]{:S(2)}) collective-permute-start(bf16[516,512]{1,0:T(8,128)(2,1)S(1)} %get-tuple-element.49), channel_id=1, source_target_pairs={{0,2},{1,3},{2,4},{3,5},{4,6},{5,7},{6,0},{7,1},{8,10},{9,11},{10,... | collective-permute-start | bytes 1585160 | tf_op jit(solution)/shard_map/ppermute | solution.py:42
  23.2 12.6 %collective-permute-start.3 = (bf16[516,512]{1,0:T(8,128)(2,1)S(1)}, bf16[516,512]{1,0:T(8,128)(2,1)S(1)}, u32[]{:S(2)}, u32[]{:S(2)}) collective-permute-start(bf16[516,512]{1,0:T(8,128)(2,1)S(1)} %get-tuple-element.51), channel_id=1, source_target_pairs={{0,1},{1,0},{2,3},{3,2},{4,5},{5,4},{6,7},{7,6},{8,9},{9,8},{10,11... | collective-permute-start | bytes 1585160 | tf_op jit(solution)/shard_map/ppermute | solution.py:42
  24.7 12.7 %collective-permute-start.4 = (bf16[516,512]{1,0:T(8,128)(2,1)S(1)}, bf16[516,512]{1,0:T(8,128)(2,1)S(1)}, u32[]{:S(2)}, u32[]{:S(2)}) collective-permute-start(bf16[516,512]{1,0:T(8,128)(2,1)S(1)} %get-tuple-element.50), channel_id=1, source_target_pairs={{0,6},{1,7},{2,0},{3,1},{4,2},{5,3},{6,4},{7,5},{8,14},{9,15},{10,... | collective-permute-start | bytes 1585160 | tf_op jit(solution)/shard_map/ppermute | solution.py:42
  33.3 8.3 %copy-start.3 = (bf16[3,512,512]{2,1,0:T(8,128)(2,1)S(1)}, bf16[3,512,512]{2,1,0:T(8,128)(2,1)}, u32[]{:S(2)}) copy-start(bf16[3,512,512]{2,1,0:T(8,128)(2,1)} %get-tuple-element.14) | copy-start | bytes 4718596
  37.5 8.2 %collective-permute-start.7 = (bf16[516,256]{1,0:T(8,128)(2,1)S(1)}, bf16[516,256]{1,0:T(8,128)(2,1)S(1)}, u32[]{:S(2)}, u32[]{:S(2)}) collective-permute-start(bf16[516,256]{1,0:T(8,128)(2,1)S(1)} %get-tuple-element.45), channel_id=1, source_target_pairs={{0,2},{1,3},{2,4},{3,5},{4,6},{5,7},{6,0},{7,1},{8,10},{9,11},{10,... | collective-permute-start | bytes 792584 | tf_op jit(solution)/shard_map/ppermute | solution.py:42
  39.0 6.7 %collective-permute-start.6 = (bf16[516,256]{1,0:T(8,128)(2,1)S(1)}, bf16[516,256]{1,0:T(8,128)(2,1)S(1)}, u32[]{:S(2)}, u32[]{:S(2)}) collective-permute-start(bf16[516,256]{1,0:T(8,128)(2,1)S(1)} %get-tuple-element.43), channel_id=1, source_target_pairs={{0,6},{1,7},{2,0},{3,1},{4,2},{5,3},{6,4},{7,5},{8,14},{9,15},{10,... | collective-permute-start | bytes 792584 | tf_op jit(solution)/shard_map/ppermute | solution.py:42
  48.4 14.2 %copy-start = (f32[3,516,512]{2,1,0:T(8,128)}, f32[3,516,512]{2,1,0:T(8,128)S(1)}, u32[]{:S(2)}) copy-start(f32[3,516,512]{2,1,0:T(8,128)S(1)} %add_bitcast_fusion.proj_ref) | copy-start | bytes 9510916
  48.4 10.0 %copy-start.21 = (f32[512]{0:T(512)S(1)}, f32[512]{0:T(512)}, u32[]{:S(2)}) copy-start(f32[512]{0:T(512)} %param.13) | copy-start | bytes 6148
  48.4 10.0 %copy-start.22 = (f32[512]{0:T(512)S(1)}, f32[512]{0:T(512)}, u32[]{:S(2)}) copy-start(f32[512]{0:T(512)} %param.12) | copy-start | bytes 6148
  48.7 6.6 %collective-permute-start.10 = (f32[2,516]{1,0:T(2,128)S(1)}, f32[2,516]{1,0:T(2,128)S(1)}, u32[]{:S(2)}, u32[]{:S(2)}) collective-permute-start(f32[2,516]{1,0:T(2,128)S(1)} %pad_maximum_fusion.14), channel_id=1, source_target_pairs={{0,4},{1,5},{2,6},{3,7},{4,0},{5,1},{6,2},{7,3},{8,12},{9,13},{10,... | collective-permute-start | bytes 12392 | tf_op jit(solution)/shard_map/ppermute | solution.py:80
  52.3 3.6 %collective-permute-start.9 = (f32[2,516]{1,0:T(2,128)S(1)}, f32[2,516]{1,0:T(2,128)S(1)}, u32[]{:S(2)}, u32[]{:S(2)}) collective-permute-start(f32[2,516]{1,0:T(2,128)S(1)} %pad_maximum_fusion.14), channel_id=1, source_target_pairs={{0,6},{1,7},{2,0},{3,1},{4,2},{5,3},{6,4},{7,5},{8,14},{9,15},{10,... | collective-permute-start | bytes 12392 | tf_op jit(solution)/shard_map/ppermute | solution.py:80
  52.9 4.8 %collective-permute-start.8 = (f32[2,516]{1,0:T(2,128)S(1)}, f32[2,516]{1,0:T(2,128)S(1)}, u32[]{:S(2)}, u32[]{:S(2)}) collective-permute-start(f32[2,516]{1,0:T(2,128)S(1)} %pad_maximum_fusion.14), channel_id=1, source_target_pairs={{0,2},{1,3},{2,4},{3,5},{4,6},{5,7},{6,0},{7,1},{8,10},{9,11},{10,... | collective-permute-start | bytes 12392 | tf_op jit(solution)/shard_map/ppermute | solution.py:80
  57.8 3.7 %collective-permute-start.11 = (f32[2,516]{1,0:T(2,128)S(1)}, f32[2,516]{1,0:T(2,128)S(1)}, u32[]{:S(2)}, u32[]{:S(2)}) collective-permute-start(f32[2,516]{1,0:T(2,128)S(1)} %add_add_fusion), channel_id=1, source_target_pairs={{0,1},{1,0},{2,3},{3,2},{4,5},{5,4},{6,7},{7,6},{8,9},{9,8},{10,11... | collective-permute-start | bytes 12392 | tf_op jit(solution)/shard_map/ppermute | solution.py:81
  66.7 13.2 %copy-start.16 = (bf16[3,4,512]{2,1,0:T(4,128)(2,1)S(1)}, bf16[3,4,512]{2,1,0:T(4,128)(2,1)}, u32[]{:S(2)}) copy-start(bf16[3,4,512]{2,1,0:T(4,128)(2,1)} %get-tuple-element.5) | copy-start | bytes 36868
  66.7 27.8 %all-to-all-start = ((bf16[16,3,128,128]{3,2,1,0:T(8,128)(2,1)}), bf16[16,3,128,128]{3,2,1,0:T(8,128)(2,1)S(1)}, u32[]{:S(2)}, u32[]{:S(2)}) async-start(bf16[16,3,128,128]{3,2,1,0:T(8,128)(2,1)} %get-tuple-element.4), calls=%async_computation | async-start | bytes 3145728 | tf_op jit(solution)/shard_map/all_to_all | solution.py:201
  98.6 1.6 copy-start.14
  101.0 2.2 %copy-start.18 = (pred[2048]{0:T(1024)(128)(4,1)S(1)}, pred[2048]{0:T(1024)(128)(4,1)}, u32[]{:S(2)}) copy-start(pred[2048]{0:T(1024)(128)(4,1)} %iota_compare_fusion.3) | copy-start | bytes 6148
  101.0 2.2 %copy-start.19 = (s32[512]{0:T(512)S(1)}, s32[512]{0:T(512)}, u32[]{:S(2)}) copy-start(s32[512]{0:T(512)} %iota_add_fusion.1) | copy-start | bytes 6148
  104.6 1.4 copy-start.12
  104.6 1.4 copy-start.15
  104.6 1.4 copy-start.17
  108.7 1.3 copy-start.10
  108.7 1.3 copy-start.11
  108.7 1.3 copy-start.23
  111.4 0.9 copy-start.9
  114.4 17.1 %all-to-all-start.1 = ((bf16[16,136,128]{2,1,0:T(8,128)(2,1)}), bf16[16,136,128]{2,1,0:T(8,128)(2,1)S(1)}, u32[]{:S(2)}, u32[]{:S(2)}) async-start(bf16[16,136,128]{2,1,0:T(8,128)(2,1)} %pad_maximum_fusion.2), calls=%async_computation.1 | async-start | bytes 1114112 | tf_op jit(solution)/shard_map/all_to_all | solution.py:216
  133.6 10.5 %collective-permute-start.16 = (bf16[516,256]{1,0:T(8,128)(2,1)S(1)}, bf16[516,256]{1,0:T(8,128)(2,1)S(1)}, u32[]{:S(2)}, u32[]{:S(2)}) collective-permute-start(bf16[516,256]{1,0:T(8,128)(2,1)S(1)} %get-tuple-element.41), channel_id=1, source_target_pairs={{0,2},{1,3},{2,4},{3,5},{4,6},{5,7},{6,0},{7,1},{8,10},{9,11},{10,... | collective-permute-start | bytes 792584 | tf_op jit(solution)/shard_map/ppermute | solution.py:61
  133.8 10.3 %collective-permute-start.13 = (bf16[516,256]{1,0:T(8,128)(2,1)S(1)}, bf16[516,256]{1,0:T(8,128)(2,1)S(1)}, u32[]{:S(2)}, u32[]{:S(2)}) collective-permute-start(bf16[516,256]{1,0:T(8,128)(2,1)S(1)} %get-tuple-element.42), channel_id=1, source_target_pairs={{0,6},{1,7},{2,0},{3,1},{4,2},{5,3},{6,4},{7,5},{8,14},{9,15},{10,... | collective-permute-start | bytes 792584 | tf_op jit(solution)/shard_map/ppermute | solution.py:61
  138.0 17.3 %collective-permute-start.12 = (bf16[516,512]{1,0:T(8,128)(2,1)S(1)}, bf16[516,512]{1,0:T(8,128)(2,1)S(1)}, u32[]{:S(2)}, u32[]{:S(2)}) collective-permute-start(bf16[516,512]{1,0:T(8,128)(2,1)S(1)} %pad_maximum_fusion.5), channel_id=1, source_target_pairs={{0,2},{1,3},{2,4},{3,5},{4,6},{5,7},{6,0},{7,1},{8,10},{9,11},{10,... | collective-permute-start | bytes 1585160 | tf_op jit(solution)/shard_map/ppermute | solution.py:61
  144.2 3.2 %copy-start.7 = (bf16[512,512]{1,0:T(8,128)(2,1)S(1)}, bf16[512,512]{1,0:T(8,128)(2,1)}, u32[]{:S(2)}) copy-start(bf16[512,512]{1,0:T(8,128)(2,1)} %get-tuple-element.23) | copy-start | bytes 1572868
  144.2 3.2 %copy-start.8 = (bf16[512,512]{1,0:T(8,128)(2,1)S(1)}, bf16[512,512]{1,0:T(8,128)(2,1)}, u32[]{:S(2)}) copy-start(bf16[512,512]{1,0:T(8,128)(2,1)} %get-tuple-element.24) | copy-start | bytes 1572868
  144.4 14.1 %collective-permute-start.14 = (bf16[516,512]{1,0:T(8,128)(2,1)S(1)}, bf16[516,512]{1,0:T(8,128)(2,1)S(1)}, u32[]{:S(2)}, u32[]{:S(2)}) collective-permute-start(bf16[516,512]{1,0:T(8,128)(2,1)S(1)} %pad_maximum_fusion.6), channel_id=1, source_target_pairs={{0,6},{1,7},{2,0},{3,1},{4,2},{5,3},{6,4},{7,5},{8,14},{9,15},{10,... | collective-permute-start | bytes 1585160 | tf_op jit(solution)/shard_map/ppermute | solution.py:61
  147.3 13.5 %collective-permute-start.17 = (bf16[516,512]{1,0:T(8,128)(2,1)S(1)}, bf16[516,512]{1,0:T(8,128)(2,1)S(1)}, u32[]{:S(2)}, u32[]{:S(2)}) collective-permute-start(bf16[516,512]{1,0:T(8,128)(2,1)S(1)} %pad_maximum_fusion.8), channel_id=1, source_target_pairs={{0,1},{1,0},{2,3},{3,2},{4,5},{5,4},{6,7},{7,6},{8,9},{9,8},{10,11... | collective-permute-start | bytes 1585160 | tf_op jit(solution)/shard_map/ppermute | solution.py:61
  161.4 12.6 %collective-permute-start.19 = (bf16[516,512]{1,0:T(8,128)(2,1)S(1)}, bf16[516,512]{1,0:T(8,128)(2,1)S(1)}, u32[]{:S(2)}, u32[]{:S(2)}) collective-permute-start(bf16[516,512]{1,0:T(8,128)(2,1)S(1)} %pad_maximum_fusion.10), channel_id=1, source_target_pairs={{0,6},{1,7},{2,0},{3,1},{4,2},{5,3},{6,4},{7,5},{8,14},{9,15},{10,... | collective-permute-start | bytes 1585160 | tf_op jit(solution)/shard_map/ppermute | solution.py:61
  163.0 24.7 %copy-start.2 = (bf16[4,128,512]{2,1,0:T(8,128)(2,1)S(1)}, bf16[4,128,512]{2,1,0:T(8,128)(2,1)}, u32[]{:S(2)}) copy-start(bf16[4,128,512]{2,1,0:T(8,128)(2,1)} %param.8) | copy-start | bytes 1572868
  163.0 24.7 %copy-start.20 = (f32[512]{0:T(512)S(1)}, f32[512]{0:T(512)}, u32[]{:S(2)}) copy-start(f32[512]{0:T(512)} %param.14) | copy-start | bytes 6148
  163.0 13.8 %collective-permute-start.18 = (bf16[516,512]{1,0:T(8,128)(2,1)S(1)}, bf16[516,512]{1,0:T(8,128)(2,1)S(1)}, u32[]{:S(2)}, u32[]{:S(2)}) collective-permute-start(bf16[516,512]{1,0:T(8,128)(2,1)S(1)} %pad_maximum_fusion.9), channel_id=1, source_target_pairs={{0,2},{1,3},{2,4},{3,5},{4,6},{5,7},{6,0},{7,1},{8,10},{9,11},{10,... | collective-permute-start | bytes 1585160 | tf_op jit(solution)/shard_map/ppermute | solution.py:61
  163.6 13.2 %collective-permute-start.15 = (bf16[516,512]{1,0:T(8,128)(2,1)S(1)}, bf16[516,512]{1,0:T(8,128)(2,1)S(1)}, u32[]{:S(2)}, u32[]{:S(2)}) collective-permute-start(bf16[516,512]{1,0:T(8,128)(2,1)S(1)} %pad_maximum_fusion.7), channel_id=1, source_target_pairs={{0,1},{1,0},{2,3},{3,2},{4,5},{5,4},{6,7},{7,6},{8,9},{9,8},{10,11... | collective-permute-start | bytes 1585160 | tf_op jit(solution)/shard_map/ppermute | solution.py:61
  177.2 5.2 %collective-permute-start.22 = (f32[516]{0:T(1024)S(1)}, f32[516]{0:T(1024)S(1)}, u32[]{:S(2)}, u32[]{:S(2)}) collective-permute-start(f32[516]{0:T(1024)S(1)} %multiply_reduce_fusion), channel_id=1, source_target_pairs={{0,4},{1,5},{2,6},{3,7},{4,0},{5,1},{6,2},{7,3},{8,12},{9,13},{10,... | collective-permute-start | bytes 6200 | tf_op jit(solution)/shard_map/ppermute | solution.py:80
  177.7 4.7 %collective-permute-start.21 = (f32[516]{0:T(1024)S(1)}, f32[516]{0:T(1024)S(1)}, u32[]{:S(2)}, u32[]{:S(2)}) collective-permute-start(f32[516]{0:T(1024)S(1)} %multiply_reduce_fusion), channel_id=1, source_target_pairs={{0,6},{1,7},{2,0},{3,1},{4,2},{5,3},{6,4},{7,5},{8,14},{9,15},{10,... | collective-permute-start | bytes 6200 | tf_op jit(solution)/shard_map/ppermute | solution.py:80
  179.2 4.8 %collective-permute-start.20 = (f32[516]{0:T(1024)S(1)}, f32[516]{0:T(1024)S(1)}, u32[]{:S(2)}, u32[]{:S(2)}) collective-permute-start(f32[516]{0:T(1024)S(1)} %multiply_reduce_fusion), channel_id=1, source_target_pairs={{0,2},{1,3},{2,4},{3,5},{4,6},{5,7},{6,0},{7,1},{8,10},{9,11},{10,... | collective-permute-start | bytes 6200 | tf_op jit(solution)/shard_map/ppermute | solution.py:80
  184.0 3.6 %collective-permute-start.23 = (f32[516]{0:T(1024)S(1)}, f32[516]{0:T(1024)S(1)}, u32[]{:S(2)}, u32[]{:S(2)}) collective-permute-start(f32[516]{0:T(1024)S(1)} %add_add_fusion.1), channel_id=1, source_target_pairs={{0,1},{1,0},{2,3},{3,2},{4,5},{5,4},{6,7},{7,6},{8,9},{9,8},{10,11... | collective-permute-start | bytes 6200 | tf_op jit(solution)/shard_map/ppermute | solution.py:81
